TPU v7x, 32 devices: a whole 2x2x4 slice. The times are simulated.
32 devices in a mesh: pair: 1, contr: 32 (over z, y, x, core).
Axes of the slice: x: 2, y: 2, z: 4, core: 2. Of those that a mesh axis runs over, the one named last changes fastest.
Arguments:
- amplitudes: bfloat16 [1024, 32768], P('pair', 'contr'), may hold values from -6 to 6
- integrals: bfloat16 [32768, 256], P('contr', 'pair'), may hold values from -0.09375 to 0.09375
- occ_irrep: int32 [64], replicated, may hold values from 0 to 7
- virt_irrep: int32 [512], replicated, may hold values from 0 to 7
- occ_energy: float32 [64], replicated, may hold values from -2 to -0.5
- virt_energy: float32 [512], replicated, may hold values from 0.5 to 3
- slab_start: int32 [2], replicated, may hold values from 0 to 496
Outputs:
- update: bfloat16 [1024, 256], P(('pair', 'contr'))
All inputs are finite; a program needn't handle non-finite values.
Results may differ from a plain program's by a relative error of at most 0.003.
Values may be sent and summed in bfloat16 or wider, within the bound.
No kernel may reach another device: no remote copies, remote signals or barrier semaphores. Data moves between devices by JAX's collectives and lax.ppermute only.
A program may use at most 64 MiB of HBM per device.

v0:
```python
import jax
import jax.numpy as jnp
from jax import lax
from jax.sharding import PartitionSpec as P


def body(amplitudes, integrals, occ_irrep, virt_irrep, occ_energy, virt_energy, slab_start):
    pair_count = lax.axis_size("pair")
    contr_count = lax.axis_size("contr")
    pair_index = lax.axis_index("pair")
    contr_index = lax.axis_index("contr")
    virt_count = virt_irrep.shape[0]
    kc_local = integrals.shape[0]
    occ_local = kc_local // virt_count
    rows_pair = amplitudes.shape[0]
    cols_pair = integrals.shape[1]
    rows_device = rows_pair // contr_count
    slab_first = amplitudes.shape[0] * pair_count // occ_irrep.shape[0]
    slab_second = cols_pair * pair_count // occ_irrep.shape[0]
    first_start = slab_start[0]
    second_start = slab_start[1]
    a_irrep = lax.dynamic_slice(virt_irrep, (first_start,), (slab_first,))
    b_irrep = lax.dynamic_slice(virt_irrep, (second_start,), (slab_second,))
    a_energy = lax.dynamic_slice(virt_energy, (first_start,), (slab_first,))
    b_energy = lax.dynamic_slice(virt_energy, (second_start,), (slab_second,))
    row_irrep = jnp.bitwise_xor(occ_irrep[:, None], a_irrep[None, :]).reshape(-1)
    col_irrep = jnp.bitwise_xor(occ_irrep[:, None], b_irrep[None, :]).reshape(-1)
    row_energy = (occ_energy[:, None] - a_energy[None, :]).reshape(-1)
    col_energy = (occ_energy[:, None] - b_energy[None, :]).reshape(-1)
    local_occ = lax.dynamic_slice(occ_irrep, (contr_index * occ_local,), (occ_local,))
    kc_irrep = jnp.bitwise_xor(local_occ[:, None], virt_irrep[None, :]).reshape(-1)
    zero = jnp.zeros((), jnp.bfloat16)
    whole_int = lax.all_gather(integrals, "pair", axis=1, tiled=True)
    int_masked = jnp.where(kc_irrep[:, None] == col_irrep[None, :], whole_int, zero)
    row_irrep_pair = lax.dynamic_slice(row_irrep, (pair_index * rows_pair,), (rows_pair,))
    amp_masked = jnp.where(row_irrep_pair[:, None] == kc_irrep[None, :], amplitudes, zero)
    summed = lax.psum_scatter(
        jnp.dot(amp_masked, int_masked, preferred_element_type=jnp.float32),
        "contr",
        scatter_dimension=0,
        tiled=True,
    )
    mine_energy = lax.dynamic_slice(
        row_energy, (pair_index * rows_pair + contr_index * rows_device,), (rows_device,)
    )
    update = (summed / (mine_energy[:, None] + col_energy[None, :])).astype(jnp.bfloat16)
    return update


def solution(mesh):
    in_specs = (P("pair", "contr"), P("contr", "pair"), P(), P(), P(), P(), P())
    out_specs = P(("pair", "contr"), None)
    return jax.shard_map(body, mesh=mesh, in_specs=in_specs, out_specs=out_specs, check_vma=False)
```

profile of v0, /device:TPU:0, one launch (start us, length us, event | category | flops | bytes accessed | tf_op | source)
XLA Modules:
  0.0 165.8 jit_solution(3835110882156718680)
XLA Ops:
  6.5 0.0 reduce-scatter.2.cloned.1.call-start
  6.5 1.3 fusion.8
  11.6 0.8 dynamic_slice.21
  12.4 0.8 dynamic_slice.19
  13.1 0.7 dynamic_slice.20
  13.9 0.8 xor_bitcast_fusion
  14.6 0.7 broadcast_xor_fusion.1
  15.4 0.1 xor.67
  15.4 0.7 broadcast_xor_fusion
  16.2 0.1 xor.75
  16.3 0.0 copy-start.1
  16.3 0.0 copy-start
  16.3 3.6 %fusion = f32[1024,256]{1,0:T(8,128)} fusion(bf16[1024,1024]{1,0:T(8,128)(2,1)} %param.7, s32[1024]{0:T(1024)S(1)} %bitcast.5, s32[1024]{0:T(1024)S(1)} %xor.67, bf16[1024,256]{1,0:T(8,128)(2,1)} %param.8, s32[256]{0:T(256)S(1)} %xor.75), kind=kOutput, calls=%fused_computation.1 | convolution fusion | flops 539492352 | bytes 3679232 | tf_op jit(solution)/shard_map/dot_general | solution.py:38
  19.9 0.0 reduce-scatter.2.cloned.1.call-update
  19.9 0.0 copy-done.1
  19.9 0.1 dynamic_slice.24
  20.0 0.1 dynamic_slice.22
  20.1 0.0 copy-done
  20.1 0.1 broadcast_subtract_fusion.1
  20.1 0.1 sub.40
  20.2 0.1 broadcast_subtract_fusion
  20.3 0.1 sub.44
  20.4 0.1 dynamic_slice.23
  20.5 137.1 %reduce-scatter.2.cloned.1.call-done = f32[32,256]{1,0:T(8,128)} async-done(((f32[1024,256]{1,0:T(8,128)}), f32[32,256]{1,0:T(8,128)}) %reduce-scatter.2.cloned.1.call-update) | async-done | bytes 32784 | tf_op jit(solution)/shard_map/reduce_scatter | solution.py:37
  157.6 1.4 divide_convert_fusion
  (1 shorter events, 0.0 us)
Async XLA Ops:
  6.5 151.0 %reduce-scatter.2.cloned.1.call-start = ((), (), s32[]{:S(2)}) async-start(), calls=%async_computation.1 | async-start | bytes 1081344 | tf_op jit(solution)/shard_map/reduce_scatter | solution.py:37
  16.3 3.6 %copy-start.1 = (f32[512]{0:T(512)S(1)}, f32[512]{0:T(512)}, u32[]{:S(2)}) copy-start(f32[512]{0:T(512)} %param.12) | copy-start | bytes 6148
  16.3 3.8 %copy-start = (f32[64]{0:T(128)S(1)}, f32[64]{0:T(128)}, u32[]{:S(2)}) copy-start(f32[64]{0:T(128)} %param.11) | copy-start | bytes 772
Sparse Core Ops, SparseCore 0:
  20.0 137.4 reduce-scatter.1
where the time goes:
time: 166 us
  waiting for transfers between devices  137 us (83%)
  between operations  17.2 us (10%)
  local copies, waits for them, and re-layouts  4.18 us (3%)
  other arithmetic  3.8 us (2%)
  matrix products  3.59 us (2%)
    reduce_scatter x1, waiting for transfers between devices, body(): lax.psum_scatter(jnp.dot(amp_masked, int_masked, preferred_element_type=j...  137 us
    dot_general x1, matrix products, body(): jnp.dot(amp_masked, int_masked, preferred_element_type=jnp.float32)  3.59 us
  transfers between devices with their start and end apart: 1, of which 1 were waited for; matrix products, arithmetic and copies ran while one was open for 0% of the time, Pallas kernels for 0%

commit v1 on v0

--- a/solution.py
+++ b/solution.py
@@ -2,6 +2,23 @@
 import jax.numpy as jnp
 from jax import lax
 from jax.sharding import PartitionSpec as P
+
+
+def halving_scatter(partial, axis, count, index):
+    rows, cols = partial.shape
+    block = rows // count
+    buf = partial.reshape(count, block, cols)
+    stage = 0
+    while (1 << stage) < count:
+        half = buf.shape[0] // 2
+        pairs = buf.reshape(half, 2, block, cols)
+        bit = (index >> stage) & 1
+        keep = lax.dynamic_index_in_dim(pairs, bit, axis=1, keepdims=False)
+        send = lax.dynamic_index_in_dim(pairs, 1 - bit, axis=1, keepdims=False)
+        perm = [(i, i ^ (1 << stage)) for i in range(count)]
+        buf = keep + lax.ppermute(send, axis, perm)
+        stage += 1
+    return buf.reshape(block, cols)
 
 
 def body(amplitudes, integrals, occ_irrep, virt_irrep, occ_energy, virt_energy, slab_start):
@@ -34,12 +51,11 @@
     int_masked = jnp.where(kc_irrep[:, None] == col_irrep[None, :], whole_int, zero)
     row_irrep_pair = lax.dynamic_slice(row_irrep, (pair_index * rows_pair,), (rows_pair,))
     amp_masked = jnp.where(row_irrep_pair[:, None] == kc_irrep[None, :], amplitudes, zero)
-    summed = lax.psum_scatter(
-        jnp.dot(amp_masked, int_masked, preferred_element_type=jnp.float32),
-        "contr",
-        scatter_dimension=0,
-        tiled=True,
-    )
+    partial = jnp.dot(amp_masked, int_masked, preferred_element_type=jnp.float32)
+    if contr_count & (contr_count - 1) == 0 and rows_pair % contr_count == 0:
+        summed = halving_scatter(partial, "contr", contr_count, contr_index)
+    else:
+        summed = lax.psum_scatter(partial, "contr", scatter_dimension=0, tiled=True)
     mine_energy = lax.dynamic_slice(
         row_energy, (pair_index * rows_pair + contr_index * rows_device,), (rows_device,)
     )

time: 166 us -> 39.7 us (0.24)
  waiting for transfers between devices: 137 us -> 15.2 us
  between operations: 17.2 us -> 3.75 us
  starting transfers between devices: 0.01 us -> 10.3 us
    reduce_scatter x1 -> x0, waiting for transfers between devices: 137 us -> none  [body(): lax.psum_scatter(jnp.dot(amp_masked, int_masked, preferred_element_type=j...]
    ppermute x0 -> x5, waiting for transfers between devices: none -> 15.2 us  [halving_scatter(): buf = keep + lax.ppermute(send, axis, perm)]
    ppermute x0 -> x5, starting transfers between devices: none -> 10.3 us  [halving_scatter(): buf = keep + lax.ppermute(send, axis, perm)]
  transfers between devices with their start and end apart: 1 -> 5, of which waited for: 1 -> 5; matrix products, arithmetic and copies ran while one was open for 0% -> 1% of each run, Pallas kernels for 0% -> 0%
where the time goes in v1:
time: 39.7 us; the launch traced here: 39.4 us
  waiting for transfers between devices  15.2 us (38%)
  starting transfers between devices  10.3 us (26%)
  local copies, waits for them, and re-layouts  4.3 us (11%)
  between operations  3.75 us (9%)
  other arithmetic  3.17 us (8%)
  matrix products  2.61 us (7%)
    ppermute x5, waiting for transfers between devices, halving_scatter(): buf = keep + lax.ppermute(send, axis, perm)  15.2 us
    ppermute x5, starting transfers between devices, halving_scatter(): buf = keep + lax.ppermute(send, axis, perm)  10.3 us
    dot_general x1, matrix products, body(): jnp.dot(amp_masked, int_masked, preferred_element_type=jnp.float32)  2.61 us
    slice x1, local copies, waits for them, and re-layouts, body(): second_start = slab_start[1]  1.31 us
  transfers between devices with their start and end apart: 5, of which 5 were waited for; matrix products, arithmetic and copies ran while one was open for 1% of the time, Pallas kernels for 0%

profile of v1, /device:TPU:0, one launch (start us, length us, event | category | flops | bytes accessed | tf_op | source)
XLA Modules:
  0.0 39.4 jit_solution(10379312406025085941)
XLA Ops:
  0.0 1.3 %fusion.9 = (s32[1]{0:T(128)}, s32[1]{0:T(128)}) fusion(s32[2]{0:T(128)} %param.13), kind=kLoop, calls=%fused_computation.26 | loop fusion | bytes 16 | tf_op jit(solution)/shard_map/slice | solution.py:38
  3.7 0.7 %dynamic_slice.51 = s32[2]{0:T(128)S(1)} dynamic-slice(s32[64]{0:T(128)} %param.9, s32[]{:T(128)S(6)} %select_n.59), dynamic_slice_sizes={2} | dynamic-slice | bytes 20 | tf_op jit(solution)/shard_map/dynamic_slice | solution.py:47
  4.5 0.8 %xor_bitcast_fusion = s32[1,4,2,128]{3,2,1,0:T(2,128)S(1)} fusion(s32[512]{0:T(512)} %param.10, s32[2]{0:T(128)S(1)} %dynamic_slice.51), kind=kLoop, calls=%fused_computation.23 | loop fusion | flops 1024 | bytes 6152
  5.8 0.8 %dynamic_slice.50 = s32[16]{0:T(128)S(1)} dynamic-slice(s32[512]{0:T(512)} %param.10, s32[]{:T(128)S(6)} %select_n.58), dynamic_slice_sizes={16} | dynamic-slice | bytes 132 | tf_op jit(solution)/shard_map/dynamic_slice | solution.py:39
  6.6 0.7 %broadcast_xor_fusion.1 = s32[64,16]{1,0:T(8,128)S(1)} fusion(s32[16]{0:T(128)S(1)} %dynamic_slice.50, s32[64]{0:T(128)} %param.9), kind=kLoop, calls=%fused_computation.22 | loop fusion | flops 1024 | bytes 4416 | tf_op jit(solution)/shard_map/xor | solution.py:43
  7.3 0.1 xor.67
  8.0 0.8 %dynamic_slice.52 = s32[4]{0:T(128)S(1)} dynamic-slice(s32[512]{0:T(512)} %param.10, s32[]{:T(128)S(6)} %select_n.61), dynamic_slice_sizes={4} | dynamic-slice | bytes 36 | tf_op jit(solution)/shard_map/dynamic_slice | solution.py:40
  8.8 0.7 %broadcast_xor_fusion = s32[64,4]{1,0:T(8,128)S(1)} fusion(s32[4]{0:T(128)S(1)} %dynamic_slice.52, s32[64]{0:T(128)} %param.9), kind=kLoop, calls=%fused_computation.21 | loop fusion | flops 256 | bytes 1296 | tf_op jit(solution)/shard_map/xor | solution.py:44
  9.5 0.1 xor.75
  9.6 2.6 %fusion = f32[1024,256]{1,0:T(8,128)S(1)} fusion(bf16[1024,1024]{1,0:T(8,128)(2,1)} %param.7, s32[1024]{0:T(1024)S(1)} %bitcast.37, s32[1024]{0:T(1024)S(1)} %xor.67, bf16[1024,256]{1,0:T(8,128)(2,1)} %param.8, s32[256]{0:T(256)S(1)} %xor.75), kind=kOutput, calls=%fused_computation.1 | convolution fusion | flops 539492352 | bytes 3679232 | tf_op jit(solution)/shard_map/dot_general | solution.py:54
  12.2 0.0 copy-start.1
  12.3 0.0 copy-start
  12.3 0.5 %collective-permute-start = (f32[16,32,256]{2,1,0:T(8,128)S(1)}, f32[16,32,256]{2,1,0:T(8,128)S(1)}, u32[]{:S(2)}, u32[]{:S(2)}) collective-permute-start(f32[16,32,256]{2,1,0:T(8,128)S(1)} %dynamic-slice_bitcast_fusion), channel_id=1, source_target_pairs={{0,1},{1,0},{2,3},{3,2},{4,5},{5,4},{6,7},{7,6},{8,9},{9,8},{10,11... | collective-permute-start | bytes 1572872 | tf_op jit(solution)/shard_map/ppermute | solution.py:19
  12.8 1.5 %collective-permute-done = f32[16,32,256]{2,1,0:T(8,128)S(1)} collective-permute-done((f32[16,32,256]{2,1,0:T(8,128)S(1)}, f32[16,32,256]{2,1,0:T(8,128)S(1)}, u32[]{:S(2)}, u32[]{:S(2)}) %collective-permute-start) | collective-permute-done | bytes 524320 | tf_op jit(solution)/shard_map/ppermute | solution.py:19
  14.4 0.1 bitcast_add_fusion
  14.5 2.9 %collective-permute-start.1 = (f32[8,32,256]{2,1,0:T(8,128)S(1)}, f32[8,32,256]{2,1,0:T(8,128)S(1)}, u32[]{:S(2)}, u32[]{:S(2)}) collective-permute-start(f32[8,32,256]{2,1,0:T(8,128)S(1)} %dynamic-slice_bitcast_fusion.1), channel_id=1, source_target_pairs={{0,2},{1,3},{2,0},{3,1},{4,6},{5,7},{6,4},{7,5},{8,10},{9,11},{10,... | collective-permute-start | bytes 786440 | tf_op jit(solution)/shard_map/ppermute | solution.py:19
  17.4 6.6 %collective-permute-done.1 = f32[8,32,256]{2,1,0:T(8,128)S(1)} collective-permute-done((f32[8,32,256]{2,1,0:T(8,128)S(1)}, f32[8,32,256]{2,1,0:T(8,128)S(1)}, u32[]{:S(2)}, u32[]{:S(2)}) %collective-permute-start.1) | collective-permute-done | bytes 262176 | tf_op jit(solution)/shard_map/ppermute | solution.py:19
  24.1 1.8 %collective-permute-start.2 = (f32[4,32,256]{2,1,0:T(8,128)S(1)}, f32[4,32,256]{2,1,0:T(8,128)S(1)}, u32[]{:S(2)}, u32[]{:S(2)}) collective-permute-start(f32[4,32,256]{2,1,0:T(8,128)S(1)} %dynamic-slice_bitcast_fusion.2), channel_id=1, source_target_pairs={{0,4},{1,5},{2,6},{3,7},{4,0},{5,1},{6,2},{7,3},{8,12},{9,13},{10,... | collective-permute-start | bytes 393224 | tf_op jit(solution)/shard_map/ppermute | solution.py:19
  25.9 0.0 copy-done.1
  25.9 0.1 dynamic_slice.61
  26.0 3.2 %collective-permute-done.2 = f32[4,32,256]{2,1,0:T(8,128)S(1)} collective-permute-done((f32[4,32,256]{2,1,0:T(8,128)S(1)}, f32[4,32,256]{2,1,0:T(8,128)S(1)}, u32[]{:S(2)}, u32[]{:S(2)}) %collective-permute-start.2) | collective-permute-done | bytes 131104 | tf_op jit(solution)/shard_map/ppermute | solution.py:19
  29.2 1.8 %collective-permute-start.3 = (f32[2,32,256]{2,1,0:T(8,128)S(1)}, f32[2,32,256]{2,1,0:T(8,128)S(1)}, u32[]{:S(2)}, u32[]{:S(2)}) collective-permute-start(f32[2,32,256]{2,1,0:T(8,128)S(1)} %dynamic-slice_bitcast_fusion.3), channel_id=1, source_target_pairs={{0,8},{1,9},{2,10},{3,11},{4,12},{5,13},{6,14},{7,15},{8,0},{9,1},... | collective-permute-start | bytes 196616 | tf_op jit(solution)/shard_map/ppermute | solution.py:19
  31.0 0.0 copy-done
  31.0 0.1 broadcast_subtract_fusion.1
  31.1 0.1 dynamic_slice.63
  31.2 2.4 %collective-permute-done.3 = f32[2,32,256]{2,1,0:T(8,128)S(1)} collective-permute-done((f32[2,32,256]{2,1,0:T(8,128)S(1)}, f32[2,32,256]{2,1,0:T(8,128)S(1)}, u32[]{:S(2)}, u32[]{:S(2)}) %collective-permute-start.3) | collective-permute-done | bytes 65568 | tf_op jit(solution)/shard_map/ppermute | solution.py:19
  33.6 3.2 %collective-permute-start.4 = (f32[1,32,256]{2,1,0:T(8,128)S(1)}, f32[1,32,256]{2,1,0:T(8,128)S(1)}, u32[]{:S(2)}, u32[]{:S(2)}) collective-permute-start(f32[1,32,256]{2,1,0:T(8,128)S(1)} %constant_dynamic-slice_fusion), channel_id=1, source_target_pairs={{0,16},{1,17},{2,18},{3,19},{4,20},{5,21},{6,22},{7,23},{8,24},{9,... | collective-permute-start | bytes 98312 | tf_op jit(solution)/shard_map/ppermute | solution.py:19
  36.8 0.1 broadcast_subtract_fusion
  36.8 0.1 sub.60
  36.9 0.1 sub.64
  37.0 0.1 dynamic_slice.62
  37.1 1.6 %collective-permute-done.4 = f32[1,32,256]{2,1,0:T(8,128)S(1)} collective-permute-done((f32[1,32,256]{2,1,0:T(8,128)S(1)}, f32[1,32,256]{2,1,0:T(8,128)S(1)}, u32[]{:S(2)}, u32[]{:S(2)}) %collective-permute-start.4) | collective-permute-done | bytes 32800 | tf_op jit(solution)/shard_map/ppermute | solution.py:19
  38.7 0.7 %fusion.7 = bf16[32,256]{1,0:T(8,128)(2,1)} fusion(f32[1,32,256]{2,1,0:T(8,128)S(1)} %collective-permute-done.4, f32[2,32,256]{2,1,0:T(8,128)S(1)} %bitcast_add_fusion.3, s32[]{:T(128)S(6)} %select_n.71, f32[256]{0:T(256)S(1)} %sub.64, f32[32]{0:T(128)S(1)} %dynamic_slice.62), kind=kLoop, calls=%fused_computation.18 | loop fusion | flops 32768 | bytes 83076 | tf_op jit(solution)/shard_map/convert_element_type | solution.py:62
  (9 shorter events, 0.2 us)
Async XLA Ops:
  12.2 13.7 %copy-start.1 = (f32[512]{0:T(512)S(1)}, f32[512]{0:T(512)}, u32[]{:S(2)}) copy-start(f32[512]{0:T(512)} %param.12) | copy-start | bytes 6148
  12.3 18.7 %copy-start = (f32[64]{0:T(128)S(1)}, f32[64]{0:T(128)}, u32[]{:S(2)}) copy-start(f32[64]{0:T(128)} %param.11) | copy-start | bytes 772
  12.3 2.1 %collective-permute-start = (f32[16,32,256]{2,1,0:T(8,128)S(1)}, f32[16,32,256]{2,1,0:T(8,128)S(1)}, u32[]{:S(2)}, u32[]{:S(2)}) collective-permute-start(f32[16,32,256]{2,1,0:T(8,128)S(1)} %dynamic-slice_bitcast_fusion), channel_id=1, source_target_pairs={{0,1},{1,0},{2,3},{3,2},{4,5},{5,4},{6,7},{7,6},{8,9},{9,8},{10,11... | collective-permute-start | bytes 1572872 | tf_op jit(solution)/shard_map/ppermute | solution.py:19
  14.5 9.5 %collective-permute-start.1 = (f32[8,32,256]{2,1,0:T(8,128)S(1)}, f32[8,32,256]{2,1,0:T(8,128)S(1)}, u32[]{:S(2)}, u32[]{:S(2)}) collective-permute-start(f32[8,32,256]{2,1,0:T(8,128)S(1)} %dynamic-slice_bitcast_fusion.1), channel_id=1, source_target_pairs={{0,2},{1,3},{2,0},{3,1},{4,6},{5,7},{6,4},{7,5},{8,10},{9,11},{10,... | collective-permute-start | bytes 786440 | tf_op jit(solution)/shard_map/ppermute | solution.py:19
  24.1 5.1 %collective-permute-start.2 = (f32[4,32,256]{2,1,0:T(8,128)S(1)}, f32[4,32,256]{2,1,0:T(8,128)S(1)}, u32[]{:S(2)}, u32[]{:S(2)}) collective-permute-start(f32[4,32,256]{2,1,0:T(8,128)S(1)} %dynamic-slice_bitcast_fusion.2), channel_id=1, source_target_pairs={{0,4},{1,5},{2,6},{3,7},{4,0},{5,1},{6,2},{7,3},{8,12},{9,13},{10,... | collective-permute-start | bytes 393224 | tf_op jit(solution)/shard_map/ppermute | solution.py:19
  29.2 4.3 %collective-permute-start.3 = (f32[2,32,256]{2,1,0:T(8,128)S(1)}, f32[2,32,256]{2,1,0:T(8,128)S(1)}, u32[]{:S(2)}, u32[]{:S(2)}) collective-permute-start(f32[2,32,256]{2,1,0:T(8,128)S(1)} %dynamic-slice_bitcast_fusion.3), channel_id=1, source_target_pairs={{0,8},{1,9},{2,10},{3,11},{4,12},{5,13},{6,14},{7,15},{8,0},{9,1},... | collective-permute-start | bytes 196616 | tf_op jit(solution)/shard_map/ppermute | solution.py:19
  33.6 5.1 %collective-permute-start.4 = (f32[1,32,256]{2,1,0:T(8,128)S(1)}, f32[1,32,256]{2,1,0:T(8,128)S(1)}, u32[]{:S(2)}, u32[]{:S(2)}) collective-permute-start(f32[1,32,256]{2,1,0:T(8,128)S(1)} %constant_dynamic-slice_fusion), channel_id=1, source_target_pairs={{0,16},{1,17},{2,18},{3,19},{4,20},{5,21},{6,22},{7,23},{8,24},{9,... | collective-permute-start | bytes 98312 | tf_op jit(solution)/shard_map/ppermute | solution.py:19

commit v2 on v1

--- a/solution.py
+++ b/solution.py
@@ -7,17 +7,37 @@
 def halving_scatter(partial, axis, count, index):
     rows, cols = partial.shape
     block = rows // count
-    buf = partial.reshape(count, block, cols)
-    stage = 0
-    while (1 << stage) < count:
-        half = buf.shape[0] // 2
-        pairs = buf.reshape(half, 2, block, cols)
-        bit = (index >> stage) & 1
-        keep = lax.dynamic_index_in_dim(pairs, bit, axis=1, keepdims=False)
-        send = lax.dynamic_index_in_dim(pairs, 1 - bit, axis=1, keepdims=False)
-        perm = [(i, i ^ (1 << stage)) for i in range(count)]
+    bits = count.bit_length() - 1
+    first = (index & 1) == 0
+
+    def order(c):
+        seq = list(range(bits))
+        if c == 1 and bits >= 3:
+            seq[1], seq[2] = seq[2], seq[1]
+        return seq
+
+    buf = partial.reshape((2,) * bits + (block, cols))
+    left = [list(range(bits - 1, -1, -1)) for _ in range(2)]
+    for stage in range(bits):
+        split = [order(c)[stage] for c in range(2)]
+        where = [left[c].index(split[c]) for c in range(2)]
+        mine = [(index >> split[c]) & 1 for c in range(2)]
+        if where[0] == where[1]:
+            bit = jnp.where(first, mine[0], mine[1]) if split[0] != split[1] else mine[0]
+            keep = lax.dynamic_index_in_dim(buf, bit, axis=where[0], keepdims=False)
+            send = lax.dynamic_index_in_dim(buf, 1 - bit, axis=where[0], keepdims=False)
+        else:
+            picks = [
+                [lax.dynamic_index_in_dim(buf, v, axis=where[c], keepdims=False)
+                 for v in (mine[c], 1 - mine[c])]
+                for c in range(2)
+            ]
+            keep = jnp.where(first, picks[0][0], picks[1][0])
+            send = jnp.where(first, picks[0][1], picks[1][1])
+        for c in range(2):
+            left[c].pop(where[c])
+        perm = [(i, i ^ (1 << order(i & 1)[stage])) for i in range(count)]
         buf = keep + lax.ppermute(send, axis, perm)
-        stage += 1
     return buf.reshape(block, cols)
 
 

time: 39.7 us -> 38 us (0.957)
  waiting for transfers between devices: 15.2 us -> 12.4 us
  starting transfers between devices: 10.3 us -> 11.1 us
    ppermute x5, waiting for transfers between devices: 15.2 us -> 12.4 us  [halving_scatter(): buf = keep + lax.ppermute(send, axis, perm)]
    ppermute x5, starting transfers between devices: 10.3 us -> 11.1 us  [halving_scatter(): buf = keep + lax.ppermute(send, axis, perm)]
where the time goes in v2:
time: 38 us; the launch traced here: 37.7 us
  waiting for transfers between devices  12.4 us (33%)
  starting transfers between devices  11.1 us (29%)
  local copies, waits for them, and re-layouts  4.38 us (12%)
  between operations  3.96 us (10%)
  other arithmetic  3.23 us (8%)
  matrix products  2.62 us (7%)
    ppermute x5, waiting for transfers between devices, halving_scatter(): buf = keep + lax.ppermute(send, axis, perm)  12.4 us
    ppermute x5, starting transfers between devices, halving_scatter(): buf = keep + lax.ppermute(send, axis, perm)  11.1 us
    dot_general x1, matrix products, body(): jnp.dot(amp_masked, int_masked, preferred_element_type=jnp.float32)  2.62 us
    slice x1, local copies, waits for them, and re-layouts, body(): second_start = slab_start[1]  1.31 us
  transfers between devices with their start and end apart: 5, of which 5 were waited for; matrix products, arithmetic and copies ran while one was open for 1% of the time, Pallas kernels for 0%

profile of v2, /device:TPU:0, one launch (start us, length us, event | category | flops | bytes accessed | tf_op | source)
XLA Modules:
  0.0 37.7 jit_solution(17475918692281926465)
XLA Ops:
  0.0 1.3 %fusion.11 = (s32[1]{0:T(128)}, s32[1]{0:T(128)}) fusion(s32[2]{0:T(128)} %param.13), kind=kLoop, calls=%fused_computation.32 | loop fusion | bytes 16 | tf_op jit(solution)/shard_map/slice | solution.py:58
  3.9 0.7 %dynamic_slice.62 = s32[2]{0:T(128)S(1)} dynamic-slice(s32[64]{0:T(128)} %param.9, s32[]{:T(128)S(6)} %select_n.83), dynamic_slice_sizes={2} | dynamic-slice | bytes 20 | tf_op jit(solution)/shard_map/dynamic_slice | solution.py:67
  4.6 0.8 %xor_bitcast_fusion = s32[1,4,2,128]{3,2,1,0:T(2,128)S(1)} fusion(s32[512]{0:T(512)} %param.10, s32[2]{0:T(128)S(1)} %dynamic_slice.62), kind=kLoop, calls=%fused_computation.26 | loop fusion | flops 1024 | bytes 6152
  6.0 0.8 %dynamic_slice.61 = s32[16]{0:T(128)S(1)} dynamic-slice(s32[512]{0:T(512)} %param.10, s32[]{:T(128)S(6)} %select_n.82), dynamic_slice_sizes={16} | dynamic-slice | bytes 132 | tf_op jit(solution)/shard_map/dynamic_slice | solution.py:59
  6.8 0.7 %broadcast_xor_fusion.1 = s32[64,16]{1,0:T(8,128)S(1)} fusion(s32[16]{0:T(128)S(1)} %dynamic_slice.61, s32[64]{0:T(128)} %param.9), kind=kLoop, calls=%fused_computation.25 | loop fusion | flops 1024 | bytes 4416 | tf_op jit(solution)/shard_map/xor | solution.py:63
  7.5 0.1 xor.67
  8.2 0.8 %dynamic_slice.63 = s32[4]{0:T(128)S(1)} dynamic-slice(s32[512]{0:T(512)} %param.10, s32[]{:T(128)S(6)} %select_n.85), dynamic_slice_sizes={4} | dynamic-slice | bytes 36 | tf_op jit(solution)/shard_map/dynamic_slice | solution.py:60
  9.0 0.7 %broadcast_xor_fusion = s32[64,4]{1,0:T(8,128)S(1)} fusion(s32[4]{0:T(128)S(1)} %dynamic_slice.63, s32[64]{0:T(128)} %param.9), kind=kLoop, calls=%fused_computation.24 | loop fusion | flops 256 | bytes 1296 | tf_op jit(solution)/shard_map/xor | solution.py:64
  9.7 0.1 xor.75
  9.8 2.6 %fusion = f32[1024,256]{1,0:T(8,128)S(1)} fusion(bf16[1024,1024]{1,0:T(8,128)(2,1)} %param.7, s32[1024]{0:T(1024)S(1)} %bitcast.39, s32[1024]{0:T(1024)S(1)} %xor.67, bf16[1024,256]{1,0:T(8,128)(2,1)} %param.8, s32[256]{0:T(256)S(1)} %xor.75), kind=kOutput, calls=%fused_computation.1 | convolution fusion | flops 539492352 | bytes 3679232 | tf_op jit(solution)/shard_map/dot_general | solution.py:74
  12.4 0.1 constant_dynamic-slice_fusion.3
  12.6 0.5 %collective-permute-start = (f32[2,2,2,2,32,256]{5,4,2,1,0,3:T(8,128)S(1)}, f32[2,2,2,2,32,256]{5,4,2,1,0,3:T(8,128)S(1)}, u32[]{:S(2)}, u32[]{:S(2)}) collective-permute-start(f32[2,2,2,2,32,256]{5,4,2,1,0,3:T(8,128)S(1)} %bitcast.38), channel_id=1, source_target_pairs={{0,1},{1,0},{2,3},{3,2},{4,5},{5,4},{6,7},{7,6},{8,9},{9,8},{10,11... | collective-permute-start | bytes 1572872 | tf_op jit(solution)/shard_map/ppermute | solution.py:40
  13.1 1.5 %collective-permute-done = f32[2,2,2,2,32,256]{5,4,2,1,0,3:T(8,128)S(1)} collective-permute-done((f32[2,2,2,2,32,256]{5,4,2,1,0,3:T(8,128)S(1)}, f32[2,2,2,2,32,256]{5,4,2,1,0,3:T(8,128)S(1)}, u32[]{:S(2)}, u32[]{:S(2)}) %collective-permute-start) | collective-permute-done | bytes 524320 | tf_op jit(solution)/shard_map/ppermute | solution.py:40
  14.6 0.0 copy-start.1
  14.6 0.1 bitcast_add_fusion
  14.7 0.0 copy-start
  14.8 2.9 %collective-permute-start.1 = (f32[2,2,2,32,256]{4,3,2,1,0:T(8,128)S(1)}, f32[2,2,2,32,256]{4,3,2,1,0:T(8,128)S(1)}, u32[]{:S(2)}, u32[]{:S(2)}) collective-permute-start(f32[2,2,2,32,256]{4,3,2,1,0:T(8,128)S(1)} %bitcast_select_fusion), channel_id=1, source_target_pairs={{0,2},{1,5},{2,0},{3,7},{4,6},{5,1},{6,4},{7,3},{8,10},{9,13},{10,... | collective-permute-start | bytes 786440 | tf_op jit(solution)/shard_map/ppermute | solution.py:40
  17.7 4.4 %collective-permute-done.1 = f32[2,2,2,32,256]{4,3,2,1,0:T(8,128)S(1)} collective-permute-done((f32[2,2,2,32,256]{4,3,2,1,0:T(8,128)S(1)}, f32[2,2,2,32,256]{4,3,2,1,0:T(8,128)S(1)}, u32[]{:S(2)}, u32[]{:S(2)}) %collective-permute-start.1) | collective-permute-done | bytes 262176 | tf_op jit(solution)/shard_map/ppermute | solution.py:40
  22.1 0.1 fusion.6
  22.2 2.1 %collective-permute-start.2 = (f32[2,2,32,256]{3,2,1,0:T(8,128)S(1)}, f32[2,2,32,256]{3,2,1,0:T(8,128)S(1)}, u32[]{:S(2)}, u32[]{:S(2)}) collective-permute-start(f32[2,2,32,256]{3,2,1,0:T(8,128)S(1)} %dynamic-slice_bitcast_fusion), channel_id=1, source_target_pairs={{0,4},{1,3},{2,6},{3,1},{4,0},{5,7},{6,2},{7,5},{8,12},{9,11},{10,... | collective-permute-start | bytes 393224 | tf_op jit(solution)/shard_map/ppermute | solution.py:40
  24.3 0.0 copy-done.1
  24.3 0.1 dynamic_slice.76
  24.4 2.9 %collective-permute-done.2 = f32[2,2,32,256]{3,2,1,0:T(8,128)S(1)} collective-permute-done((f32[2,2,32,256]{3,2,1,0:T(8,128)S(1)}, f32[2,2,32,256]{3,2,1,0:T(8,128)S(1)}, u32[]{:S(2)}, u32[]{:S(2)}) %collective-permute-start.2) | collective-permute-done | bytes 131104 | tf_op jit(solution)/shard_map/ppermute | solution.py:40
  27.3 2.1 %collective-permute-start.3 = (f32[2,32,256]{2,1,0:T(8,128)S(1)}, f32[2,32,256]{2,1,0:T(8,128)S(1)}, u32[]{:S(2)}, u32[]{:S(2)}) collective-permute-start(f32[2,32,256]{2,1,0:T(8,128)S(1)} %dynamic-slice_bitcast_fusion.1), channel_id=1, source_target_pairs={{0,8},{1,9},{2,10},{3,11},{4,12},{5,13},{6,14},{7,15},{8,0},{9,1},... | collective-permute-start | bytes 196616 | tf_op jit(solution)/shard_map/ppermute | solution.py:40
  29.4 0.0 copy-done
  29.4 0.1 broadcast_subtract_fusion.1
  29.5 0.1 dynamic_slice.78
  29.6 2.1 %collective-permute-done.3 = f32[2,32,256]{2,1,0:T(8,128)S(1)} collective-permute-done((f32[2,32,256]{2,1,0:T(8,128)S(1)}, f32[2,32,256]{2,1,0:T(8,128)S(1)}, u32[]{:S(2)}, u32[]{:S(2)}) %collective-permute-start.3) | collective-permute-done | bytes 65568 | tf_op jit(solution)/shard_map/ppermute | solution.py:40
  31.7 3.4 %collective-permute-start.4 = (f32[32,256]{1,0:T(8,128)S(1)}, f32[32,256]{1,0:T(8,128)S(1)}, u32[]{:S(2)}, u32[]{:S(2)}) collective-permute-start(f32[32,256]{1,0:T(8,128)S(1)} %dynamic-slice_bitcast_fusion.2), channel_id=1, source_target_pairs={{0,16},{1,17},{2,18},{3,19},{4,20},{5,21},{6,22},{7,23},{8,24},{9,... | collective-permute-start | bytes 98312 | tf_op jit(solution)/shard_map/ppermute | solution.py:40
  35.2 0.1 broadcast_subtract_fusion
  35.2 0.1 sub.64
  35.3 0.1 sub.68
  35.4 0.1 dynamic_slice.77
  35.5 1.6 %collective-permute-done.4 = f32[32,256]{1,0:T(8,128)S(1)} collective-permute-done((f32[32,256]{1,0:T(8,128)S(1)}, f32[32,256]{1,0:T(8,128)S(1)}, u32[]{:S(2)}, u32[]{:S(2)}) %collective-permute-start.4) | collective-permute-done | bytes 32800 | tf_op jit(solution)/shard_map/ppermute | solution.py:40
  37.0 0.7 %fusion.9 = bf16[32,256]{1,0:T(8,128)(2,1)} fusion(f32[32,256]{1,0:T(8,128)S(1)} %collective-permute-done.4, f32[2,32,256]{2,1,0:T(8,128)S(1)} %bitcast_add_fusion.2, s32[]{:T(128)S(6)} %select_n.100, f32[256]{0:T(256)S(1)} %sub.68, f32[32]{0:T(128)S(1)} %dynamic_slice.77), kind=kLoop, calls=%fused_computation.20 | loop fusion | flops 32768 | bytes 83076 | tf_op jit(solution)/shard_map/convert_element_type | solution.py:82
  (9 shorter events, 0.2 us)
Async XLA Ops:
  12.6 2.0 %collective-permute-start = (f32[2,2,2,2,32,256]{5,4,2,1,0,3:T(8,128)S(1)}, f32[2,2,2,2,32,256]{5,4,2,1,0,3:T(8,128)S(1)}, u32[]{:S(2)}, u32[]{:S(2)}) collective-permute-start(f32[2,2,2,2,32,256]{5,4,2,1,0,3:T(8,128)S(1)} %bitcast.38), channel_id=1, source_target_pairs={{0,1},{1,0},{2,3},{3,2},{4,5},{5,4},{6,7},{7,6},{8,9},{9,8},{10,11... | collective-permute-start | bytes 1572872 | tf_op jit(solution)/shard_map/ppermute | solution.py:40
  14.6 9.7 %copy-start.1 = (f32[512]{0:T(512)S(1)}, f32[512]{0:T(512)}, u32[]{:S(2)}) copy-start(f32[512]{0:T(512)} %param.12) | copy-start | bytes 6148
  14.7 14.7 %copy-start = (f32[64]{0:T(128)S(1)}, f32[64]{0:T(128)}, u32[]{:S(2)}) copy-start(f32[64]{0:T(128)} %param.11) | copy-start | bytes 772
  14.8 7.3 %collective-permute-start.1 = (f32[2,2,2,32,256]{4,3,2,1,0:T(8,128)S(1)}, f32[2,2,2,32,256]{4,3,2,1,0:T(8,128)S(1)}, u32[]{:S(2)}, u32[]{:S(2)}) collective-permute-start(f32[2,2,2,32,256]{4,3,2,1,0:T(8,128)S(1)} %bitcast_select_fusion), channel_id=1, source_target_pairs={{0,2},{1,5},{2,0},{3,7},{4,6},{5,1},{6,4},{7,3},{8,10},{9,13},{10,... | collective-permute-start | bytes 786440 | tf_op jit(solution)/shard_map/ppermute | solution.py:40
  22.2 5.1 %collective-permute-start.2 = (f32[2,2,32,256]{3,2,1,0:T(8,128)S(1)}, f32[2,2,32,256]{3,2,1,0:T(8,128)S(1)}, u32[]{:S(2)}, u32[]{:S(2)}) collective-permute-start(f32[2,2,32,256]{3,2,1,0:T(8,128)S(1)} %dynamic-slice_bitcast_fusion), channel_id=1, source_target_pairs={{0,4},{1,3},{2,6},{3,1},{4,0},{5,7},{6,2},{7,5},{8,12},{9,11},{10,... | collective-permute-start | bytes 393224 | tf_op jit(solution)/shard_map/ppermute | solution.py:40
  27.3 4.4 %collective-permute-start.3 = (f32[2,32,256]{2,1,0:T(8,128)S(1)}, f32[2,32,256]{2,1,0:T(8,128)S(1)}, u32[]{:S(2)}, u32[]{:S(2)}) collective-permute-start(f32[2,32,256]{2,1,0:T(8,128)S(1)} %dynamic-slice_bitcast_fusion.1), channel_id=1, source_target_pairs={{0,8},{1,9},{2,10},{3,11},{4,12},{5,13},{6,14},{7,15},{8,0},{9,1},... | collective-permute-start | bytes 196616 | tf_op jit(solution)/shard_map/ppermute | solution.py:40
  31.7 5.3 %collective-permute-start.4 = (f32[32,256]{1,0:T(8,128)S(1)}, f32[32,256]{1,0:T(8,128)S(1)}, u32[]{:S(2)}, u32[]{:S(2)}) collective-permute-start(f32[32,256]{1,0:T(8,128)S(1)} %dynamic-slice_bitcast_fusion.2), channel_id=1, source_target_pairs={{0,16},{1,17},{2,18},{3,19},{4,20},{5,21},{6,22},{7,23},{8,24},{9,... | collective-permute-start | bytes 98312 | tf_op jit(solution)/shard_map/ppermute | solution.py:40

commit v3 on v2

--- a/solution.py
+++ b/solution.py
@@ -69,13 +69,15 @@
     zero = jnp.zeros((), jnp.bfloat16)
     whole_int = lax.all_gather(integrals, "pair", axis=1, tiled=True)
     int_masked = jnp.where(kc_irrep[:, None] == col_irrep[None, :], whole_int, zero)
-    row_irrep_pair = lax.dynamic_slice(row_irrep, (pair_index * rows_pair,), (rows_pair,))
-    amp_masked = jnp.where(row_irrep_pair[:, None] == kc_irrep[None, :], amplitudes, zero)
-    partial = jnp.dot(amp_masked, int_masked, preferred_element_type=jnp.float32)
+    partial = jnp.dot(amplitudes, int_masked, preferred_element_type=jnp.float32)
     if contr_count & (contr_count - 1) == 0 and rows_pair % contr_count == 0:
         summed = halving_scatter(partial, "contr", contr_count, contr_index)
     else:
         summed = lax.psum_scatter(partial, "contr", scatter_dimension=0, tiled=True)
+    mine_irrep = lax.dynamic_slice(
+        row_irrep, (pair_index * rows_pair + contr_index * rows_device,), (rows_device,)
+    )
+    summed = jnp.where(mine_irrep[:, None] == col_irrep[None, :], summed, 0.0)
     mine_energy = lax.dynamic_slice(
         row_energy, (pair_index * rows_pair + contr_index * rows_device,), (rows_device,)
     )

time: 38 us -> 39 us (1.026)
  local copies, waits for them, and re-layouts: 4.38 us -> 6.96 us
  waiting for transfers between devices: 12.4 us -> 9.83 us
  other arithmetic: 3.23 us -> 3.77 us
  matrix products: 2.62 us -> 3.04 us
    ppermute x5, waiting for transfers between devices: 12.4 us -> 9.83 us  [halving_scatter(): buf = keep + lax.ppermute(send, axis, perm)]
    dot_general x0 -> x1, local copies, waits for them, and re-layouts: none -> 1.55 us  [body(): jnp.dot(amplitudes, int_masked, preferred_element_type=jnp.float32)]
    add x4, other arithmetic: 0.15 us -> 1.35 us  [halving_scatter(): buf = keep + lax.ppermute(send, axis, perm)]
    squeeze x3 -> x4, local copies, waits for them, and re-layouts: 0.05 us -> 0.99 us  [halving_scatter(): send = lax.dynamic_index_in_dim(buf, 1 - bit, axis=where[0], keepdims=False)]
    xor x1, other arithmetic: 0.73 us -> 0.07 us  [body(): jnp.bitwise_xor(occ_irrep[:, None], a_irrep[None, :]).reshape(-1)]
    dot_general x1, matrix products: 2.62 us -> 3.04 us  [body(): jnp.dot(amplitudes, int_masked, preferred_element_type=jnp.float32)]
  transfers between devices with their start and end apart: 5 -> 5, of which waited for: 5 -> 5; matrix products, arithmetic and copies ran while one was open for 1% -> 4% of each run, Pallas kernels for 0% -> 0%
where the time goes in v3:
time: 39 us; the launch traced here: 38.6 us
  starting transfers between devices  11.1 us (28%)
  waiting for transfers between devices  9.83 us (25%)
  local copies, waits for them, and re-layouts  6.96 us (18%)
  between operations  3.96 us (10%)
  other arithmetic  3.77 us (10%)
  matrix products  3.04 us (8%)
    ppermute x5, starting transfers between devices, halving_scatter(): buf = keep + lax.ppermute(send, axis, perm)  11.1 us
    ppermute x5, waiting for transfers between devices, halving_scatter(): buf = keep + lax.ppermute(send, axis, perm)  9.83 us
    dot_general x1, matrix products, body(): jnp.dot(amplitudes, int_masked, preferred_element_type=jnp.float32)  3.04 us
    dot_general x1, local copies, waits for them, and re-layouts, body(): jnp.dot(amplitudes, int_masked, preferred_element_type=jnp.float32)  1.55 us
    add x4, other arithmetic, halving_scatter(): buf = keep + lax.ppermute(send, axis, perm)  1.35 us
    slice x1, local copies, waits for them, and re-layouts, body(): first_start = slab_start[0]  1.34 us
    squeeze x4, local copies, waits for them, and re-layouts, halving_scatter(): send = lax.dynamic_index_in_dim(buf, 1 - bit, axis=where[0], keepdims=False)  0.99 us
    dynamic_slice x1, local copies, waits for them, and re-layouts, body(): lax.dynamic_slice(occ_irrep, (contr_index * occ_local,), (occ_local,))  0.88 us
  transfers between devices with their start and end apart: 5, of which 5 were waited for; matrix products, arithmetic and copies ran while one was open for 4% of the time, Pallas kernels for 0%

profile of v3, /device:TPU:0, one launch (start us, length us, event | category | flops | bytes accessed | tf_op | source)
XLA Modules:
  0.0 38.6 jit_solution(15065859910849159068)
XLA Ops:
  0.0 0.0 copy-start
  0.0 0.9 %dynamic_slice.66 = s32[2]{0:T(128)S(1)} dynamic-slice(s32[64]{0:T(128)} %param.9, s32[]{:T(128)S(6)} %select_n.85), dynamic_slice_sizes={2} | dynamic-slice | bytes 20 | tf_op jit(solution)/shard_map/dynamic_slice | solution.py:67
  0.9 0.8 %xor_bitcast_fusion = s32[1,4,2,128]{3,2,1,0:T(2,128)S(1)} fusion(s32[512]{0:T(512)} %param.10, s32[2]{0:T(128)S(1)} %dynamic_slice.66), kind=kLoop, calls=%fused_computation.23 | loop fusion | flops 1024 | bytes 6152
  1.6 1.3 %fusion.8 = (s32[1]{0:T(128)}, s32[1]{0:T(128)}) fusion(s32[2]{0:T(128)} %param.13), kind=kLoop, calls=%fused_computation.25 | loop fusion | bytes 16 | tf_op jit(solution)/shard_map/slice | solution.py:57
  4.9 0.8 %dynamic_slice.65 = s32[4]{0:T(128)S(1)} dynamic-slice(s32[512]{0:T(512)} %param.10, s32[]{:T(128)S(6)} %select_n.83), dynamic_slice_sizes={4} | dynamic-slice | bytes 36 | tf_op jit(solution)/shard_map/dynamic_slice | solution.py:60
  5.6 0.7 %broadcast_xor_fusion = s32[64,4]{1,0:T(8,128)S(1)} fusion(s32[4]{0:T(128)S(1)} %dynamic_slice.65, s32[64]{0:T(128)} %param.9), kind=kLoop, calls=%fused_computation.21 | loop fusion | flops 256 | bytes 1296 | tf_op jit(solution)/shard_map/xor | solution.py:64
  6.4 0.1 xor.64
  6.5 0.0 copy-done
  6.5 3.0 %convolution_bitcast_fusion = f32[1024,256]{0,1:T(8,128)} fusion(bf16[1024,1024]{1,0:T(8,128)(2,1)S(1)} %copy-done, bf16[1024,256]{1,0:T(8,128)(2,1)} %param.8, s32[256]{0:T(256)S(1)} %xor.64, s32[1024]{0:T(1024)S(1)} %bitcast.43), kind=kOutput, calls=%fused_computation | convolution fusion | flops 537395200 | bytes 3675136 | tf_op jit(solution)/shard_map/dot_general | solution.py:72
  9.5 1.6 %copy.13 = f32[1024,256]{1,0:T(8,128)S(1)} copy(f32[1024,256]{0,1:T(8,128)} %convolution_bitcast_fusion) | data formatting | bytes 2097152 | tf_op jit(solution)/shard_map/dot_general | solution.py:72
  11.1 0.0 copy-start.1
  11.1 0.0 copy-start.4
  11.1 0.9 %dynamic-slice_bitcast_fusion = f32[2,2,2,2,32,256]{5,4,3,2,1,0:T(8,128)} fusion(f32[2,2,2,2,2,32,256]{6,5,4,3,2,1,0:T(8,128)S(1)} %bitcast.41, s32[]{:T(128)S(6)} %select_n.88), kind=kLoop, calls=%fused_computation.3 | loop fusion | bytes 1048580 | tf_op jit(solution)/shard_map/jit(dynamic_index_in_dim)/squeeze | solution.py:28
  12.1 0.0 copy-start.2
  12.1 0.5 %collective-permute-start = (f32[2,2,2,2,32,256]{5,4,3,2,1,0:T(8,128)}, f32[2,2,2,2,32,256]{5,4,3,2,1,0:T(8,128)}, u32[]{:S(2)}, u32[]{:S(2)}) collective-permute-start(f32[2,2,2,2,32,256]{5,4,3,2,1,0:T(8,128)} %dynamic-slice_bitcast_fusion), channel_id=1, source_target_pairs={{0,1},{1,0},{2,3},{3,2},{4,5},{5,4},{6,7},{7,6},{8,9},{9,8},{10,11... | collective-permute-start | bytes 1572872 | tf_op jit(solution)/shard_map/ppermute | solution.py:40
  12.5 0.0 copy-done.1
  12.5 0.0 copy-start.3
  12.5 1.9 %collective-permute-done = f32[2,2,2,2,32,256]{5,4,3,2,1,0:T(8,128)} collective-permute-done((f32[2,2,2,2,32,256]{5,4,3,2,1,0:T(8,128)}, f32[2,2,2,2,32,256]{5,4,3,2,1,0:T(8,128)}, u32[]{:S(2)}, u32[]{:S(2)}) %collective-permute-start) | collective-permute-done | bytes 524320 | tf_op jit(solution)/shard_map/ppermute | solution.py:40
  14.4 1.3 %bitcast_add_fusion = f32[2,2,2,2,32,256]{5,4,3,2,1,0:T(8,128)S(1)} fusion(f32[2,2,2,2,32,256]{5,4,3,2,1,0:T(8,128)} %collective-permute-done, f32[2,2,2,2,2,32,256]{6,5,4,3,2,1,0:T(8,128)} %bitcast.42, s32[]{:T(128)S(6)} %select_n.87), kind=kLoop, calls=%fused_computation.2 | loop fusion | flops 131072 | bytes 1572868 | tf_op jit(solution)/shard_map/add | solution.py:40
  15.7 2.9 %collective-permute-start.1 = (f32[2,2,2,32,256]{4,3,2,1,0:T(8,128)S(1)}, f32[2,2,2,32,256]{4,3,2,1,0:T(8,128)S(1)}, u32[]{:S(2)}, u32[]{:S(2)}) collective-permute-start(f32[2,2,2,32,256]{4,3,2,1,0:T(8,128)S(1)} %bitcast_select_fusion), channel_id=1, source_target_pairs={{0,2},{1,5},{2,0},{3,7},{4,6},{5,1},{6,4},{7,3},{8,10},{9,13},{10,... | collective-permute-start | bytes 786440 | tf_op jit(solution)/shard_map/ppermute | solution.py:40
  20.6 0.8 %dynamic_slice.63 = s32[16]{0:T(128)S(1)} dynamic-slice(s32[512]{0:T(512)} %param.10, s32[]{:T(128)S(6)} %select_n.81), dynamic_slice_sizes={16} | dynamic-slice | bytes 132 | tf_op jit(solution)/shard_map/dynamic_slice | solution.py:59
  21.3 0.0 copy-done.4
  21.3 0.1 dynamic_slice.79
  21.4 1.6 %collective-permute-done.1 = f32[2,2,2,32,256]{4,3,2,1,0:T(8,128)S(1)} collective-permute-done((f32[2,2,2,32,256]{4,3,2,1,0:T(8,128)S(1)}, f32[2,2,2,32,256]{4,3,2,1,0:T(8,128)S(1)}, u32[]{:S(2)}, u32[]{:S(2)}) %collective-permute-start.1) | collective-permute-done | bytes 262176 | tf_op jit(solution)/shard_map/ppermute | solution.py:40
  23.0 0.1 fusion.2
  23.1 2.1 %collective-permute-start.2 = (f32[2,2,32,256]{3,2,1,0:T(8,128)S(1)}, f32[2,2,32,256]{3,2,1,0:T(8,128)S(1)}, u32[]{:S(2)}, u32[]{:S(2)}) collective-permute-start(f32[2,2,32,256]{3,2,1,0:T(8,128)S(1)} %dynamic-slice_bitcast_fusion.1), channel_id=1, source_target_pairs={{0,4},{1,3},{2,6},{3,1},{4,0},{5,7},{6,2},{7,5},{8,12},{9,11},{10,... | collective-permute-start | bytes 393224 | tf_op jit(solution)/shard_map/ppermute | solution.py:40
  25.2 0.0 copy-done.2
  25.2 0.1 broadcast_xor_fusion.1
  25.3 2.9 %collective-permute-done.2 = f32[2,2,32,256]{3,2,1,0:T(8,128)S(1)} collective-permute-done((f32[2,2,32,256]{3,2,1,0:T(8,128)S(1)}, f32[2,2,32,256]{3,2,1,0:T(8,128)S(1)}, u32[]{:S(2)}, u32[]{:S(2)}) %collective-permute-start.2) | collective-permute-done | bytes 131104 | tf_op jit(solution)/shard_map/ppermute | solution.py:40
  28.2 2.1 %collective-permute-start.3 = (f32[2,32,256]{2,1,0:T(8,128)S(1)}, f32[2,32,256]{2,1,0:T(8,128)S(1)}, u32[]{:S(2)}, u32[]{:S(2)}) collective-permute-start(f32[2,32,256]{2,1,0:T(8,128)S(1)} %dynamic-slice_bitcast_fusion.2), channel_id=1, source_target_pairs={{0,8},{1,9},{2,10},{3,11},{4,12},{5,13},{6,14},{7,15},{8,0},{9,1},... | collective-permute-start | bytes 196616 | tf_op jit(solution)/shard_map/ppermute | solution.py:40
  30.3 0.0 copy-done.3
  30.3 0.1 broadcast_subtract_fusion.1
  30.4 0.1 dynamic_slice.81
  30.5 2.1 %collective-permute-done.3 = f32[2,32,256]{2,1,0:T(8,128)S(1)} collective-permute-done((f32[2,32,256]{2,1,0:T(8,128)S(1)}, f32[2,32,256]{2,1,0:T(8,128)S(1)}, u32[]{:S(2)}, u32[]{:S(2)}) %collective-permute-start.3) | collective-permute-done | bytes 65568 | tf_op jit(solution)/shard_map/ppermute | solution.py:40
  32.6 3.5 %collective-permute-start.4 = (f32[32,256]{1,0:T(8,128)S(1)}, f32[32,256]{1,0:T(8,128)S(1)}, u32[]{:S(2)}, u32[]{:S(2)}) collective-permute-start(f32[32,256]{1,0:T(8,128)S(1)} %dynamic-slice_bitcast_fusion.3), channel_id=1, source_target_pairs={{0,16},{1,17},{2,18},{3,19},{4,20},{5,21},{6,22},{7,23},{8,24},{9,... | collective-permute-start | bytes 98312 | tf_op jit(solution)/shard_map/ppermute | solution.py:40
  36.1 0.1 broadcast_subtract_fusion
  36.1 0.1 xor.60
  36.2 0.1 sub.64
  36.3 0.1 dynamic_slice.64
  36.4 0.1 dynamic_slice.80
  36.4 0.1 sub.68
  36.5 1.4 %collective-permute-done.4 = f32[32,256]{1,0:T(8,128)S(1)} collective-permute-done((f32[32,256]{1,0:T(8,128)S(1)}, f32[32,256]{1,0:T(8,128)S(1)}, u32[]{:S(2)}, u32[]{:S(2)}) %collective-permute-start.4) | collective-permute-done | bytes 32800 | tf_op jit(solution)/shard_map/ppermute | solution.py:40
  38.0 0.7 %fusion.6 = bf16[32,256]{1,0:T(8,128)(2,1)} fusion(f32[32,256]{1,0:T(8,128)S(1)} %collective-permute-done.4, f32[2,32,256]{2,1,0:T(8,128)S(1)} %bitcast_add_fusion.2, s32[]{:T(128)S(6)} %select_n.100, f32[256]{0:T(256)S(1)} %sub.68, f32[32]{0:T(128)S(1)} %dynamic_slice.80, s32[256]{0:T(256)S(1)} %xor.64, s32[32]{0:T(128)S(1)} %dynamic_slice.64), kind=kLoop, calls=%fused_computation.17 | loop fusion | flops 49152 | bytes 84228 | tf_op jit(solution)/shard_map/convert_element_type | solution.py:84
  (7 shorter events, 0.1 us)
Async XLA Ops:
  0.0 6.5 %copy-start = (bf16[1024,1024]{1,0:T(8,128)(2,1)S(1)}, bf16[1024,1024]{1,0:T(8,128)(2,1)}, u32[]{:S(2)}) copy-start(bf16[1024,1024]{1,0:T(8,128)(2,1)} %param.7) | copy-start | bytes 6291460
  11.1 1.4 %copy-start.1 = (f32[1024,256]{1,0:T(8,128)}, f32[1024,256]{1,0:T(8,128)S(1)}, u32[]{:S(2)}) copy-start(f32[1024,256]{1,0:T(8,128)S(1)} %copy.13) | copy-start | bytes 3145732
  11.1 10.3 %copy-start.4 = (f32[512]{0:T(512)S(1)}, f32[512]{0:T(512)}, u32[]{:S(2)}) copy-start(f32[512]{0:T(512)} %param.12) | copy-start | bytes 6148
  12.1 13.1 %copy-start.2 = (s32[64]{0:T(128)S(1)}, s32[64]{0:T(128)}, u32[]{:S(2)}) copy-start(s32[64]{0:T(128)} %param.9) | copy-start | bytes 772
  12.1 2.3 %collective-permute-start = (f32[2,2,2,2,32,256]{5,4,3,2,1,0:T(8,128)}, f32[2,2,2,2,32,256]{5,4,3,2,1,0:T(8,128)}, u32[]{:S(2)}, u32[]{:S(2)}) collective-permute-start(f32[2,2,2,2,32,256]{5,4,3,2,1,0:T(8,128)} %dynamic-slice_bitcast_fusion), channel_id=1, source_target_pairs={{0,1},{1,0},{2,3},{3,2},{4,5},{5,4},{6,7},{7,6},{8,9},{9,8},{10,11... | collective-permute-start | bytes 1572872 | tf_op jit(solution)/shard_map/ppermute | solution.py:40
  12.5 17.8 %copy-start.3 = (f32[64]{0:T(128)S(1)}, f32[64]{0:T(128)}, u32[]{:S(2)}) copy-start(f32[64]{0:T(128)} %param.11) | copy-start | bytes 772
  15.7 7.3 %collective-permute-start.1 = (f32[2,2,2,32,256]{4,3,2,1,0:T(8,128)S(1)}, f32[2,2,2,32,256]{4,3,2,1,0:T(8,128)S(1)}, u32[]{:S(2)}, u32[]{:S(2)}) collective-permute-start(f32[2,2,2,32,256]{4,3,2,1,0:T(8,128)S(1)} %bitcast_select_fusion), channel_id=1, source_target_pairs={{0,2},{1,5},{2,0},{3,7},{4,6},{5,1},{6,4},{7,3},{8,10},{9,13},{10,... | collective-permute-start | bytes 786440 | tf_op jit(solution)/shard_map/ppermute | solution.py:40
  23.1 5.1 %collective-permute-start.2 = (f32[2,2,32,256]{3,2,1,0:T(8,128)S(1)}, f32[2,2,32,256]{3,2,1,0:T(8,128)S(1)}, u32[]{:S(2)}, u32[]{:S(2)}) collective-permute-start(f32[2,2,32,256]{3,2,1,0:T(8,128)S(1)} %dynamic-slice_bitcast_fusion.1), channel_id=1, source_target_pairs={{0,4},{1,3},{2,6},{3,1},{4,0},{5,7},{6,2},{7,5},{8,12},{9,11},{10,... | collective-permute-start | bytes 393224 | tf_op jit(solution)/shard_map/ppermute | solution.py:40
  28.2 4.4 %collective-permute-start.3 = (f32[2,32,256]{2,1,0:T(8,128)S(1)}, f32[2,32,256]{2,1,0:T(8,128)S(1)}, u32[]{:S(2)}, u32[]{:S(2)}) collective-permute-start(f32[2,32,256]{2,1,0:T(8,128)S(1)} %dynamic-slice_bitcast_fusion.2), channel_id=1, source_target_pairs={{0,8},{1,9},{2,10},{3,11},{4,12},{5,13},{6,14},{7,15},{8,0},{9,1},... | collective-permute-start | bytes 196616 | tf_op jit(solution)/shard_map/ppermute | solution.py:40
  32.6 5.3 %collective-permute-start.4 = (f32[32,256]{1,0:T(8,128)S(1)}, f32[32,256]{1,0:T(8,128)S(1)}, u32[]{:S(2)}, u32[]{:S(2)}) collective-permute-start(f32[32,256]{1,0:T(8,128)S(1)} %dynamic-slice_bitcast_fusion.3), channel_id=1, source_target_pairs={{0,16},{1,17},{2,18},{3,19},{4,20},{5,21},{6,22},{7,23},{8,24},{9,... | collective-permute-start | bytes 98312 | tf_op jit(solution)/shard_map/ppermute | solution.py:40

commit v4 on v3

--- a/solution.py
+++ b/solution.py
@@ -1,6 +1,8 @@
 import jax
 import jax.numpy as jnp
 from jax import lax
+from jax.experimental import pallas as pl
+from jax.experimental.pallas import tpu as pltpu
 from jax.sharding import PartitionSpec as P
 
 
@@ -41,6 +43,58 @@
     return buf.reshape(block, cols)
 
 
+def _masked_product_kernel(slab_ref, occ_s_ref, occ_v_ref, virt_v_ref, amp_ref, int_ref, out_ref):
+    virt_count = virt_v_ref.shape[0]
+    occ_count = occ_v_ref.shape[0]
+    kc_local, cols = int_ref.shape
+    occ_local = kc_local // virt_count
+    per_occ = cols // occ_count
+    second_start = slab_ref[1]
+    base = lax.axis_index("contr") * occ_local
+    f32, bf16 = jnp.float32, jnp.bfloat16
+    occ_rows = jnp.broadcast_to(occ_v_ref[...].reshape(1, occ_count), (8, occ_count)).astype(bf16)
+    virt_rows = jnp.broadcast_to(virt_v_ref[...].reshape(1, virt_count), (8, virt_count)).astype(bf16)
+    q_of = lax.broadcasted_iota(jnp.int32, (occ_count, cols), 1)
+    j_of = lax.broadcasted_iota(jnp.int32, (occ_count, cols), 0)
+    occ_pick = (q_of // per_occ == j_of).astype(bf16)
+    q_of = lax.broadcasted_iota(jnp.int32, (virt_count, cols), 1)
+    c_of = lax.broadcasted_iota(jnp.int32, (virt_count, cols), 0)
+    virt_pick = (c_of == second_start + q_of % per_occ).astype(bf16)
+    col_occ = jnp.dot(occ_rows, occ_pick, preferred_element_type=f32)
+    col_virt = jnp.dot(virt_rows, virt_pick, preferred_element_type=f32)
+    col_irrep = jnp.bitwise_xor(col_occ.astype(jnp.int32), col_virt.astype(jnp.int32))[0:1, :]
+    eye = (lax.broadcasted_iota(jnp.int32, (virt_count, virt_count), 0)
+           == lax.broadcasted_iota(jnp.int32, (virt_count, virt_count), 1)).astype(bf16)
+    virt_col = lax.dot_general(eye, virt_rows, (((1,), (1,)), ((), ())), preferred_element_type=f32)
+    virt_col = virt_col.astype(jnp.int32)[:, 0:1]
+    total = None
+    for k in range(occ_local):
+        kc_irrep = jnp.bitwise_xor(virt_col, occ_s_ref[base + k])
+        block = int_ref[k * virt_count:(k + 1) * virt_count, :]
+        masked = jnp.where(kc_irrep == col_irrep, block, jnp.zeros_like(block))
+        term = jnp.dot(amp_ref[:, k * virt_count:(k + 1) * virt_count], masked, preferred_element_type=f32)
+        total = term if total is None else total + term
+    out_ref[...] = total
+
+
+def masked_product(slab_start, occ_irrep, virt_irrep, amplitudes, integrals):
+    rows, kc_local = amplitudes.shape
+    cols = integrals.shape[1]
+    smem = pl.BlockSpec(memory_space=pltpu.SMEM)
+    vmem = pl.BlockSpec(memory_space=pltpu.VMEM)
+    return pl.pallas_call(
+        _masked_product_kernel,
+        out_shape=jax.ShapeDtypeStruct((rows, cols), jnp.float32),
+        in_specs=[smem, smem, vmem, vmem, vmem, vmem],
+        out_specs=vmem,
+        cost_estimate=pl.CostEstimate(
+            flops=2 * rows * kc_local * cols,
+            bytes_accessed=2 * rows * kc_local + 2 * kc_local * cols + 4 * rows * cols,
+            transcendentals=0,
+        ),
+    )(slab_start, occ_irrep, occ_irrep, virt_irrep, amplitudes, integrals)
+
+
 def body(amplitudes, integrals, occ_irrep, virt_irrep, occ_energy, virt_energy, slab_start):
     pair_count = lax.axis_size("pair")
     contr_count = lax.axis_size("contr")
@@ -64,12 +118,8 @@
     col_irrep = jnp.bitwise_xor(occ_irrep[:, None], b_irrep[None, :]).reshape(-1)
     row_energy = (occ_energy[:, None] - a_energy[None, :]).reshape(-1)
     col_energy = (occ_energy[:, None] - b_energy[None, :]).reshape(-1)
-    local_occ = lax.dynamic_slice(occ_irrep, (contr_index * occ_local,), (occ_local,))
-    kc_irrep = jnp.bitwise_xor(local_occ[:, None], virt_irrep[None, :]).reshape(-1)
-    zero = jnp.zeros((), jnp.bfloat16)
     whole_int = lax.all_gather(integrals, "pair", axis=1, tiled=True)
-    int_masked = jnp.where(kc_irrep[:, None] == col_irrep[None, :], whole_int, zero)
-    partial = jnp.dot(amplitudes, int_masked, preferred_element_type=jnp.float32)
+    partial = masked_product(slab_start, occ_irrep, virt_irrep, amplitudes, whole_int)
     if contr_count & (contr_count - 1) == 0 and rows_pair % contr_count == 0:
         summed = halving_scatter(partial, "contr", contr_count, contr_index)
     else:

time: 39 us -> 30.6 us (0.78)
  local copies, waits for them, and re-layouts: 6.96 us -> 2.86 us
  Pallas kernels: 0 us -> 3.92 us
  matrix products: 3.04 us -> 0 us
  other arithmetic: 3.77 us -> 1.17 us
  starting transfers between devices: 11.1 us -> 9.59 us
  waiting for transfers between devices: 9.83 us -> 8.82 us
    pallas_call x0 -> x1, Pallas kernels: none -> 3.92 us  [masked_product(): pl.pallas_call(_masked_product_kernel, out_shape=jax.ShapeDtypeStruct((ro...]
    dot_general x1 -> x0, matrix products: 3.04 us -> none  [body(): jnp.dot(amplitudes, int_masked, preferred_element_type=jnp.float32)]
    dot_general x1 -> x0, local copies, waits for them, and re-layouts: 1.55 us -> none  [body(): jnp.dot(amplitudes, int_masked, preferred_element_type=jnp.float32)]
    ppermute x5, starting transfers between devices: 11.1 us -> 9.59 us  [halving_scatter(): buf = keep + lax.ppermute(send, axis, perm)]
    add x4, other arithmetic: 1.35 us -> 0.16 us  [halving_scatter(): buf = keep + lax.ppermute(send, axis, perm)]
    ppermute x5, waiting for transfers between devices: 9.83 us -> 8.82 us  [halving_scatter(): buf = keep + lax.ppermute(send, axis, perm)]
    squeeze x4 -> x3, local copies, waits for them, and re-layouts: 0.99 us -> 0.05 us  [halving_scatter(): send = lax.dynamic_index_in_dim(buf, 1 - bit, axis=where[0], keepdims=False)]
    unnamed x1 -> x0, other arithmetic: 0.75 us -> none
  transfers between devices with their start and end apart: 5 -> 5, of which waited for: 5 -> 4; matrix products, arithmetic and copies ran while one was open for 4% -> 6% of each run, Pallas kernels for 0% -> 0%
where the time goes in v4:
time: 30.6 us; the launch traced here: 30.4 us
  starting transfers between devices  9.59 us (31%)
  waiting for transfers between devices  8.82 us (29%)
  between operations  3.99 us (13%)
  Pallas kernels  3.92 us (13%)
  local copies, waits for them, and re-layouts  2.86 us (9%)
  other arithmetic  1.17 us (4%)
    ppermute x5, starting transfers between devices, halving_scatter(): buf = keep + lax.ppermute(send, axis, perm)  9.59 us
    ppermute x5, waiting for transfers between devices, halving_scatter(): buf = keep + lax.ppermute(send, axis, perm)  8.82 us
    pallas_call x1, Pallas kernels, masked_product(): pl.pallas_call(_masked_product_kernel, out_shape=jax.ShapeDtypeStruct((ro...  3.92 us
    dynamic_slice x1, local copies, waits for them, and re-layouts, halving_scatter(): keep = lax.dynamic_index_in_dim(buf, bit, axis=where[0], keepdims=False)  1.29 us
    convert_element_type x1, other arithmetic, body(): (summed / (mine_energy[:, None] + col_energy[None, :])).astype(jnp.bfloat16)  0.69 us
  transfers between devices with their start and end apart: 5, of which 4 were waited for; matrix products, arithmetic and copies ran while one was open for 6% of the time, Pallas kernels for 0%

profile of v4, /device:TPU:0, one launch (start us, length us, event | category | flops | bytes accessed | tf_op | source)
XLA Modules:
  0.0 30.4 jit_solution(2461676234474130831)
XLA Ops:
  0.0 3.9 %shard_map.73 = f32[1024,256]{1,0:T(8,128)} custom-call(s32[2]{0:T(128)} %slab_ref.1, s32[64]{0:T(128)} %occ_v_ref.1, s32[64]{0:T(128)} %occ_v_ref.1, s32[512]{0:T(512)} %virt_v_ref.1, bf16[1024,1024]{1,0:T(8,128)(2,1)} %amp_ref.1, bf16[1024,256]{1,0:T(8,128)(2,1)} %int_ref), custom_call_target="tpu_custom_call" | custom-call | flops 536870912 | bytes 3670016 | tf_op jit(solution)/shard_map/pallas_call | solution.py:85
  3.9 1.3 %constant_dynamic-slice_fusion.3 = (f32[2,2,2,2,1,32,256]{6,5,4,3,2,1,0:T(8,128)S(1)}, f32[2,2,2,2,1,32,256]{6,5,4,3,2,1,0:T(8,128)S(1)}) fusion(f32[2,2,2,2,2,32,256]{6,5,4,3,2,1,0:T(8,128)} %bitcast.36, s32[]{:T(128)S(6)} %select_n.78, s32[]{:T(128)S(6)} %select_n.79), kind=kLoop, calls=%fused_computation.21 | loop fusion | bytes 2097160 | tf_op jit(solution)/shard_map/jit(dynamic_index_in_dim)/dynamic_slice | solution.py:29
  5.2 0.0 copy-start.1
  5.2 0.0 copy-start.2
  5.2 0.0 copy-start.4
  5.3 0.0 copy-start
  5.3 0.5 %collective-permute-start = (f32[2,2,2,2,32,256]{5,4,2,1,0,3:T(8,128)S(1)}, f32[2,2,2,2,32,256]{5,4,2,1,0,3:T(8,128)S(1)}, u32[]{:S(2)}, u32[]{:S(2)}) collective-permute-start(f32[2,2,2,2,32,256]{5,4,2,1,0,3:T(8,128)S(1)} %bitcast.37), channel_id=1, source_target_pairs={{0,1},{1,0},{2,3},{3,2},{4,5},{5,4},{6,7},{7,6},{8,9},{9,8},{10,11... | collective-permute-start | bytes 1572872 | tf_op jit(solution)/shard_map/ppermute | solution.py:42
  5.8 1.5 %collective-permute-done = f32[2,2,2,2,32,256]{5,4,2,1,0,3:T(8,128)S(1)} collective-permute-done((f32[2,2,2,2,32,256]{5,4,2,1,0,3:T(8,128)S(1)}, f32[2,2,2,2,32,256]{5,4,2,1,0,3:T(8,128)S(1)}, u32[]{:S(2)}, u32[]{:S(2)}) %collective-permute-start) | collective-permute-done | bytes 524320 | tf_op jit(solution)/shard_map/ppermute | solution.py:42
  7.4 0.0 copy-start.3
  7.4 0.1 bitcast_add_fusion
  7.6 2.9 %collective-permute-start.1 = (f32[2,2,2,32,256]{4,3,2,1,0:T(8,128)S(1)}, f32[2,2,2,32,256]{4,3,2,1,0:T(8,128)S(1)}, u32[]{:S(2)}, u32[]{:S(2)}) collective-permute-start(f32[2,2,2,32,256]{4,3,2,1,0:T(8,128)S(1)} %bitcast_select_fusion), channel_id=1, source_target_pairs={{0,2},{1,5},{2,0},{3,7},{4,6},{5,1},{6,4},{7,3},{8,10},{9,13},{10,... | collective-permute-start | bytes 786440 | tf_op jit(solution)/shard_map/ppermute | solution.py:42
  10.5 0.0 copy-done.1
  10.5 0.6 %fusion.4 = (s32[1]{0:T(128)}, s32[1]{0:T(128)}) fusion(s32[2]{0:T(128)S(1)} %copy-done.1), kind=kLoop, calls=%fused_computation.22 | loop fusion | bytes 16 | tf_op jit(solution)/shard_map/slice | solution.py:111
  14.3 0.0 copy-done.2
  14.3 0.1 dynamic_slice.60
  14.4 0.0 copy-done.4
  14.4 0.1 dynamic_slice.75
  15.1 0.1 dynamic_slice.77
  15.2 0.0 copy-done
  15.2 0.1 broadcast_xor_fusion.1
  15.3 0.0 collective-permute-done.1
  15.3 0.1 fusion
  15.4 1.7 %collective-permute-start.2 = (f32[2,2,32,256]{3,2,1,0:T(8,128)S(1)}, f32[2,2,32,256]{3,2,1,0:T(8,128)S(1)}, u32[]{:S(2)}, u32[]{:S(2)}) collective-permute-start(f32[2,2,32,256]{3,2,1,0:T(8,128)S(1)} %dynamic-slice_bitcast_fusion), channel_id=1, source_target_pairs={{0,4},{1,3},{2,6},{3,1},{4,0},{5,7},{6,2},{7,5},{8,12},{9,11},{10,... | collective-permute-start | bytes 393224 | tf_op jit(solution)/shard_map/ppermute | solution.py:42
  17.0 0.0 copy-done.3
  17.0 0.1 broadcast_subtract_fusion.1
  17.1 3.3 %collective-permute-done.2 = f32[2,2,32,256]{3,2,1,0:T(8,128)S(1)} collective-permute-done((f32[2,2,32,256]{3,2,1,0:T(8,128)S(1)}, f32[2,2,32,256]{3,2,1,0:T(8,128)S(1)}, u32[]{:S(2)}, u32[]{:S(2)}) %collective-permute-start.2) | collective-permute-done | bytes 131104 | tf_op jit(solution)/shard_map/ppermute | solution.py:42
  20.4 1.7 %collective-permute-start.3 = (f32[2,32,256]{2,1,0:T(8,128)S(1)}, f32[2,32,256]{2,1,0:T(8,128)S(1)}, u32[]{:S(2)}, u32[]{:S(2)}) collective-permute-start(f32[2,32,256]{2,1,0:T(8,128)S(1)} %dynamic-slice_bitcast_fusion.1), channel_id=1, source_target_pairs={{0,8},{1,9},{2,10},{3,11},{4,12},{5,13},{6,14},{7,15},{8,0},{9,1},... | collective-permute-start | bytes 196616 | tf_op jit(solution)/shard_map/ppermute | solution.py:42
  22.2 0.1 broadcast_subtract_fusion
  22.2 0.1 dynamic_slice.62
  22.3 2.5 %collective-permute-done.3 = f32[2,32,256]{2,1,0:T(8,128)S(1)} collective-permute-done((f32[2,32,256]{2,1,0:T(8,128)S(1)}, f32[2,32,256]{2,1,0:T(8,128)S(1)}, u32[]{:S(2)}, u32[]{:S(2)}) %collective-permute-start.3) | collective-permute-done | bytes 65568 | tf_op jit(solution)/shard_map/ppermute | solution.py:42
  24.8 2.7 %collective-permute-start.4 = (f32[32,256]{1,0:T(8,128)S(1)}, f32[32,256]{1,0:T(8,128)S(1)}, u32[]{:S(2)}, u32[]{:S(2)}) collective-permute-start(f32[32,256]{1,0:T(8,128)S(1)} %dynamic-slice_bitcast_fusion.2), channel_id=1, source_target_pairs={{0,16},{1,17},{2,18},{3,19},{4,20},{5,21},{6,22},{7,23},{8,24},{9,... | collective-permute-start | bytes 98312 | tf_op jit(solution)/shard_map/ppermute | solution.py:42
  27.5 0.1 broadcast_xor_fusion
  27.6 0.1 xor.40
  27.7 0.1 sub.64
  27.8 0.1 dynamic_slice.61
  27.8 0.1 dynamic_slice.76
  27.9 0.1 sub.68
  28.0 0.1 xor.44
  28.1 1.5 %collective-permute-done.4 = f32[32,256]{1,0:T(8,128)S(1)} collective-permute-done((f32[32,256]{1,0:T(8,128)S(1)}, f32[32,256]{1,0:T(8,128)S(1)}, u32[]{:S(2)}, u32[]{:S(2)}) %collective-permute-start.4) | collective-permute-done | bytes 32800 | tf_op jit(solution)/shard_map/ppermute | solution.py:42
  29.7 0.7 %fusion.3 = bf16[32,256]{1,0:T(8,128)(2,1)} fusion(f32[32,256]{1,0:T(8,128)S(1)} %collective-permute-done.4, f32[2,32,256]{2,1,0:T(8,128)S(1)} %bitcast_add_fusion.2, s32[]{:T(128)S(6)} %select_n.91, f32[256]{0:T(256)S(1)} %sub.68, f32[32]{0:T(128)S(1)} %dynamic_slice.76, s32[256]{0:T(256)S(1)} %xor.44, s32[32]{0:T(128)S(1)} %dynamic_slice.61), kind=kLoop, calls=%fused_computation.12 | loop fusion | flops 49152 | bytes 84228 | tf_op jit(solution)/shard_map/convert_element_type | solution.py:134
  (8 shorter events, 0.2 us)
Async XLA Ops:
  5.2 5.3 %copy-start.1 = (s32[2]{0:T(128)S(1)}, s32[2]{0:T(128)}, u32[]{:S(2)}) copy-start(s32[2]{0:T(128)} %slab_ref.1) | copy-start | bytes 28
  5.2 9.1 %copy-start.2 = (s32[512]{0:T(512)S(1)}, s32[512]{0:T(512)}, u32[]{:S(2)}) copy-start(s32[512]{0:T(512)} %virt_v_ref.1) | copy-start | bytes 6148
  5.2 9.1 %copy-start.4 = (f32[512]{0:T(512)S(1)}, f32[512]{0:T(512)}, u32[]{:S(2)}) copy-start(f32[512]{0:T(512)} %param.12) | copy-start | bytes 6148
  5.3 9.9 %copy-start = (s32[64]{0:T(128)S(1)}, s32[64]{0:T(128)}, u32[]{:S(2)}) copy-start(s32[64]{0:T(128)} %occ_v_ref.1) | copy-start | bytes 772
  5.3 2.1 %collective-permute-start = (f32[2,2,2,2,32,256]{5,4,2,1,0,3:T(8,128)S(1)}, f32[2,2,2,2,32,256]{5,4,2,1,0,3:T(8,128)S(1)}, u32[]{:S(2)}, u32[]{:S(2)}) collective-permute-start(f32[2,2,2,2,32,256]{5,4,2,1,0,3:T(8,128)S(1)} %bitcast.37), channel_id=1, source_target_pairs={{0,1},{1,0},{2,3},{3,2},{4,5},{5,4},{6,7},{7,6},{8,9},{9,8},{10,11... | collective-permute-start | bytes 1572872 | tf_op jit(solution)/shard_map/ppermute | solution.py:42
  7.4 9.7 %copy-start.3 = (f32[64]{0:T(128)S(1)}, f32[64]{0:T(128)}, u32[]{:S(2)}) copy-start(f32[64]{0:T(128)} %param.11) | copy-start | bytes 772
  7.6 7.7 %collective-permute-start.1 = (f32[2,2,2,32,256]{4,3,2,1,0:T(8,128)S(1)}, f32[2,2,2,32,256]{4,3,2,1,0:T(8,128)S(1)}, u32[]{:S(2)}, u32[]{:S(2)}) collective-permute-start(f32[2,2,2,32,256]{4,3,2,1,0:T(8,128)S(1)} %bitcast_select_fusion), channel_id=1, source_target_pairs={{0,2},{1,5},{2,0},{3,7},{4,6},{5,1},{6,4},{7,3},{8,10},{9,13},{10,... | collective-permute-start | bytes 786440 | tf_op jit(solution)/shard_map/ppermute | solution.py:42
  15.4 5.0 %collective-permute-start.2 = (f32[2,2,32,256]{3,2,1,0:T(8,128)S(1)}, f32[2,2,32,256]{3,2,1,0:T(8,128)S(1)}, u32[]{:S(2)}, u32[]{:S(2)}) collective-permute-start(f32[2,2,32,256]{3,2,1,0:T(8,128)S(1)} %dynamic-slice_bitcast_fusion), channel_id=1, source_target_pairs={{0,4},{1,3},{2,6},{3,1},{4,0},{5,7},{6,2},{7,5},{8,12},{9,11},{10,... | collective-permute-start | bytes 393224 | tf_op jit(solution)/shard_map/ppermute | solution.py:42
  20.4 4.3 %collective-permute-start.3 = (f32[2,32,256]{2,1,0:T(8,128)S(1)}, f32[2,32,256]{2,1,0:T(8,128)S(1)}, u32[]{:S(2)}, u32[]{:S(2)}) collective-permute-start(f32[2,32,256]{2,1,0:T(8,128)S(1)} %dynamic-slice_bitcast_fusion.1), channel_id=1, source_target_pairs={{0,8},{1,9},{2,10},{3,11},{4,12},{5,13},{6,14},{7,15},{8,0},{9,1},... | collective-permute-start | bytes 196616 | tf_op jit(solution)/shard_map/ppermute | solution.py:42
  24.8 4.9 %collective-permute-start.4 = (f32[32,256]{1,0:T(8,128)S(1)}, f32[32,256]{1,0:T(8,128)S(1)}, u32[]{:S(2)}, u32[]{:S(2)}) collective-permute-start(f32[32,256]{1,0:T(8,128)S(1)} %dynamic-slice_bitcast_fusion.2), channel_id=1, source_target_pairs={{0,16},{1,17},{2,18},{3,19},{4,20},{5,21},{6,22},{7,23},{8,24},{9,... | collective-permute-start | bytes 98312 | tf_op jit(solution)/shard_map/ppermute | solution.py:42

commit v5 on v4

--- a/solution.py
+++ b/solution.py
@@ -3,13 +3,13 @@
 from jax import lax
 from jax.experimental import pallas as pl
 from jax.experimental.pallas import tpu as pltpu
-from jax.sharding import PartitionSpec as P
+from jax.sharding import Mesh, PartitionSpec as P
 
 
-def halving_scatter(partial, axis, count, index):
+def halving_scatter(partial, axes, count, index, tail):
     rows, cols = partial.shape
     block = rows // count
-    bits = count.bit_length() - 1
+    bits = (count // tail).bit_length() - 1
     first = (index & 1) == 0
 
     def order(c):
@@ -18,11 +18,11 @@
             seq[1], seq[2] = seq[2], seq[1]
         return seq
 
-    buf = partial.reshape((2,) * bits + (block, cols))
+    buf = partial.reshape((tail,) + (2,) * bits + (block, cols))
     left = [list(range(bits - 1, -1, -1)) for _ in range(2)]
     for stage in range(bits):
         split = [order(c)[stage] for c in range(2)]
-        where = [left[c].index(split[c]) for c in range(2)]
+        where = [1 + left[c].index(split[c]) for c in range(2)]
         mine = [(index >> split[c]) & 1 for c in range(2)]
         if where[0] == where[1]:
             bit = jnp.where(first, mine[0], mine[1]) if split[0] != split[1] else mine[0]
@@ -37,10 +37,14 @@
             keep = jnp.where(first, picks[0][0], picks[1][0])
             send = jnp.where(first, picks[0][1], picks[1][1])
         for c in range(2):
-            left[c].pop(where[c])
+            left[c].pop(where[c] - 1)
         perm = [(i, i ^ (1 << order(i & 1)[stage])) for i in range(count)]
-        buf = keep + lax.ppermute(send, axis, perm)
-    return buf.reshape(block, cols)
+        buf = keep + lax.ppermute(send, axes, perm)
+    buf = buf.reshape(tail * block, cols)
+    if tail > 1:
+        got = lax.all_to_all(buf, axes[0], 0, 0, tiled=True)
+        buf = got.reshape(tail, block, cols).sum(axis=0)
+    return buf
 
 
 def _masked_product_kernel(slab_ref, occ_s_ref, occ_v_ref, virt_v_ref, amp_ref, int_ref, out_ref):
@@ -50,7 +54,7 @@
     occ_local = kc_local // virt_count
     per_occ = cols // occ_count
     second_start = slab_ref[1]
-    base = lax.axis_index("contr") * occ_local
+    base = (lax.axis_index("hi") * lax.axis_size("lo") + lax.axis_index("lo")) * occ_local
     f32, bf16 = jnp.float32, jnp.bfloat16
     occ_rows = jnp.broadcast_to(occ_v_ref[...].reshape(1, occ_count), (8, occ_count)).astype(bf16)
     virt_rows = jnp.broadcast_to(virt_v_ref[...].reshape(1, virt_count), (8, virt_count)).astype(bf16)
@@ -97,9 +101,9 @@
 
 def body(amplitudes, integrals, occ_irrep, virt_irrep, occ_energy, virt_energy, slab_start):
     pair_count = lax.axis_size("pair")
-    contr_count = lax.axis_size("contr")
+    contr_count = lax.axis_size("hi") * lax.axis_size("lo")
     pair_index = lax.axis_index("pair")
-    contr_index = lax.axis_index("contr")
+    contr_index = lax.axis_index("hi") * lax.axis_size("lo") + lax.axis_index("lo")
     virt_count = virt_irrep.shape[0]
     kc_local = integrals.shape[0]
     occ_local = kc_local // virt_count
@@ -120,10 +124,7 @@
     col_energy = (occ_energy[:, None] - b_energy[None, :]).reshape(-1)
     whole_int = lax.all_gather(integrals, "pair", axis=1, tiled=True)
     partial = masked_product(slab_start, occ_irrep, virt_irrep, amplitudes, whole_int)
-    if contr_count & (contr_count - 1) == 0 and rows_pair % contr_count == 0:
-        summed = halving_scatter(partial, "contr", contr_count, contr_index)
-    else:
-        summed = lax.psum_scatter(partial, "contr", scatter_dimension=0, tiled=True)
+    summed = halving_scatter(partial, ("hi", "lo"), contr_count, contr_index, lax.axis_size("hi"))
     mine_irrep = lax.dynamic_slice(
         row_irrep, (pair_index * rows_pair + contr_index * rows_device,), (rows_device,)
     )
@@ -136,6 +137,10 @@
 
 
 def solution(mesh):
-    in_specs = (P("pair", "contr"), P("contr", "pair"), P(), P(), P(), P(), P())
-    out_specs = P(("pair", "contr"), None)
-    return jax.shard_map(body, mesh=mesh, in_specs=in_specs, out_specs=out_specs, check_vma=False)
+    pair_count, contr_count = mesh.devices.shape
+    lo = 8 if contr_count % 8 == 0 and contr_count & (contr_count - 1) == 0 else contr_count
+    view = Mesh(mesh.devices.reshape(pair_count, contr_count // lo, lo), ("pair", "hi", "lo"))
+    contr = ("hi", "lo")
+    in_specs = (P("pair", contr), P(contr, "pair"), P(), P(), P(), P(), P())
+    out_specs = P(("pair",) + contr, None)
+    return jax.shard_map(body, mesh=view, in_specs=in_specs, out_specs=out_specs, check_vma=False)

time: 30.6 us -> 34.5 us (1.13)
  other arithmetic: 1.17 us -> 2.86 us
  waiting for transfers between devices: 8.82 us -> 10.3 us
  starting transfers between devices: 9.59 us -> 10.6 us
    all_to_all x0 -> x1, waiting for transfers between devices: none -> 5.74 us  [halving_scatter(): got = lax.all_to_all(buf, axes[0], 0, 0, tiled=True)]
    all_to_all x0 -> x1, starting transfers between devices: none -> 5.37 us  [halving_scatter(): got = lax.all_to_all(buf, axes[0], 0, 0, tiled=True)]
    ppermute x5 -> x3, starting transfers between devices: 9.59 us -> 5.22 us  [halving_scatter(): buf = keep + lax.ppermute(send, axes, perm)]
    ppermute x5 -> x3, waiting for transfers between devices: 8.82 us -> 4.55 us  [halving_scatter(): buf = keep + lax.ppermute(send, axes, perm)]
    add x4 -> x3, other arithmetic: 0.16 us -> 1.83 us  [halving_scatter(): buf = keep + lax.ppermute(send, axes, perm)]
    dynamic_slice x3 -> x0, local copies, waits for them, and re-layouts: 1.37 us -> none  [the longest x1 1.29 us: halving_scatter(): keep = lax.dynamic_index_in_dim(buf, bit, axis=where[0], keepdims=False)]
    squeeze x3 -> x2, local copies, waits for them, and re-layouts: 0.05 us -> 1.13 us  [halving_scatter(): send = lax.dynamic_index_in_dim(buf, 1 - bit, axis=where[0], keepdims=False)]
  transfers between devices with their start and end apart: 5 -> 4, of which waited for: 4 -> 3; matrix products, arithmetic and copies ran while one was open for 6% -> 5% of each run, Pallas kernels for 0% -> 0%
where the time goes in v5:
time: 34.5 us; the launch traced here: 34.1 us
  starting transfers between devices  10.6 us (31%)
  waiting for transfers between devices  10.3 us (30%)
  Pallas kernels  3.94 us (11%)
  between operations  3.89 us (11%)
  other arithmetic  2.86 us (8%)
  local copies, waits for them, and re-layouts  2.58 us (7%)
    all_to_all x1, waiting for transfers between devices, halving_scatter(): got = lax.all_to_all(buf, axes[0], 0, 0, tiled=True)  5.74 us
    all_to_all x1, starting transfers between devices, halving_scatter(): got = lax.all_to_all(buf, axes[0], 0, 0, tiled=True)  5.37 us
    ppermute x3, starting transfers between devices, halving_scatter(): buf = keep + lax.ppermute(send, axes, perm)  5.22 us
    ppermute x3, waiting for transfers between devices, halving_scatter(): buf = keep + lax.ppermute(send, axes, perm)  4.55 us
    pallas_call x1, Pallas kernels, masked_product(): pl.pallas_call(_masked_product_kernel, out_shape=jax.ShapeDtypeStruct((ro...  3.94 us
    add x3, other arithmetic, halving_scatter(): buf = keep + lax.ppermute(send, axes, perm)  1.83 us
    squeeze x2, local copies, waits for them, and re-layouts, halving_scatter(): send = lax.dynamic_index_in_dim(buf, 1 - bit, axis=where[0], keepdims=False)  1.13 us
  transfers between devices with their start and end apart: 4, of which 3 were waited for; matrix products, arithmetic and copies ran while one was open for 5% of the time, Pallas kernels for 0%

profile of v5, /device:TPU:0, one launch (start us, length us, event | category | flops | bytes accessed | tf_op | source)
XLA Modules:
  0.0 34.1 jit_solution(2163438529570780520)
XLA Ops:
  0.0 0.0 copy-start.1
  0.0 0.0 copy-start.2
  0.0 3.9 %shard_map.73 = f32[1024,256]{1,0:T(8,128)} custom-call(s32[2]{0:T(128)} %slab_ref.1, s32[64]{0:T(128)} %occ_v_ref.1, s32[64]{0:T(128)} %occ_v_ref.1, s32[512]{0:T(512)} %virt_v_ref.1, bf16[1024,1024]{1,0:T(8,128)(2,1)} %amp_ref.1, bf16[1024,256]{1,0:T(8,128)(2,1)} %int_ref), custom_call_target="tpu_custom_call" | custom-call | flops 536870912 | bytes 3670016 | tf_op jit(solution)/shard_map/pallas_call | solution.py:89
  3.9 0.0 copy-start
  3.9 0.0 copy-start.4
  3.9 0.0 copy-start.3
  4.0 1.1 %dynamic-slice_bitcast_fusion = f32[4,2,2,32,256]{4,3,2,1,0:T(8,128)S(1)} fusion(f32[4,2,2,2,32,256]{5,4,3,2,1,0:T(8,128)} %bitcast.21, s32[]{:T(128)S(6)} %select_n.65), kind=kLoop, calls=%fused_computation.1 | loop fusion | bytes 1048580 | tf_op jit(solution)/shard_map/jit(dynamic_index_in_dim)/squeeze | solution.py:30
  5.1 0.5 %collective-permute-start = (f32[4,2,2,32,256]{4,3,2,1,0:T(8,128)S(1)}, f32[4,2,2,32,256]{4,3,2,1,0:T(8,128)S(1)}, u32[]{:S(2)}, u32[]{:S(2)}) collective-permute-start(f32[4,2,2,32,256]{4,3,2,1,0:T(8,128)S(1)} %dynamic-slice_bitcast_fusion), channel_id=1, source_target_pairs={{0,1},{1,0},{2,3},{3,2},{4,5},{5,4},{6,7},{7,6},{8,9},{9,8},{10,11... | collective-permute-start | bytes 1572872 | tf_op jit(solution)/shard_map/ppermute | solution.py:42
  5.6 0.0 copy-done.1
  5.6 0.6 %fusion.1 = (s32[1]{0:T(128)}, s32[1]{0:T(128)}) fusion(s32[2]{0:T(128)S(1)} %copy-done.1), kind=kLoop, calls=%fused_computation.12 | loop fusion | bytes 16 | tf_op jit(solution)/shard_map/slice | solution.py:115
  8.1 0.0 copy-done.2
  8.2 0.1 dynamic_slice.46
  8.2 0.0 collective-permute-done
  8.2 1.1 %bitcast_add_fusion = f32[4,2,2,32,256]{4,3,2,1,0:T(8,128)S(1)} fusion(f32[4,2,2,32,256]{4,3,2,1,0:T(8,128)S(1)} %collective-permute-done, f32[4,2,2,2,32,256]{5,4,3,2,1,0:T(8,128)} %bitcast.22, s32[]{:T(128)S(6)} %select_n.64), kind=kLoop, calls=%fused_computation | loop fusion | flops 131072 | bytes 1572868 | tf_op jit(solution)/shard_map/add | solution.py:42
  9.4 2.6 %collective-permute-start.1 = (f32[4,2,32,256]{3,2,1,0:T(8,128)S(1)}, f32[4,2,32,256]{3,2,1,0:T(8,128)S(1)}, u32[]{:S(2)}, u32[]{:S(2)}) collective-permute-start(f32[4,2,32,256]{3,2,1,0:T(8,128)S(1)} %bitcast_select_fusion), channel_id=1, source_target_pairs={{0,2},{1,5},{2,0},{3,7},{4,6},{5,1},{6,4},{7,3},{8,10},{9,13},{10,... | collective-permute-start | bytes 786440 | tf_op jit(solution)/shard_map/ppermute | solution.py:42
  12.0 0.0 copy-done
  12.0 0.1 broadcast_xor_fusion.1
  13.3 0.0 copy-done.4
  13.3 0.1 dynamic_slice.57
  14.0 0.1 dynamic_slice.59
  14.1 0.1 dynamic_slice.48
  14.2 0.1 xor.40
  14.3 0.0 copy-done.3
  14.3 0.1 broadcast_subtract_fusion.1
  14.3 0.1 sub.56
  14.4 0.1 dynamic_slice.47
  14.5 0.1 dynamic_slice.58
  14.6 1.8 %collective-permute-done.1 = f32[4,2,32,256]{3,2,1,0:T(8,128)S(1)} collective-permute-done((f32[4,2,32,256]{3,2,1,0:T(8,128)S(1)}, f32[4,2,32,256]{3,2,1,0:T(8,128)S(1)}, u32[]{:S(2)}, u32[]{:S(2)}) %collective-permute-start.1) | collective-permute-done | bytes 262176 | tf_op jit(solution)/shard_map/ppermute | solution.py:42
  16.3 0.1 fusion
  16.4 2.1 %collective-permute-start.2 = (f32[4,32,256]{2,1,0:T(8,128)S(1)}, f32[4,32,256]{2,1,0:T(8,128)S(1)}, u32[]{:S(2)}, u32[]{:S(2)}) collective-permute-start(f32[4,32,256]{2,1,0:T(8,128)S(1)} %dynamic-slice_bitcast_fusion.1), channel_id=1, source_target_pairs={{0,4},{1,3},{2,6},{3,1},{4,0},{5,7},{6,2},{7,5},{8,12},{9,11},{10,... | collective-permute-start | bytes 393224 | tf_op jit(solution)/shard_map/ppermute | solution.py:42
  18.5 0.1 broadcast_subtract_fusion
  18.6 0.1 sub.60
  18.7 2.8 %collective-permute-done.2 = f32[4,32,256]{2,1,0:T(8,128)S(1)} collective-permute-done((f32[4,32,256]{2,1,0:T(8,128)S(1)}, f32[4,32,256]{2,1,0:T(8,128)S(1)}, u32[]{:S(2)}, u32[]{:S(2)}) %collective-permute-start.2) | collective-permute-done | bytes 131104 | tf_op jit(solution)/shard_map/ppermute | solution.py:42
  21.5 0.7 %bitcast_add_fusion.1 = f32[4,32,256]{2,1,0:T(8,128)} fusion(f32[4,32,256]{2,1,0:T(8,128)S(1)} %collective-permute-done.2, f32[4,2,32,256]{3,2,1,0:T(8,128)S(1)} %fusion, s32[]{:T(128)S(6)} %select_n.73), kind=kLoop, calls=%fused_computation.5 | loop fusion | flops 32768 | bytes 393220 | tf_op jit(solution)/shard_map/add | solution.py:42
  22.1 5.4 %all-to-all-start = ((f32[4,32,256]{2,1,0:T(8,128)}), f32[4,32,256]{2,1,0:T(8,128)S(1)}, u32[]{:S(2)}, u32[]{:S(2)}) async-start(f32[4,32,256]{2,1,0:T(8,128)} %bitcast_add_fusion.1), calls=%async_computation | async-start | bytes 262144 | tf_op jit(solution)/shard_map/all_to_all | solution.py:45
  27.5 0.1 broadcast_xor_fusion
  27.6 0.1 xor.44
  27.7 5.7 %all-to-all-done = f32[4,32,256]{2,1,0:T(8,128)S(1)} async-done(((f32[4,32,256]{2,1,0:T(8,128)}), f32[4,32,256]{2,1,0:T(8,128)S(1)}, u32[]{:S(2)}, u32[]{:S(2)}) %all-to-all-start) | async-done | bytes 131104 | tf_op jit(solution)/shard_map/all_to_all | solution.py:45
  33.5 0.7 %divide_convert_fusion = bf16[32,256]{1,0:T(8,128)(2,1)} fusion(f32[32,256]{1,0:T(8,128)S(1)} %reduce_sum.9, f32[256]{0:T(256)S(1)} %sub.60, f32[32]{0:T(128)S(1)} %dynamic_slice.58, s32[256]{0:T(256)S(1)} %xor.44, s32[32]{0:T(128)S(1)} %dynamic_slice.47), kind=kLoop, calls=%fused_computation.7 | loop fusion | flops 40960 | bytes 51456 | tf_op jit(solution)/shard_map/convert_element_type | solution.py:135
  (3 shorter events, 0.1 us)
Async XLA Ops:
  0.0 5.6 %copy-start.1 = (s32[2]{0:T(128)S(1)}, s32[2]{0:T(128)}, u32[]{:S(2)}) copy-start(s32[2]{0:T(128)} %slab_ref.1) | copy-start | bytes 28
  0.0 8.1 %copy-start.2 = (s32[512]{0:T(512)S(1)}, s32[512]{0:T(512)}, u32[]{:S(2)}) copy-start(s32[512]{0:T(512)} %virt_v_ref.1) | copy-start | bytes 6148
  3.9 8.0 %copy-start = (s32[64]{0:T(128)S(1)}, s32[64]{0:T(128)}, u32[]{:S(2)}) copy-start(s32[64]{0:T(128)} %occ_v_ref.1) | copy-start | bytes 772
  3.9 9.4 %copy-start.4 = (f32[512]{0:T(512)S(1)}, f32[512]{0:T(512)}, u32[]{:S(2)}) copy-start(f32[512]{0:T(512)} %param.12) | copy-start | bytes 6148
  3.9 10.3 %copy-start.3 = (f32[64]{0:T(128)S(1)}, f32[64]{0:T(128)}, u32[]{:S(2)}) copy-start(f32[64]{0:T(128)} %param.11) | copy-start | bytes 772
  5.1 3.2 %collective-permute-start = (f32[4,2,2,32,256]{4,3,2,1,0:T(8,128)S(1)}, f32[4,2,2,32,256]{4,3,2,1,0:T(8,128)S(1)}, u32[]{:S(2)}, u32[]{:S(2)}) collective-permute-start(f32[4,2,2,32,256]{4,3,2,1,0:T(8,128)S(1)} %dynamic-slice_bitcast_fusion), channel_id=1, source_target_pairs={{0,1},{1,0},{2,3},{3,2},{4,5},{5,4},{6,7},{7,6},{8,9},{9,8},{10,11... | collective-permute-start | bytes 1572872 | tf_op jit(solution)/shard_map/ppermute | solution.py:42
  9.4 6.9 %collective-permute-start.1 = (f32[4,2,32,256]{3,2,1,0:T(8,128)S(1)}, f32[4,2,32,256]{3,2,1,0:T(8,128)S(1)}, u32[]{:S(2)}, u32[]{:S(2)}) collective-permute-start(f32[4,2,32,256]{3,2,1,0:T(8,128)S(1)} %bitcast_select_fusion), channel_id=1, source_target_pairs={{0,2},{1,5},{2,0},{3,7},{4,6},{5,1},{6,4},{7,3},{8,10},{9,13},{10,... | collective-permute-start | bytes 786440 | tf_op jit(solution)/shard_map/ppermute | solution.py:42
  16.4 5.1 %collective-permute-start.2 = (f32[4,32,256]{2,1,0:T(8,128)S(1)}, f32[4,32,256]{2,1,0:T(8,128)S(1)}, u32[]{:S(2)}, u32[]{:S(2)}) collective-permute-start(f32[4,32,256]{2,1,0:T(8,128)S(1)} %dynamic-slice_bitcast_fusion.1), channel_id=1, source_target_pairs={{0,4},{1,3},{2,6},{3,1},{4,0},{5,7},{6,2},{7,5},{8,12},{9,11},{10,... | collective-permute-start | bytes 393224 | tf_op jit(solution)/shard_map/ppermute | solution.py:42
  22.1 11.3 %all-to-all-start = ((f32[4,32,256]{2,1,0:T(8,128)}), f32[4,32,256]{2,1,0:T(8,128)S(1)}, u32[]{:S(2)}, u32[]{:S(2)}) async-start(f32[4,32,256]{2,1,0:T(8,128)} %bitcast_add_fusion.1), calls=%async_computation | async-start | bytes 262144 | tf_op jit(solution)/shard_map/all_to_all | solution.py:45

commit v6 on v4

--- a/solution.py
+++ b/solution.py
@@ -1,3 +1,5 @@
+import functools
+
 import jax
 import jax.numpy as jnp
 from jax import lax
@@ -6,8 +8,10 @@
 from jax.sharding import PartitionSpec as P
 
 
-def halving_scatter(partial, axis, count, index):
+def halving_scatter(partial, axis, count, index, second=None):
     rows, cols = partial.shape
+    if second is not None:
+        rows = 2 * rows
     block = rows // count
     bits = count.bit_length() - 1
     first = (index & 1) == 0
@@ -18,9 +22,16 @@
             seq[1], seq[2] = seq[2], seq[1]
         return seq
 
-    buf = partial.reshape((2,) * bits + (block, cols))
     left = [list(range(bits - 1, -1, -1)) for _ in range(2)]
-    for stage in range(bits):
+    stages = range(bits)
+    if second is not None:
+        got = lax.ppermute(partial, axis, [(i, i ^ 1) for i in range(count)])
+        buf = (second() + got).reshape((2,) * (bits - 1) + (block, cols))
+        left = [seq[:-1] for seq in left]
+        stages = range(1, bits)
+    else:
+        buf = partial.reshape((2,) * bits + (block, cols))
+    for stage in stages:
         split = [order(c)[stage] for c in range(2)]
         where = [left[c].index(split[c]) for c in range(2)]
         mine = [(index >> split[c]) & 1 for c in range(2)]
@@ -43,7 +54,7 @@
     return buf.reshape(block, cols)
 
 
-def _masked_product_kernel(slab_ref, occ_s_ref, occ_v_ref, virt_v_ref, amp_ref, int_ref, out_ref):
+def _irrep_mask(slab_ref, occ_s_ref, occ_v_ref, virt_v_ref, int_ref):
     virt_count = virt_v_ref.shape[0]
     occ_count = occ_v_ref.shape[0]
     kc_local, cols = int_ref.shape
@@ -67,14 +78,53 @@
            == lax.broadcasted_iota(jnp.int32, (virt_count, virt_count), 1)).astype(bf16)
     virt_col = lax.dot_general(eye, virt_rows, (((1,), (1,)), ((), ())), preferred_element_type=f32)
     virt_col = virt_col.astype(jnp.int32)[:, 0:1]
-    total = None
+    parts = []
     for k in range(occ_local):
         kc_irrep = jnp.bitwise_xor(virt_col, occ_s_ref[base + k])
         block = int_ref[k * virt_count:(k + 1) * virt_count, :]
-        masked = jnp.where(kc_irrep == col_irrep, block, jnp.zeros_like(block))
-        term = jnp.dot(amp_ref[:, k * virt_count:(k + 1) * virt_count], masked, preferred_element_type=f32)
+        parts.append(jnp.where(kc_irrep == col_irrep, block, jnp.zeros_like(block)))
+    return parts
+
+
+def _masked_product_kernel(slab_ref, occ_s_ref, occ_v_ref, virt_v_ref, amp_ref, int_ref, out_ref):
+    virt_count = virt_v_ref.shape[0]
+    total = None
+    for k, masked in enumerate(_irrep_mask(slab_ref, occ_s_ref, occ_v_ref, virt_v_ref, int_ref)):
+        term = jnp.dot(amp_ref[:, k * virt_count:(k + 1) * virt_count], masked,
+                       preferred_element_type=jnp.float32)
         total = term if total is None else total + term
     out_ref[...] = total
+
+
+def _half_rows(block, keep, amp_hbm, amp_buf, sems):
+    core = lax.axis_index("contr") % 2
+    parity = core if keep else 1 - core
+    copies = []
+    for m in range(amp_buf.shape[0] // block):
+        src = amp_hbm.at[pl.ds(pl.multiple_of((2 * m + parity) * block, block), block), :]
+        copy = pltpu.make_async_copy(src, amp_buf.at[pl.ds(m * block, block), :], sems.at[m])
+        copy.start()
+        copies.append(copy)
+    return copies
+
+
+def _send_half_kernel(block, slab_ref, occ_s_ref, occ_v_ref, virt_v_ref, amp_hbm, int_ref,
+                      out_ref, masked_ref, amp_buf, sems):
+    copies = _half_rows(block, False, amp_hbm, amp_buf, sems)
+    parts = _irrep_mask(slab_ref, occ_s_ref, occ_v_ref, virt_v_ref, int_ref)
+    virt_count = virt_v_ref.shape[0]
+    for k, masked in enumerate(parts):
+        masked_ref[k * virt_count:(k + 1) * virt_count, :] = masked
+    for copy in copies:
+        copy.wait()
+    out_ref[...] = jnp.dot(amp_buf[...], masked_ref[...], preferred_element_type=jnp.float32)
+
+
+def _keep_half_kernel(block, amp_hbm, masked_ref, out_ref, amp_buf, sems):
+    copies = _half_rows(block, True, amp_hbm, amp_buf, sems)
+    for copy in copies:
+        copy.wait()
+    out_ref[...] = jnp.dot(amp_buf[...], masked_ref[...], preferred_element_type=jnp.float32)
 
 
 def masked_product(slab_start, occ_irrep, virt_irrep, amplitudes, integrals):
@@ -93,6 +143,39 @@
             transcendentals=0,
         ),
     )(slab_start, occ_irrep, occ_irrep, virt_irrep, amplitudes, integrals)
+
+
+def split_product(block, slab_start, occ_irrep, virt_irrep, amplitudes, integrals):
+    rows, kc_local = amplitudes.shape
+    cols = integrals.shape[1]
+    half = rows // 2
+    smem = pl.BlockSpec(memory_space=pltpu.SMEM)
+    vmem = pl.BlockSpec(memory_space=pltpu.VMEM)
+    hbm = pl.BlockSpec(memory_space=pl.ANY)
+    scratch = [pltpu.VMEM((half, kc_local), jnp.bfloat16), pltpu.SemaphoreType.DMA((half // block,))]
+    cost = pl.CostEstimate(
+        flops=2 * half * kc_local * cols,
+        bytes_accessed=2 * half * kc_local + 2 * kc_local * cols + 4 * half * cols,
+        transcendentals=0,
+    )
+    send, masked = pl.pallas_call(
+        functools.partial(_send_half_kernel, block),
+        out_shape=(jax.ShapeDtypeStruct((half, cols), jnp.float32),
+                   jax.ShapeDtypeStruct((kc_local, cols), jnp.bfloat16)),
+        in_specs=[smem, smem, vmem, vmem, hbm, vmem],
+        out_specs=(vmem, vmem),
+        scratch_shapes=scratch,
+        cost_estimate=cost,
+    )(slab_start, occ_irrep, occ_irrep, virt_irrep, amplitudes, integrals)
+    keep_fn = pl.pallas_call(
+        functools.partial(_keep_half_kernel, block),
+        out_shape=jax.ShapeDtypeStruct((half, cols), jnp.float32),
+        in_specs=[hbm, vmem],
+        out_specs=vmem,
+        scratch_shapes=scratch,
+        cost_estimate=cost,
+    )
+    return send, lambda: keep_fn(amplitudes, masked)
 
 
 def body(amplitudes, integrals, occ_irrep, virt_irrep, occ_energy, virt_energy, slab_start):
@@ -119,11 +202,17 @@
     row_energy = (occ_energy[:, None] - a_energy[None, :]).reshape(-1)
     col_energy = (occ_energy[:, None] - b_energy[None, :]).reshape(-1)
     whole_int = lax.all_gather(integrals, "pair", axis=1, tiled=True)
-    partial = masked_product(slab_start, occ_irrep, virt_irrep, amplitudes, whole_int)
-    if contr_count & (contr_count - 1) == 0 and rows_pair % contr_count == 0:
-        summed = halving_scatter(partial, "contr", contr_count, contr_index)
+    power = contr_count & (contr_count - 1) == 0 and rows_pair % contr_count == 0
+    block = rows_pair // contr_count
+    if power and contr_count >= 2 and block % 16 == 0:
+        send, keep = split_product(block, slab_start, occ_irrep, virt_irrep, amplitudes, whole_int)
+        summed = halving_scatter(send, "contr", contr_count, contr_index, keep)
     else:
-        summed = lax.psum_scatter(partial, "contr", scatter_dimension=0, tiled=True)
+        partial = masked_product(slab_start, occ_irrep, virt_irrep, amplitudes, whole_int)
+        if power:
+            summed = halving_scatter(partial, "contr", contr_count, contr_index)
+        else:
+            summed = lax.psum_scatter(partial, "contr", scatter_dimension=0, tiled=True)
     mine_irrep = lax.dynamic_slice(
         row_irrep, (pair_index * rows_pair + contr_index * rows_device,), (rows_device,)
     )

time: 30.6 us -> 32 us (1.046)
  Pallas kernels: 3.92 us -> 7.5 us
  waiting for transfers between devices: 8.82 us -> 6.57 us
  local copies, waits for them, and re-layouts: 2.86 us -> 1.56 us
  other arithmetic: 1.17 us -> 2.21 us
  starting transfers between devices: 9.59 us -> 9.96 us
    pallas_call x1 -> x2, Pallas kernels: 3.92 us -> 7.5 us  [the longest x1 3.82 us: split_product(): pl.pallas_call(functools.partial(_send_half_kernel, block), out_shape=(ja...]
    ppermute x5 -> x4, waiting for transfers between devices: 8.82 us -> 6.57 us  [halving_scatter(): buf = keep + lax.ppermute(send, axis, perm)]
    dynamic_slice x2 -> x0, local copies, waits for them, and re-layouts: 1.33 us -> none  [the longest x1 1.29 us: halving_scatter(): keep = lax.dynamic_index_in_dim(buf, bit, axis=where[0], keepdims=False)]
    add x0 -> x1, other arithmetic: none -> 1.12 us  [halving_scatter(): buf = (second() + got).reshape((2,) * (bits - 1) + (block, cols))]
    ppermute x0 -> x1, starting transfers between devices: none -> 0.51 us  [halving_scatter(): got = lax.ppermute(partial, axis, [(i, i ^ 1) for i in range(count)])]
    ppermute x5 -> x4, starting transfers between devices: 9.59 us -> 9.45 us  [halving_scatter(): buf = keep + lax.ppermute(send, axis, perm)]
  transfers between devices with their start and end apart: 5 -> 5, of which waited for: 4 -> 3; matrix products, arithmetic and copies ran while one was open for 6% -> 5% of each run, Pallas kernels for 0% -> 12%
where the time goes in v6:
time: 32 us; the launch traced here: 31.6 us
  starting transfers between devices  9.96 us (31%)
  Pallas kernels  7.5 us (23%)
  waiting for transfers between devices  6.57 us (21%)
  between operations  3.79 us (12%)
  other arithmetic  2.21 us (7%)
  local copies, waits for them, and re-layouts  1.56 us (5%)
    ppermute x4, starting transfers between devices, halving_scatter(): buf = keep + lax.ppermute(send, axis, perm)  9.45 us
    ppermute x4, waiting for transfers between devices, halving_scatter(): buf = keep + lax.ppermute(send, axis, perm)  6.57 us
    pallas_call x1, Pallas kernels, split_product(): pl.pallas_call(functools.partial(_send_half_kernel, block), out_shape=(ja...  3.82 us
    pallas_call x1, Pallas kernels, split_product(): return (send, lambda: keep_fn(amplitudes, masked))  3.68 us
    add x1, other arithmetic, halving_scatter(): buf = (second() + got).reshape((2,) * (bits - 1) + (block, cols))  1.12 us
    convert_element_type x1, other arithmetic, body(): (summed / (mine_energy[:, None] + col_energy[None, :])).astype(jnp.bfloat16)  0.69 us
  transfers between devices with their start and end apart: 5, of which 3 were waited for; matrix products, arithmetic and copies ran while one was open for 5% of the time, Pallas kernels for 12%

profile of v6, /device:TPU:0, one launch (start us, length us, event | category | flops | bytes accessed | tf_op | source)
XLA Modules:
  0.0 31.6 jit_solution(2966054884925924026)
XLA Ops:
  0.0 3.8 %shard_map.73 = (f32[512,256]{1,0:T(8,128)}, bf16[1024,256]{1,0:T(8,128)(2,1)}) custom-call(s32[2]{0:T(128)} %slab_ref.1, s32[64]{0:T(128)} %occ_v_ref.1, s32[64]{0:T(128)} %occ_v_ref.1, s32[512]{0:T(512)} %virt_v_ref.1, bf16[1024,1024]{1,0:T(8,128)(2,1)} %amp_hbm.3, bf16[1024,256]{1,0:T(8,128)(2,1)} %int_ref), custom_call_target="tpu_custom_call" | custom-call | flops 268435456 | bytes 2097152 | tf_op jit(solution)/shard_map/pallas_call | solution.py:161
  3.8 0.5 %collective-permute-start = (f32[512,256]{1,0:T(8,128)}, f32[512,256]{1,0:T(8,128)S(1)}, u32[]{:S(2)}, u32[]{:S(2)}) collective-permute-start(f32[512,256]{1,0:T(8,128)} %get-tuple-element.8), channel_id=1, source_target_pairs={{0,1},{1,0},{2,3},{3,2},{4,5},{5,4},{6,7},{7,6},{8,9},{9,8},{10,11... | collective-permute-start | bytes 1572872 | tf_op jit(solution)/shard_map/ppermute | solution.py:28
  4.3 3.7 %shard_map.74 = f32[512,256]{1,0:T(8,128)} custom-call(bf16[1024,1024]{1,0:T(8,128)(2,1)} %amp_hbm.3, bf16[1024,256]{1,0:T(8,128)(2,1)} %get-tuple-element.7.masked_ref), custom_call_target="tpu_custom_call" | custom-call | flops 268435456 | bytes 2097152 | tf_op jit(solution)/shard_map/pallas_call | solution.py:178
  8.0 0.0 copy-start.1
  8.0 0.0 copy-start.2
  8.0 0.0 copy-start.4
  8.1 0.0 copy-start.3
  8.1 0.0 collective-permute-done
  8.1 1.1 %add.85 = f32[512,256]{1,0:T(8,128)S(1)} add(f32[512,256]{1,0:T(8,128)} %shard_map.74, f32[512,256]{1,0:T(8,128)S(1)} %collective-permute-done) | non-fusion elementwise | flops 131072 | bytes 1572864 | tf_op jit(solution)/shard_map/add | solution.py:29
  9.3 0.0 copy-start
  9.4 2.6 %collective-permute-start.1 = (f32[2,2,2,32,256]{4,3,1,0,2:T(8,128)S(1)}, f32[2,2,2,32,256]{4,3,1,0,2:T(8,128)S(1)}, u32[]{:S(2)}, u32[]{:S(2)}) collective-permute-start(f32[2,2,2,32,256]{4,3,1,0,2:T(8,128)S(1)} %bitcast_select_fusion), channel_id=1, source_target_pairs={{0,2},{1,5},{2,0},{3,7},{4,6},{5,1},{6,4},{7,3},{8,10},{9,13},{10,... | collective-permute-start | bytes 786440 | tf_op jit(solution)/shard_map/ppermute | solution.py:53
  11.9 0.0 copy-done.1
  11.9 0.6 %fusion.4 = (s32[1]{0:T(128)}, s32[1]{0:T(128)}) fusion(s32[2]{0:T(128)S(1)} %copy-done.1), kind=kLoop, calls=%fused_computation.20 | loop fusion | bytes 16 | tf_op jit(solution)/shard_map/slice | solution.py:194
  15.5 0.0 copy-done.2
  15.5 0.1 dynamic_slice.55
  15.6 0.0 copy-done.4
  15.6 0.1 dynamic_slice.68
  16.3 0.1 dynamic_slice.66
  16.4 0.0 copy-done.3
  16.4 0.1 broadcast_subtract_fusion
  16.5 0.0 collective-permute-done.1
  16.5 0.1 fusion
  16.6 1.9 %collective-permute-start.2 = (f32[2,2,32,256]{3,2,1,0:T(8,128)S(1)}, f32[2,2,32,256]{3,2,1,0:T(8,128)S(1)}, u32[]{:S(2)}, u32[]{:S(2)}) collective-permute-start(f32[2,2,32,256]{3,2,1,0:T(8,128)S(1)} %dynamic-slice_bitcast_fusion), channel_id=1, source_target_pairs={{0,4},{1,3},{2,6},{3,1},{4,0},{5,7},{6,2},{7,5},{8,12},{9,11},{10,... | collective-permute-start | bytes 393224 | tf_op jit(solution)/shard_map/ppermute | solution.py:53
  18.5 0.1 broadcast_subtract_fusion.1
  18.6 3.0 %collective-permute-done.2 = f32[2,2,32,256]{3,2,1,0:T(8,128)S(1)} collective-permute-done((f32[2,2,32,256]{3,2,1,0:T(8,128)S(1)}, f32[2,2,32,256]{3,2,1,0:T(8,128)S(1)}, u32[]{:S(2)}, u32[]{:S(2)}) %collective-permute-start.2) | collective-permute-done | bytes 131104 | tf_op jit(solution)/shard_map/ppermute | solution.py:53
  21.7 2.0 %collective-permute-start.3 = (f32[2,32,256]{2,1,0:T(8,128)S(1)}, f32[2,32,256]{2,1,0:T(8,128)S(1)}, u32[]{:S(2)}, u32[]{:S(2)}) collective-permute-start(f32[2,32,256]{2,1,0:T(8,128)S(1)} %dynamic-slice_bitcast_fusion.1), channel_id=1, source_target_pairs={{0,8},{1,9},{2,10},{3,11},{4,12},{5,13},{6,14},{7,15},{8,0},{9,1},... | collective-permute-start | bytes 196616 | tf_op jit(solution)/shard_map/ppermute | solution.py:53
  23.6 0.0 copy-done
  23.6 0.1 broadcast_xor_fusion
  23.7 0.1 dynamic_slice.53
  23.8 2.2 %collective-permute-done.3 = f32[2,32,256]{2,1,0:T(8,128)S(1)} collective-permute-done((f32[2,32,256]{2,1,0:T(8,128)S(1)}, f32[2,32,256]{2,1,0:T(8,128)S(1)}, u32[]{:S(2)}, u32[]{:S(2)}) %collective-permute-start.3) | collective-permute-done | bytes 65568 | tf_op jit(solution)/shard_map/ppermute | solution.py:53
  26.0 3.0 %collective-permute-start.4 = (f32[32,256]{1,0:T(8,128)S(1)}, f32[32,256]{1,0:T(8,128)S(1)}, u32[]{:S(2)}, u32[]{:S(2)}) collective-permute-start(f32[32,256]{1,0:T(8,128)S(1)} %dynamic-slice_bitcast_fusion.2), channel_id=1, source_target_pairs={{0,16},{1,17},{2,18},{3,19},{4,20},{5,21},{6,22},{7,23},{8,24},{9,... | collective-permute-start | bytes 98312 | tf_op jit(solution)/shard_map/ppermute | solution.py:53
  29.0 0.1 broadcast_xor_fusion.1
  29.1 0.1 sub.64
  29.2 0.1 sub.60
  29.3 0.1 xor.44
  29.4 0.1 xor.40
  29.4 0.1 dynamic_slice.67
  29.5 0.1 dynamic_slice.54
  29.6 1.3 %collective-permute-done.4 = f32[32,256]{1,0:T(8,128)S(1)} collective-permute-done((f32[32,256]{1,0:T(8,128)S(1)}, f32[32,256]{1,0:T(8,128)S(1)}, u32[]{:S(2)}, u32[]{:S(2)}) %collective-permute-start.4) | collective-permute-done | bytes 32800 | tf_op jit(solution)/shard_map/ppermute | solution.py:53
  30.9 0.7 %fusion.3 = bf16[32,256]{1,0:T(8,128)(2,1)} fusion(f32[32,256]{1,0:T(8,128)S(1)} %collective-permute-done.4, f32[2,32,256]{2,1,0:T(8,128)S(1)} %bitcast_add_fusion.1, s32[]{:T(128)S(6)} %select_n.82, f32[256]{0:T(256)S(1)} %sub.64, f32[32]{0:T(128)S(1)} %dynamic_slice.67, s32[256]{0:T(256)S(1)} %xor.44, s32[32]{0:T(128)S(1)} %dynamic_slice.54), kind=kLoop, calls=%fused_computation.10 | loop fusion | flops 49152 | bytes 84228 | tf_op jit(solution)/shard_map/convert_element_type | solution.py:223
  (8 shorter events, 0.2 us)
Async XLA Ops:
  3.8 4.2 %collective-permute-start = (f32[512,256]{1,0:T(8,128)}, f32[512,256]{1,0:T(8,128)S(1)}, u32[]{:S(2)}, u32[]{:S(2)}) collective-permute-start(f32[512,256]{1,0:T(8,128)} %get-tuple-element.8), channel_id=1, source_target_pairs={{0,1},{1,0},{2,3},{3,2},{4,5},{5,4},{6,7},{7,6},{8,9},{9,8},{10,11... | collective-permute-start | bytes 1572872 | tf_op jit(solution)/shard_map/ppermute | solution.py:28
  8.0 3.9 %copy-start.1 = (s32[2]{0:T(128)S(1)}, s32[2]{0:T(128)}, u32[]{:S(2)}) copy-start(s32[2]{0:T(128)} %slab_ref.1) | copy-start | bytes 28
  8.0 7.5 %copy-start.2 = (s32[512]{0:T(512)S(1)}, s32[512]{0:T(512)}, u32[]{:S(2)}) copy-start(s32[512]{0:T(512)} %virt_v_ref.1) | copy-start | bytes 6148
  8.0 7.6 %copy-start.4 = (f32[512]{0:T(512)S(1)}, f32[512]{0:T(512)}, u32[]{:S(2)}) copy-start(f32[512]{0:T(512)} %param.12) | copy-start | bytes 6148
  8.1 8.4 %copy-start.3 = (f32[64]{0:T(128)S(1)}, f32[64]{0:T(128)}, u32[]{:S(2)}) copy-start(f32[64]{0:T(128)} %param.11) | copy-start | bytes 772
  9.3 14.4 %copy-start = (s32[64]{0:T(128)S(1)}, s32[64]{0:T(128)}, u32[]{:S(2)}) copy-start(s32[64]{0:T(128)} %occ_v_ref.1) | copy-start | bytes 772
  9.4 7.1 %collective-permute-start.1 = (f32[2,2,2,32,256]{4,3,1,0,2:T(8,128)S(1)}, f32[2,2,2,32,256]{4,3,1,0,2:T(8,128)S(1)}, u32[]{:S(2)}, u32[]{:S(2)}) collective-permute-start(f32[2,2,2,32,256]{4,3,1,0,2:T(8,128)S(1)} %bitcast_select_fusion), channel_id=1, source_target_pairs={{0,2},{1,5},{2,0},{3,7},{4,6},{5,1},{6,4},{7,3},{8,10},{9,13},{10,... | collective-permute-start | bytes 786440 | tf_op jit(solution)/shard_map/ppermute | solution.py:53
  16.6 5.0 %collective-permute-start.2 = (f32[2,2,32,256]{3,2,1,0:T(8,128)S(1)}, f32[2,2,32,256]{3,2,1,0:T(8,128)S(1)}, u32[]{:S(2)}, u32[]{:S(2)}) collective-permute-start(f32[2,2,32,256]{3,2,1,0:T(8,128)S(1)} %dynamic-slice_bitcast_fusion), channel_id=1, source_target_pairs={{0,4},{1,3},{2,6},{3,1},{4,0},{5,7},{6,2},{7,5},{8,12},{9,11},{10,... | collective-permute-start | bytes 393224 | tf_op jit(solution)/shard_map/ppermute | solution.py:53
  21.7 4.3 %collective-permute-start.3 = (f32[2,32,256]{2,1,0:T(8,128)S(1)}, f32[2,32,256]{2,1,0:T(8,128)S(1)}, u32[]{:S(2)}, u32[]{:S(2)}) collective-permute-start(f32[2,32,256]{2,1,0:T(8,128)S(1)} %dynamic-slice_bitcast_fusion.1), channel_id=1, source_target_pairs={{0,8},{1,9},{2,10},{3,11},{4,12},{5,13},{6,14},{7,15},{8,0},{9,1},... | collective-permute-start | bytes 196616 | tf_op jit(solution)/shard_map/ppermute | solution.py:53
  26.0 4.9 %collective-permute-start.4 = (f32[32,256]{1,0:T(8,128)S(1)}, f32[32,256]{1,0:T(8,128)S(1)}, u32[]{:S(2)}, u32[]{:S(2)}) collective-permute-start(f32[32,256]{1,0:T(8,128)S(1)} %dynamic-slice_bitcast_fusion.2), channel_id=1, source_target_pairs={{0,16},{1,17},{2,18},{3,19},{4,20},{5,21},{6,22},{7,23},{8,24},{9,... | collective-permute-start | bytes 98312 | tf_op jit(solution)/shard_map/ppermute | solution.py:53

commit v7 on v4

--- a/solution.py
+++ b/solution.py
@@ -87,6 +87,7 @@
         out_shape=jax.ShapeDtypeStruct((rows, cols), jnp.float32),
         in_specs=[smem, smem, vmem, vmem, vmem, vmem],
         out_specs=vmem,
+        compiler_params=pltpu.CompilerParams(vmem_limit_bytes=16 * 1024 * 1024),
         cost_estimate=pl.CostEstimate(
             flops=2 * rows * kc_local * cols,
             bytes_accessed=2 * rows * kc_local + 2 * kc_local * cols + 4 * rows * cols,

time: 30.6 us -> 32 us (1.046)
  local copies, waits for them, and re-layouts: 2.86 us -> 6.24 us
  Pallas kernels: 3.92 us -> 1.78 us
  starting transfers between devices: 9.59 us -> 10.9 us
  waiting for transfers between devices: 8.82 us -> 7.93 us
    unnamed x10 -> x20, local copies, waits for them, and re-layouts: 0.03 us -> 4.65 us
    pallas_call x1, Pallas kernels: 3.92 us -> 1.78 us  [masked_product(): pl.pallas_call(_masked_product_kernel, out_shape=jax.ShapeDtypeStruct((ro...]
    ppermute x5, starting transfers between devices: 9.59 us -> 10.9 us  [halving_scatter(): buf = keep + lax.ppermute(send, axis, perm)]
    dynamic_slice x1, local copies, waits for them, and re-layouts: 1.29 us -> 0.08 us  [halving_scatter(): keep = lax.dynamic_index_in_dim(buf, bit, axis=where[0], keepdims=False)]
    ppermute x5, waiting for transfers between devices: 8.82 us -> 7.93 us  [halving_scatter(): buf = keep + lax.ppermute(send, axis, perm)]
  transfers between devices with their start and end apart: 5 -> 5, of which waited for: 4 -> 4; matrix products, arithmetic and copies ran while one was open for 6% -> 5% of each run, Pallas kernels for 0% -> 0%
where the time goes in v7:
time: 32 us; the launch traced here: 31.7 us
  starting transfers between devices  10.9 us (34%)
  waiting for transfers between devices  7.93 us (25%)
  local copies, waits for them, and re-layouts  6.24 us (20%)
  between operations  3.73 us (12%)
  Pallas kernels  1.78 us (6%)
  other arithmetic  1.18 us (4%)
    ppermute x5, starting transfers between devices, halving_scatter(): buf = keep + lax.ppermute(send, axis, perm)  10.9 us
    ppermute x5, waiting for transfers between devices, halving_scatter(): buf = keep + lax.ppermute(send, axis, perm)  7.93 us
    unnamed x20, local copies, waits for them, and re-layouts  4.65 us
    pallas_call x1, Pallas kernels, masked_product(): pl.pallas_call(_masked_product_kernel, out_shape=jax.ShapeDtypeStruct((ro...  1.78 us
    convert_element_type x1, other arithmetic, body(): (summed / (mine_energy[:, None] + col_energy[None, :])).astype(jnp.bfloat16)  0.69 us
  transfers between devices with their start and end apart: 5, of which 4 were waited for; matrix products, arithmetic and copies ran while one was open for 5% of the time, Pallas kernels for 0%

profile of v7, /device:TPU:0, one launch (start us, length us, event | category | flops | bytes accessed | tf_op | source)
XLA Modules:
  0.0 31.7 jit_solution(16859644702364468678)
XLA Ops:
  0.0 0.0 copy-start
  0.0 1.6 %copy-done = bf16[1024,1024]{1,0:T(8,128)(2,1)S(1)} copy-done((bf16[1024,1024]{1,0:T(8,128)(2,1)S(1)}, bf16[1024,1024]{1,0:T(8,128)(2,1)}, u32[]{:S(2)}) %copy-start) | copy-done | bytes 2097176
  1.6 0.0 copy-start.1
  1.6 1.0 %copy-done.1 = bf16[1024,256]{1,0:T(8,128)(2,1)S(1)} copy-done((bf16[1024,256]{1,0:T(8,128)(2,1)S(1)}, bf16[1024,256]{1,0:T(8,128)(2,1)}, u32[]{:S(2)}) %copy-start.1) | copy-done | bytes 524312
  2.6 0.7 %copy-done.2 = s32[64]{0:T(128)S(1)} copy-done((s32[64]{0:T(128)S(1)}, s32[64]{0:T(128)}, u32[]{:S(2)}) %copy-start.2) | copy-done | bytes 280
  3.3 0.7 %copy-done.4 = s32[2]{0:T(128)S(1)} copy-done((s32[2]{0:T(128)S(1)}, s32[2]{0:T(128)}, u32[]{:S(2)}) %copy-start.4) | copy-done | bytes 32
  3.9 0.7 %copy-done.6 = s32[512]{0:T(512)S(1)} copy-done((s32[512]{0:T(512)S(1)}, s32[512]{0:T(512)}, u32[]{:S(2)}) %copy-start.6) | copy-done | bytes 2072
  4.6 1.8 %shard_map.73 = f32[1024,256]{1,0:T(8,128)S(1)} custom-call(s32[2]{0:T(128)S(1)} %copy-done.4, s32[64]{0:T(128)S(1)} %copy-done.2, s32[64]{0:T(128)S(1)} %copy-done.2, s32[512]{0:T(512)S(1)} %copy-done.6, bf16[1024,1024]{1,0:T(8,128)(2,1)S(1)} %copy-done, bf16[1024,256]{1,0:T(8,128)(2,1)S(1)} %copy-done.1), custom_call_target="tpu_custom_call" | custom-call | flops 536870912 | bytes 3670016 | tf_op jit(solution)/shard_map/pallas_call | solution.py:85
  6.4 0.1 constant_dynamic-slice_fusion.3
  6.5 0.0 copy-start.5
  6.5 0.0 copy-start.7
  6.5 0.0 copy-start.9
  6.5 0.0 copy-start.3
  6.6 0.5 %collective-permute-start = (f32[2,2,2,2,32,256]{5,4,2,1,0,3:T(8,128)S(1)}, f32[2,2,2,2,32,256]{5,4,2,1,0,3:T(8,128)S(1)}, u32[]{:S(2)}, u32[]{:S(2)}) collective-permute-start(f32[2,2,2,2,32,256]{5,4,2,1,0,3:T(8,128)S(1)} %bitcast.37), channel_id=1, source_target_pairs={{0,1},{1,0},{2,3},{3,2},{4,5},{5,4},{6,7},{7,6},{8,9},{9,8},{10,11... | collective-permute-start | bytes 1572872 | tf_op jit(solution)/shard_map/ppermute | solution.py:42
  7.1 1.5 %collective-permute-done = f32[2,2,2,2,32,256]{5,4,2,1,0,3:T(8,128)S(1)} collective-permute-done((f32[2,2,2,2,32,256]{5,4,2,1,0,3:T(8,128)S(1)}, f32[2,2,2,2,32,256]{5,4,2,1,0,3:T(8,128)S(1)}, u32[]{:S(2)}, u32[]{:S(2)}) %collective-permute-start) | collective-permute-done | bytes 524320 | tf_op jit(solution)/shard_map/ppermute | solution.py:42
  8.7 0.1 bitcast_add_fusion
  8.7 0.1 constant_dynamic-slice_fusion.1
  8.8 0.1 bitcast_select_fusion
  8.9 2.9 %collective-permute-start.1 = (f32[2,2,2,32,256]{4,3,2,1,0:T(8,128)S(1)}, f32[2,2,2,32,256]{4,3,2,1,0:T(8,128)S(1)}, u32[]{:S(2)}, u32[]{:S(2)}) collective-permute-start(f32[2,2,2,32,256]{4,3,2,1,0:T(8,128)S(1)} %bitcast_select_fusion), channel_id=1, source_target_pairs={{0,2},{1,5},{2,0},{3,7},{4,6},{5,1},{6,4},{7,3},{8,10},{9,13},{10,... | collective-permute-start | bytes 786440 | tf_op jit(solution)/shard_map/ppermute | solution.py:42
  11.8 0.0 copy-done.5
  11.8 0.6 %fusion.4 = (s32[1]{0:T(128)}, s32[1]{0:T(128)}) fusion(s32[2]{0:T(128)S(1)} %copy-done.5), kind=kLoop, calls=%fused_computation.22 | loop fusion | bytes 16 | tf_op jit(solution)/shard_map/slice | solution.py:112
  15.4 0.0 copy-done.7
  15.4 0.1 dynamic_slice.60
  15.5 0.0 copy-done.9
  15.5 0.1 dynamic_slice.75
  16.1 0.1 dynamic_slice.77
  16.2 0.0 copy-done.3
  16.2 0.1 broadcast_xor_fusion.1
  16.2 0.0 collective-permute-done.1
  16.2 0.1 fusion
  16.3 2.0 %collective-permute-start.2 = (f32[2,2,32,256]{3,2,1,0:T(8,128)S(1)}, f32[2,2,32,256]{3,2,1,0:T(8,128)S(1)}, u32[]{:S(2)}, u32[]{:S(2)}) collective-permute-start(f32[2,2,32,256]{3,2,1,0:T(8,128)S(1)} %dynamic-slice_bitcast_fusion), channel_id=1, source_target_pairs={{0,4},{1,3},{2,6},{3,1},{4,0},{5,7},{6,2},{7,5},{8,12},{9,11},{10,... | collective-permute-start | bytes 393224 | tf_op jit(solution)/shard_map/ppermute | solution.py:42
  18.3 0.0 copy-done.8
  18.3 0.1 broadcast_subtract_fusion.1
  18.4 3.0 %collective-permute-done.2 = f32[2,2,32,256]{3,2,1,0:T(8,128)S(1)} collective-permute-done((f32[2,2,32,256]{3,2,1,0:T(8,128)S(1)}, f32[2,2,32,256]{3,2,1,0:T(8,128)S(1)}, u32[]{:S(2)}, u32[]{:S(2)}) %collective-permute-start.2) | collective-permute-done | bytes 131104 | tf_op jit(solution)/shard_map/ppermute | solution.py:42
  21.4 2.1 %collective-permute-start.3 = (f32[2,32,256]{2,1,0:T(8,128)S(1)}, f32[2,32,256]{2,1,0:T(8,128)S(1)}, u32[]{:S(2)}, u32[]{:S(2)}) collective-permute-start(f32[2,32,256]{2,1,0:T(8,128)S(1)} %dynamic-slice_bitcast_fusion.1), channel_id=1, source_target_pairs={{0,8},{1,9},{2,10},{3,11},{4,12},{5,13},{6,14},{7,15},{8,0},{9,1},... | collective-permute-start | bytes 196616 | tf_op jit(solution)/shard_map/ppermute | solution.py:42
  23.5 0.1 broadcast_subtract_fusion
  23.5 0.1 dynamic_slice.62
  23.6 2.1 %collective-permute-done.3 = f32[2,32,256]{2,1,0:T(8,128)S(1)} collective-permute-done((f32[2,32,256]{2,1,0:T(8,128)S(1)}, f32[2,32,256]{2,1,0:T(8,128)S(1)}, u32[]{:S(2)}, u32[]{:S(2)}) %collective-permute-start.3) | collective-permute-done | bytes 65568 | tf_op jit(solution)/shard_map/ppermute | solution.py:42
  25.8 3.4 %collective-permute-start.4 = (f32[32,256]{1,0:T(8,128)S(1)}, f32[32,256]{1,0:T(8,128)S(1)}, u32[]{:S(2)}, u32[]{:S(2)}) collective-permute-start(f32[32,256]{1,0:T(8,128)S(1)} %dynamic-slice_bitcast_fusion.2), channel_id=1, source_target_pairs={{0,16},{1,17},{2,18},{3,19},{4,20},{5,21},{6,22},{7,23},{8,24},{9,... | collective-permute-start | bytes 98312 | tf_op jit(solution)/shard_map/ppermute | solution.py:42
  29.2 0.1 broadcast_xor_fusion
  29.2 0.1 xor.40
  29.3 0.1 sub.64
  29.4 0.1 dynamic_slice.61
  29.5 0.1 dynamic_slice.76
  29.5 0.1 sub.68
  29.6 0.1 xor.44
  29.8 1.3 %collective-permute-done.4 = f32[32,256]{1,0:T(8,128)S(1)} collective-permute-done((f32[32,256]{1,0:T(8,128)S(1)}, f32[32,256]{1,0:T(8,128)S(1)}, u32[]{:S(2)}, u32[]{:S(2)}) %collective-permute-start.4) | collective-permute-done | bytes 32800 | tf_op jit(solution)/shard_map/ppermute | solution.py:42
  31.1 0.7 %fusion.3 = bf16[32,256]{1,0:T(8,128)(2,1)} fusion(f32[32,256]{1,0:T(8,128)S(1)} %collective-permute-done.4, f32[2,32,256]{2,1,0:T(8,128)S(1)} %bitcast_add_fusion.2, s32[]{:T(128)S(6)} %select_n.91, f32[256]{0:T(256)S(1)} %sub.68, f32[32]{0:T(128)S(1)} %dynamic_slice.76, s32[256]{0:T(256)S(1)} %xor.44, s32[32]{0:T(128)S(1)} %dynamic_slice.61), kind=kLoop, calls=%fused_computation.12 | loop fusion | flops 49152 | bytes 84228 | tf_op jit(solution)/shard_map/convert_element_type | solution.py:135
  (10 shorter events, 0.1 us)
Async XLA Ops:
  0.0 1.6 %copy-start = (bf16[1024,1024]{1,0:T(8,128)(2,1)S(1)}, bf16[1024,1024]{1,0:T(8,128)(2,1)}, u32[]{:S(2)}) copy-start(bf16[1024,1024]{1,0:T(8,128)(2,1)} %amp_ref.1) | copy-start | bytes 6291460
  1.6 1.0 %copy-start.1 = (bf16[1024,256]{1,0:T(8,128)(2,1)S(1)}, bf16[1024,256]{1,0:T(8,128)(2,1)}, u32[]{:S(2)}) copy-start(bf16[1024,256]{1,0:T(8,128)(2,1)} %int_ref) | copy-start | bytes 1572868
  2.6 0.7 %copy-start.2 = (s32[64]{0:T(128)S(1)}, s32[64]{0:T(128)}, u32[]{:S(2)}) copy-start(s32[64]{0:T(128)} %occ_v_ref.1) | copy-start | bytes 772
  3.3 0.7 %copy-start.4 = (s32[2]{0:T(128)S(1)}, s32[2]{0:T(128)}, u32[]{:S(2)}) copy-start(s32[2]{0:T(128)} %slab_ref.1) | copy-start | bytes 28
  3.9 0.7 %copy-start.6 = (s32[512]{0:T(512)S(1)}, s32[512]{0:T(512)}, u32[]{:S(2)}) copy-start(s32[512]{0:T(512)} %virt_v_ref.1) | copy-start | bytes 6148
  6.5 5.3 %copy-start.5 = (s32[2]{0:T(128)S(1)}, s32[2]{0:T(128)}, u32[]{:S(2)}) copy-start(s32[2]{0:T(128)} %slab_ref.1) | copy-start | bytes 28
  6.5 8.9 %copy-start.7 = (s32[512]{0:T(512)S(1)}, s32[512]{0:T(512)}, u32[]{:S(2)}) copy-start(s32[512]{0:T(512)} %virt_v_ref.1) | copy-start | bytes 6148
  6.5 8.9 %copy-start.9 = (f32[512]{0:T(512)S(1)}, f32[512]{0:T(512)}, u32[]{:S(2)}) copy-start(f32[512]{0:T(512)} %param.12) | copy-start | bytes 6148
  6.5 9.6 %copy-start.3 = (s32[64]{0:T(128)S(1)}, s32[64]{0:T(128)}, u32[]{:S(2)}) copy-start(s32[64]{0:T(128)} %occ_v_ref.1) | copy-start | bytes 772
  6.6 2.1 %collective-permute-start = (f32[2,2,2,2,32,256]{5,4,2,1,0,3:T(8,128)S(1)}, f32[2,2,2,2,32,256]{5,4,2,1,0,3:T(8,128)S(1)}, u32[]{:S(2)}, u32[]{:S(2)}) collective-permute-start(f32[2,2,2,2,32,256]{5,4,2,1,0,3:T(8,128)S(1)} %bitcast.37), channel_id=1, source_target_pairs={{0,1},{1,0},{2,3},{3,2},{4,5},{5,4},{6,7},{7,6},{8,9},{9,8},{10,11... | collective-permute-start | bytes 1572872 | tf_op jit(solution)/shard_map/ppermute | solution.py:42
  8.7 9.7 %copy-start.8 = (f32[64]{0:T(128)S(1)}, f32[64]{0:T(128)}, u32[]{:S(2)}) copy-start(f32[64]{0:T(128)} %param.11) | copy-start | bytes 772
  8.9 7.4 %collective-permute-start.1 = (f32[2,2,2,32,256]{4,3,2,1,0:T(8,128)S(1)}, f32[2,2,2,32,256]{4,3,2,1,0:T(8,128)S(1)}, u32[]{:S(2)}, u32[]{:S(2)}) collective-permute-start(f32[2,2,2,32,256]{4,3,2,1,0:T(8,128)S(1)} %bitcast_select_fusion), channel_id=1, source_target_pairs={{0,2},{1,5},{2,0},{3,7},{4,6},{5,1},{6,4},{7,3},{8,10},{9,13},{10,... | collective-permute-start | bytes 786440 | tf_op jit(solution)/shard_map/ppermute | solution.py:42
  16.3 5.0 %collective-permute-start.2 = (f32[2,2,32,256]{3,2,1,0:T(8,128)S(1)}, f32[2,2,32,256]{3,2,1,0:T(8,128)S(1)}, u32[]{:S(2)}, u32[]{:S(2)}) collective-permute-start(f32[2,2,32,256]{3,2,1,0:T(8,128)S(1)} %dynamic-slice_bitcast_fusion), channel_id=1, source_target_pairs={{0,4},{1,3},{2,6},{3,1},{4,0},{5,7},{6,2},{7,5},{8,12},{9,11},{10,... | collective-permute-start | bytes 393224 | tf_op jit(solution)/shard_map/ppermute | solution.py:42
  21.4 4.3 %collective-permute-start.3 = (f32[2,32,256]{2,1,0:T(8,128)S(1)}, f32[2,32,256]{2,1,0:T(8,128)S(1)}, u32[]{:S(2)}, u32[]{:S(2)}) collective-permute-start(f32[2,32,256]{2,1,0:T(8,128)S(1)} %dynamic-slice_bitcast_fusion.1), channel_id=1, source_target_pairs={{0,8},{1,9},{2,10},{3,11},{4,12},{5,13},{6,14},{7,15},{8,0},{9,1},... | collective-permute-start | bytes 196616 | tf_op jit(solution)/shard_map/ppermute | solution.py:42
  25.8 5.3 %collective-permute-start.4 = (f32[32,256]{1,0:T(8,128)S(1)}, f32[32,256]{1,0:T(8,128)S(1)}, u32[]{:S(2)}, u32[]{:S(2)}) collective-permute-start(f32[32,256]{1,0:T(8,128)S(1)} %dynamic-slice_bitcast_fusion.2), channel_id=1, source_target_pairs={{0,16},{1,17},{2,18},{3,19},{4,20},{5,21},{6,22},{7,23},{8,24},{9,... | collective-permute-start | bytes 98312 | tf_op jit(solution)/shard_map/ppermute | solution.py:42

commit v8 on v4

--- a/solution.py
+++ b/solution.py
@@ -43,10 +43,31 @@
     return buf.reshape(block, cols)
 
 
-def _masked_product_kernel(slab_ref, occ_s_ref, occ_v_ref, virt_v_ref, amp_ref, int_ref, out_ref):
+def _masked_product_kernel(slab_hbm, occ_hbm, virt_hbm, amp_hbm, int_hbm, out_hbm,
+                           slab_ref, occ_s_ref, occ_v_ref, virt_v_ref, amp_v, int_v, out_v, sems, out_sems):
+    rows = amp_v.shape[0]
+    chunks = amp_v.shape[0] // 256 if amp_v.shape[0] % 256 == 0 else 1
+    step = rows // chunks
+    small = [
+        pltpu.make_async_copy(slab_hbm, slab_ref, sems.at[0]),
+        pltpu.make_async_copy(occ_hbm, occ_s_ref, sems.at[1]),
+        pltpu.make_async_copy(occ_hbm, occ_v_ref, sems.at[2]),
+        pltpu.make_async_copy(virt_hbm, virt_v_ref, sems.at[3]),
+        pltpu.make_async_copy(int_hbm, int_v, sems.at[4]),
+    ]
+    for copy in small:
+        copy.start()
+    parts = []
+    for m in range(chunks):
+        copy = pltpu.make_async_copy(amp_hbm.at[pl.ds(m * step, step), :], amp_v.at[pl.ds(m * step, step), :],
+                                     sems.at[5 + m])
+        copy.start()
+        parts.append(copy)
+    for copy in small[:4]:
+        copy.wait()
     virt_count = virt_v_ref.shape[0]
     occ_count = occ_v_ref.shape[0]
-    kc_local, cols = int_ref.shape
+    kc_local, cols = int_v.shape
     occ_local = kc_local // virt_count
     per_occ = cols // occ_count
     second_start = slab_ref[1]
@@ -67,32 +88,57 @@
            == lax.broadcasted_iota(jnp.int32, (virt_count, virt_count), 1)).astype(bf16)
     virt_col = lax.dot_general(eye, virt_rows, (((1,), (1,)), ((), ())), preferred_element_type=f32)
     virt_col = virt_col.astype(jnp.int32)[:, 0:1]
-    total = None
+    small[4].wait()
+    masks = []
     for k in range(occ_local):
         kc_irrep = jnp.bitwise_xor(virt_col, occ_s_ref[base + k])
-        block = int_ref[k * virt_count:(k + 1) * virt_count, :]
-        masked = jnp.where(kc_irrep == col_irrep, block, jnp.zeros_like(block))
-        term = jnp.dot(amp_ref[:, k * virt_count:(k + 1) * virt_count], masked, preferred_element_type=f32)
-        total = term if total is None else total + term
-    out_ref[...] = total
+        block = int_v[k * virt_count:(k + 1) * virt_count, :]
+        masks.append(jnp.where(kc_irrep == col_irrep, block, jnp.zeros_like(block)))
+    outs = []
+    for m in range(chunks):
+        parts[m].wait()
+        total = None
+        for k in range(occ_local):
+            term = jnp.dot(amp_v[m * step:(m + 1) * step, k * virt_count:(k + 1) * virt_count], masks[k],
+                           preferred_element_type=f32)
+            total = term if total is None else total + term
+        out_v[m * step:(m + 1) * step, :] = total
+        rows_out = pltpu.make_async_copy(out_v.at[pl.ds(m * step, step), :], out_hbm.at[pl.ds(m * step, step), :],
+                                         out_sems.at[m])
+        rows_out.start()
+        outs.append(rows_out)
+    for rows_out in outs:
+        rows_out.wait()
 
 
 def masked_product(slab_start, occ_irrep, virt_irrep, amplitudes, integrals):
     rows, kc_local = amplitudes.shape
     cols = integrals.shape[1]
-    smem = pl.BlockSpec(memory_space=pltpu.SMEM)
+    hbm = pl.BlockSpec(memory_space=pl.ANY)
     vmem = pl.BlockSpec(memory_space=pltpu.VMEM)
+    chunks = rows // 256 if rows % 256 == 0 else 1
     return pl.pallas_call(
         _masked_product_kernel,
         out_shape=jax.ShapeDtypeStruct((rows, cols), jnp.float32),
-        in_specs=[smem, smem, vmem, vmem, vmem, vmem],
-        out_specs=vmem,
+        in_specs=[hbm] * 5,
+        out_specs=hbm,
+        scratch_shapes=[
+            pltpu.SMEM(slab_start.shape, jnp.int32),
+            pltpu.SMEM(occ_irrep.shape, jnp.int32),
+            pltpu.VMEM(occ_irrep.shape, jnp.int32),
+            pltpu.VMEM(virt_irrep.shape, jnp.int32),
+            pltpu.VMEM(amplitudes.shape, amplitudes.dtype),
+            pltpu.VMEM(integrals.shape, integrals.dtype),
+            pltpu.VMEM((rows, cols), jnp.float32),
+            pltpu.SemaphoreType.DMA((5 + chunks,)),
+            pltpu.SemaphoreType.DMA((chunks,)),
+        ],
         cost_estimate=pl.CostEstimate(
             flops=2 * rows * kc_local * cols,
             bytes_accessed=2 * rows * kc_local + 2 * kc_local * cols + 4 * rows * cols,
             transcendentals=0,
         ),
-    )(slab_start, occ_irrep, occ_irrep, virt_irrep, amplitudes, integrals)
+    )(slab_start, occ_irrep, virt_irrep, amplitudes, integrals)
 
 
 def body(amplitudes, integrals, occ_irrep, virt_irrep, occ_energy, virt_energy, slab_start):

time: 30.6 us -> 30.4 us (level)
  no operation moved by 1% of the time
where the time goes in v8:
time: 30.4 us; the launch traced here: 30.2 us
  starting transfers between devices  9.59 us (32%)
  waiting for transfers between devices  8.82 us (29%)
  between operations  4 us (13%)
  Pallas kernels  3.78 us (12%)
  local copies, waits for them, and re-layouts  2.88 us (9%)
  other arithmetic  1.17 us (4%)
    ppermute x5, starting transfers between devices, halving_scatter(): buf = keep + lax.ppermute(send, axis, perm)  9.59 us
    ppermute x5, waiting for transfers between devices, halving_scatter(): buf = keep + lax.ppermute(send, axis, perm)  8.82 us
    pallas_call x1, Pallas kernels, masked_product(): pl.pallas_call(_masked_product_kernel, out_shape=jax.ShapeDtypeStruct((ro...  3.78 us
    dynamic_slice x1, local copies, waits for them, and re-layouts, halving_scatter(): keep = lax.dynamic_index_in_dim(buf, bit, axis=where[0], keepdims=False)  1.3 us
    convert_element_type x1, other arithmetic, body(): (summed / (mine_energy[:, None] + col_energy[None, :])).astype(jnp.bfloat16)  0.69 us
  transfers between devices with their start and end apart: 5, of which 4 were waited for; matrix products, arithmetic and copies ran while one was open for 6% of the time, Pallas kernels for 0%

profile of v8, /device:TPU:0, one launch (start us, length us, event | category | flops | bytes accessed | tf_op | source)
XLA Modules:
  0.0 30.2 jit_solution(16769882035097509411)
XLA Ops:
  0.0 3.8 %shard_map.73 = f32[1024,256]{1,0:T(8,128)} custom-call(s32[2]{0:T(128)} %slab_hbm.1, s32[64]{0:T(128)} %occ_hbm.1, s32[512]{0:T(512)} %virt_hbm.1, bf16[1024,1024]{1,0:T(8,128)(2,1)} %amp_hbm.1, bf16[1024,256]{1,0:T(8,128)(2,1)} %int_hbm), custom_call_target="tpu_custom_call" | custom-call | flops 536870912 | bytes 3670016 | tf_op jit(solution)/shard_map/pallas_call | solution.py:120
  3.8 1.3 %constant_dynamic-slice_fusion.3 = (f32[2,2,2,2,1,32,256]{6,5,4,3,2,1,0:T(8,128)S(1)}, f32[2,2,2,2,1,32,256]{6,5,4,3,2,1,0:T(8,128)S(1)}) fusion(f32[2,2,2,2,2,32,256]{6,5,4,3,2,1,0:T(8,128)} %bitcast.36, s32[]{:T(128)S(6)} %select_n.78, s32[]{:T(128)S(6)} %select_n.79), kind=kLoop, calls=%fused_computation.21 | loop fusion | bytes 2097160 | tf_op jit(solution)/shard_map/jit(dynamic_index_in_dim)/dynamic_slice | solution.py:29
  5.1 0.0 copy-start.1
  5.1 0.0 copy-start.2
  5.1 0.0 copy-start.4
  5.1 0.0 copy-start
  5.2 0.5 %collective-permute-start = (f32[2,2,2,2,32,256]{5,4,2,1,0,3:T(8,128)S(1)}, f32[2,2,2,2,32,256]{5,4,2,1,0,3:T(8,128)S(1)}, u32[]{:S(2)}, u32[]{:S(2)}) collective-permute-start(f32[2,2,2,2,32,256]{5,4,2,1,0,3:T(8,128)S(1)} %bitcast.37), channel_id=1, source_target_pairs={{0,1},{1,0},{2,3},{3,2},{4,5},{5,4},{6,7},{7,6},{8,9},{9,8},{10,11... | collective-permute-start | bytes 1572872 | tf_op jit(solution)/shard_map/ppermute | solution.py:42
  5.7 1.5 %collective-permute-done = f32[2,2,2,2,32,256]{5,4,2,1,0,3:T(8,128)S(1)} collective-permute-done((f32[2,2,2,2,32,256]{5,4,2,1,0,3:T(8,128)S(1)}, f32[2,2,2,2,32,256]{5,4,2,1,0,3:T(8,128)S(1)}, u32[]{:S(2)}, u32[]{:S(2)}) %collective-permute-start) | collective-permute-done | bytes 524320 | tf_op jit(solution)/shard_map/ppermute | solution.py:42
  7.2 0.0 copy-start.3
  7.3 0.1 bitcast_add_fusion
  7.4 2.9 %collective-permute-start.1 = (f32[2,2,2,32,256]{4,3,2,1,0:T(8,128)S(1)}, f32[2,2,2,32,256]{4,3,2,1,0:T(8,128)S(1)}, u32[]{:S(2)}, u32[]{:S(2)}) collective-permute-start(f32[2,2,2,32,256]{4,3,2,1,0:T(8,128)S(1)} %bitcast_select_fusion), channel_id=1, source_target_pairs={{0,2},{1,5},{2,0},{3,7},{4,6},{5,1},{6,4},{7,3},{8,10},{9,13},{10,... | collective-permute-start | bytes 786440 | tf_op jit(solution)/shard_map/ppermute | solution.py:42
  10.4 0.0 copy-done.1
  10.4 0.6 %fusion.4 = (s32[1]{0:T(128)}, s32[1]{0:T(128)}) fusion(s32[2]{0:T(128)S(1)} %copy-done.1), kind=kLoop, calls=%fused_computation.22 | loop fusion | bytes 16 | tf_op jit(solution)/shard_map/slice | solution.py:157
  14.2 0.0 copy-done.2
  14.2 0.1 dynamic_slice.60
  14.3 0.0 copy-done.4
  14.3 0.1 dynamic_slice.75
  15.0 0.1 dynamic_slice.77
  15.1 0.0 copy-done
  15.1 0.1 broadcast_xor_fusion.1
  15.1 0.0 collective-permute-done.1
  15.1 0.1 fusion
  15.2 1.7 %collective-permute-start.2 = (f32[2,2,32,256]{3,2,1,0:T(8,128)S(1)}, f32[2,2,32,256]{3,2,1,0:T(8,128)S(1)}, u32[]{:S(2)}, u32[]{:S(2)}) collective-permute-start(f32[2,2,32,256]{3,2,1,0:T(8,128)S(1)} %dynamic-slice_bitcast_fusion), channel_id=1, source_target_pairs={{0,4},{1,3},{2,6},{3,1},{4,0},{5,7},{6,2},{7,5},{8,12},{9,11},{10,... | collective-permute-start | bytes 393224 | tf_op jit(solution)/shard_map/ppermute | solution.py:42
  16.9 0.0 copy-done.3
  16.9 0.1 broadcast_subtract_fusion.1
  17.0 3.3 %collective-permute-done.2 = f32[2,2,32,256]{3,2,1,0:T(8,128)S(1)} collective-permute-done((f32[2,2,32,256]{3,2,1,0:T(8,128)S(1)}, f32[2,2,32,256]{3,2,1,0:T(8,128)S(1)}, u32[]{:S(2)}, u32[]{:S(2)}) %collective-permute-start.2) | collective-permute-done | bytes 131104 | tf_op jit(solution)/shard_map/ppermute | solution.py:42
  20.3 1.7 %collective-permute-start.3 = (f32[2,32,256]{2,1,0:T(8,128)S(1)}, f32[2,32,256]{2,1,0:T(8,128)S(1)}, u32[]{:S(2)}, u32[]{:S(2)}) collective-permute-start(f32[2,32,256]{2,1,0:T(8,128)S(1)} %dynamic-slice_bitcast_fusion.1), channel_id=1, source_target_pairs={{0,8},{1,9},{2,10},{3,11},{4,12},{5,13},{6,14},{7,15},{8,0},{9,1},... | collective-permute-start | bytes 196616 | tf_op jit(solution)/shard_map/ppermute | solution.py:42
  22.0 0.1 broadcast_subtract_fusion
  22.1 0.1 dynamic_slice.62
  22.2 2.5 %collective-permute-done.3 = f32[2,32,256]{2,1,0:T(8,128)S(1)} collective-permute-done((f32[2,32,256]{2,1,0:T(8,128)S(1)}, f32[2,32,256]{2,1,0:T(8,128)S(1)}, u32[]{:S(2)}, u32[]{:S(2)}) %collective-permute-start.3) | collective-permute-done | bytes 65568 | tf_op jit(solution)/shard_map/ppermute | solution.py:42
  24.7 2.7 %collective-permute-start.4 = (f32[32,256]{1,0:T(8,128)S(1)}, f32[32,256]{1,0:T(8,128)S(1)}, u32[]{:S(2)}, u32[]{:S(2)}) collective-permute-start(f32[32,256]{1,0:T(8,128)S(1)} %dynamic-slice_bitcast_fusion.2), channel_id=1, source_target_pairs={{0,16},{1,17},{2,18},{3,19},{4,20},{5,21},{6,22},{7,23},{8,24},{9,... | collective-permute-start | bytes 98312 | tf_op jit(solution)/shard_map/ppermute | solution.py:42
  27.4 0.1 broadcast_xor_fusion
  27.5 0.1 xor.40
  27.6 0.1 sub.64
  27.6 0.1 dynamic_slice.61
  27.7 0.1 dynamic_slice.76
  27.8 0.1 sub.68
  27.9 0.1 xor.44
  28.0 1.5 %collective-permute-done.4 = f32[32,256]{1,0:T(8,128)S(1)} collective-permute-done((f32[32,256]{1,0:T(8,128)S(1)}, f32[32,256]{1,0:T(8,128)S(1)}, u32[]{:S(2)}, u32[]{:S(2)}) %collective-permute-start.4) | collective-permute-done | bytes 32800 | tf_op jit(solution)/shard_map/ppermute | solution.py:42
  29.6 0.7 %fusion.3 = bf16[32,256]{1,0:T(8,128)(2,1)} fusion(f32[32,256]{1,0:T(8,128)S(1)} %collective-permute-done.4, f32[2,32,256]{2,1,0:T(8,128)S(1)} %bitcast_add_fusion.2, s32[]{:T(128)S(6)} %select_n.91, f32[256]{0:T(256)S(1)} %sub.68, f32[32]{0:T(128)S(1)} %dynamic_slice.76, s32[256]{0:T(256)S(1)} %xor.44, s32[32]{0:T(128)S(1)} %dynamic_slice.61), kind=kLoop, calls=%fused_computation.12 | loop fusion | flops 49152 | bytes 84228 | tf_op jit(solution)/shard_map/convert_element_type | solution.py:180
  (8 shorter events, 0.2 us)
Async XLA Ops:
  5.1 5.3 %copy-start.1 = (s32[2]{0:T(128)S(1)}, s32[2]{0:T(128)}, u32[]{:S(2)}) copy-start(s32[2]{0:T(128)} %slab_hbm.1) | copy-start | bytes 28
  5.1 9.1 %copy-start.2 = (s32[512]{0:T(512)S(1)}, s32[512]{0:T(512)}, u32[]{:S(2)}) copy-start(s32[512]{0:T(512)} %virt_hbm.1) | copy-start | bytes 6148
  5.1 9.1 %copy-start.4 = (f32[512]{0:T(512)S(1)}, f32[512]{0:T(512)}, u32[]{:S(2)}) copy-start(f32[512]{0:T(512)} %param.12) | copy-start | bytes 6148
  5.1 9.9 %copy-start = (s32[64]{0:T(128)S(1)}, s32[64]{0:T(128)}, u32[]{:S(2)}) copy-start(s32[64]{0:T(128)} %occ_hbm.1) | copy-start | bytes 772
  5.2 2.1 %collective-permute-start = (f32[2,2,2,2,32,256]{5,4,2,1,0,3:T(8,128)S(1)}, f32[2,2,2,2,32,256]{5,4,2,1,0,3:T(8,128)S(1)}, u32[]{:S(2)}, u32[]{:S(2)}) collective-permute-start(f32[2,2,2,2,32,256]{5,4,2,1,0,3:T(8,128)S(1)} %bitcast.37), channel_id=1, source_target_pairs={{0,1},{1,0},{2,3},{3,2},{4,5},{5,4},{6,7},{7,6},{8,9},{9,8},{10,11... | collective-permute-start | bytes 1572872 | tf_op jit(solution)/shard_map/ppermute | solution.py:42
  7.2 9.7 %copy-start.3 = (f32[64]{0:T(128)S(1)}, f32[64]{0:T(128)}, u32[]{:S(2)}) copy-start(f32[64]{0:T(128)} %param.11) | copy-start | bytes 772
  7.4 7.7 %collective-permute-start.1 = (f32[2,2,2,32,256]{4,3,2,1,0:T(8,128)S(1)}, f32[2,2,2,32,256]{4,3,2,1,0:T(8,128)S(1)}, u32[]{:S(2)}, u32[]{:S(2)}) collective-permute-start(f32[2,2,2,32,256]{4,3,2,1,0:T(8,128)S(1)} %bitcast_select_fusion), channel_id=1, source_target_pairs={{0,2},{1,5},{2,0},{3,7},{4,6},{5,1},{6,4},{7,3},{8,10},{9,13},{10,... | collective-permute-start | bytes 786440 | tf_op jit(solution)/shard_map/ppermute | solution.py:42
  15.2 5.0 %collective-permute-start.2 = (f32[2,2,32,256]{3,2,1,0:T(8,128)S(1)}, f32[2,2,32,256]{3,2,1,0:T(8,128)S(1)}, u32[]{:S(2)}, u32[]{:S(2)}) collective-permute-start(f32[2,2,32,256]{3,2,1,0:T(8,128)S(1)} %dynamic-slice_bitcast_fusion), channel_id=1, source_target_pairs={{0,4},{1,3},{2,6},{3,1},{4,0},{5,7},{6,2},{7,5},{8,12},{9,11},{10,... | collective-permute-start | bytes 393224 | tf_op jit(solution)/shard_map/ppermute | solution.py:42
  20.3 4.3 %collective-permute-start.3 = (f32[2,32,256]{2,1,0:T(8,128)S(1)}, f32[2,32,256]{2,1,0:T(8,128)S(1)}, u32[]{:S(2)}, u32[]{:S(2)}) collective-permute-start(f32[2,32,256]{2,1,0:T(8,128)S(1)} %dynamic-slice_bitcast_fusion.1), channel_id=1, source_target_pairs={{0,8},{1,9},{2,10},{3,11},{4,12},{5,13},{6,14},{7,15},{8,0},{9,1},... | collective-permute-start | bytes 196616 | tf_op jit(solution)/shard_map/ppermute | solution.py:42
  24.7 4.9 %collective-permute-start.4 = (f32[32,256]{1,0:T(8,128)S(1)}, f32[32,256]{1,0:T(8,128)S(1)}, u32[]{:S(2)}, u32[]{:S(2)}) collective-permute-start(f32[32,256]{1,0:T(8,128)S(1)} %dynamic-slice_bitcast_fusion.2), channel_id=1, source_target_pairs={{0,16},{1,17},{2,18},{3,19},{4,20},{5,21},{6,22},{7,23},{8,24},{9,... | collective-permute-start | bytes 98312 | tf_op jit(solution)/shard_map/ppermute | solution.py:42

commit v9 on v2

--- a/solution.py
+++ b/solution.py
@@ -1,6 +1,10 @@
+import functools
+
 import jax
 import jax.numpy as jnp
 from jax import lax
+from jax.experimental import pallas as pl
+from jax.experimental.pallas import tpu as pltpu
 from jax.sharding import PartitionSpec as P
 
 
@@ -41,6 +45,46 @@
     return buf.reshape(block, cols)
 
 
+def _irrep_kernel(pair_rows, slab_ref, occ_s_ref, occ_v_ref, virt_v_ref, row_ref, kc_ref, col_ref):
+    virt_count = virt_v_ref.shape[0]
+    occ_count = occ_v_ref.shape[0]
+    rows = row_ref.shape[1]
+    kc_local = kc_ref.shape[1]
+    cols = col_ref.shape[1]
+    occ_local = kc_local // virt_count
+    f32, bf16, i32 = jnp.float32, jnp.bfloat16, jnp.int32
+    occ_rows = jnp.broadcast_to(occ_v_ref[...].reshape(1, occ_count), (8, occ_count)).astype(bf16)
+    virt_rows = jnp.broadcast_to(virt_v_ref[...].reshape(1, virt_count), (8, virt_count)).astype(bf16)
+
+    def spread(count, starts, per, dst):
+        x_of = lax.broadcasted_iota(i32, (occ_count, count), 1)
+        j_of = lax.broadcasted_iota(i32, (occ_count, count), 0)
+        occ_part = jnp.dot(occ_rows, (x_of // per == j_of).astype(bf16), preferred_element_type=f32)
+        x_of = lax.broadcasted_iota(i32, (virt_count, count), 1)
+        c_of = lax.broadcasted_iota(i32, (virt_count, count), 0)
+        virt_part = jnp.dot(virt_rows, (c_of == starts + x_of % per).astype(bf16), preferred_element_type=f32)
+        return jnp.bitwise_xor(occ_part.astype(i32), virt_part.astype(i32))[0:1, :]
+
+    per_row = rows * pair_rows // occ_count
+    row_ref[...] = spread(rows, slab_ref[0], per_row, None)
+    col_ref[...] = spread(cols, slab_ref[1], cols // occ_count, None)
+    base = lax.axis_index("contr") * occ_local
+    parts = [jnp.bitwise_xor(virt_v_ref[...].reshape(1, virt_count), occ_s_ref[base + k]) for k in range(occ_local)]
+    kc_ref[...] = jnp.concatenate(parts, axis=1) if occ_local > 1 else parts[0]
+
+
+def irreps(pair_count, slab_start, occ_irrep, virt_irrep, rows, kc_local, cols):
+    smem = pl.BlockSpec(memory_space=pltpu.SMEM)
+    vmem = pl.BlockSpec(memory_space=pltpu.VMEM)
+    shapes = [jax.ShapeDtypeStruct((1, n), jnp.int32) for n in (rows, kc_local, cols)]
+    return pl.pallas_call(
+        functools.partial(_irrep_kernel, pair_count),
+        out_shape=shapes,
+        in_specs=[smem, smem, vmem, vmem],
+        out_specs=[vmem, vmem, vmem],
+    )(slab_start, occ_irrep, occ_irrep, virt_irrep)
+
+
 def body(amplitudes, integrals, occ_irrep, virt_irrep, occ_energy, virt_energy, slab_start):
     pair_count = lax.axis_size("pair")
     contr_count = lax.axis_size("contr")
@@ -64,12 +108,13 @@
     col_irrep = jnp.bitwise_xor(occ_irrep[:, None], b_irrep[None, :]).reshape(-1)
     row_energy = (occ_energy[:, None] - a_energy[None, :]).reshape(-1)
     col_energy = (occ_energy[:, None] - b_energy[None, :]).reshape(-1)
-    local_occ = lax.dynamic_slice(occ_irrep, (contr_index * occ_local,), (occ_local,))
-    kc_irrep = jnp.bitwise_xor(local_occ[:, None], virt_irrep[None, :]).reshape(-1)
     zero = jnp.zeros((), jnp.bfloat16)
     whole_int = lax.all_gather(integrals, "pair", axis=1, tiled=True)
-    int_masked = jnp.where(kc_irrep[:, None] == col_irrep[None, :], whole_int, zero)
-    row_irrep_pair = lax.dynamic_slice(row_irrep, (pair_index * rows_pair,), (rows_pair,))
+    row_k, kc_k, col_k = irreps(pair_count, slab_start, occ_irrep, virt_irrep,
+                                rows_pair * pair_count, kc_local, cols_pair * pair_count)
+    kc_irrep = kc_k.reshape(-1)
+    int_masked = jnp.where(kc_irrep[:, None] == col_k.reshape(-1)[None, :], whole_int, zero)
+    row_irrep_pair = lax.dynamic_slice(row_k.reshape(-1), (pair_index * rows_pair,), (rows_pair,))
     amp_masked = jnp.where(row_irrep_pair[:, None] == kc_irrep[None, :], amplitudes, zero)
     partial = jnp.dot(amp_masked, int_masked, preferred_element_type=jnp.float32)
     if contr_count & (contr_count - 1) == 0 and rows_pair % contr_count == 0:

time: 38 us -> 29.8 us (0.78)
  waiting for transfers between devices: 12.4 us -> 7.93 us
  local copies, waits for them, and re-layouts: 4.38 us -> 1.28 us
  other arithmetic: 3.23 us -> 1.03 us
  Pallas kernels: 0 us -> 1.61 us
    ppermute x5, waiting for transfers between devices: 12.4 us -> 7.93 us  [halving_scatter(): buf = keep + lax.ppermute(send, axis, perm)]
    dynamic_slice x3 -> x0, local copies, waits for them, and re-layouts: 2.25 us -> none  [the longest x1 0.76 us: body(): a_irrep = lax.dynamic_slice(virt_irrep, (first_start,), (slab_first,))]
    pallas_call x0 -> x1, Pallas kernels: none -> 1.61 us  [irreps(): pl.pallas_call(functools.partial(_irrep_kernel, pair_count), out_shape=sh...]
    xor x2 -> x0, other arithmetic: 1.45 us -> none  [the longest x1 0.73 us: body(): jnp.bitwise_xor(occ_irrep[:, None], a_irrep[None, :]).reshape(-1)]
    unnamed x1 -> x0, other arithmetic: 0.75 us -> none
    slice x1, local copies, waits for them, and re-layouts: 1.31 us -> 0.65 us  [body(): first_start = slab_start[0]]
  transfers between devices with their start and end apart: 5 -> 5, of which waited for: 5 -> 5; matrix products, arithmetic and copies ran while one was open for 1% -> 4% of each run, Pallas kernels for 0% -> 0%
where the time goes in v9:
time: 29.8 us; the launch traced here: 29.6 us
  starting transfers between devices  11.1 us (37%)
  waiting for transfers between devices  7.93 us (27%)
  between operations  3.93 us (13%)
  matrix products  2.71 us (9%)
  Pallas kernels  1.61 us (5%)
  local copies, waits for them, and re-layouts  1.28 us (4%)
  other arithmetic  1.03 us (3%)
    ppermute x5, starting transfers between devices, halving_scatter(): buf = keep + lax.ppermute(send, axis, perm)  11.1 us
    ppermute x5, waiting for transfers between devices, halving_scatter(): buf = keep + lax.ppermute(send, axis, perm)  7.93 us
    dot_general x1, matrix products, body(): jnp.dot(amp_masked, int_masked, preferred_element_type=jnp.float32)  2.71 us
    pallas_call x1, Pallas kernels, irreps(): pl.pallas_call(functools.partial(_irrep_kernel, pair_count), out_shape=sh...  1.61 us
    convert_element_type x1, other arithmetic, body(): (summed / (mine_energy[:, None] + col_energy[None, :])).astype(jnp.bfloat16)  0.69 us
    slice x1, local copies, waits for them, and re-layouts, body(): first_start = slab_start[0]  0.65 us
  transfers between devices with their start and end apart: 5, of which 5 were waited for; matrix products, arithmetic and copies ran while one was open for 4% of the time, Pallas kernels for 0%

profile of v9, /device:TPU:0, one launch (start us, length us, event | category | flops | bytes accessed | tf_op | source)
XLA Modules:
  0.0 29.6 jit_solution(4659536748017245843)
XLA Ops:
  0.0 1.6 %shard_map.73 = (s32[1,1024]{1,0:T(1,128)}, s32[1,1024]{1,0:T(1,128)}, s32[1,256]{1,0:T(1,128)}) custom-call(s32[2]{0:T(128)} %slab_ref.1, s32[64]{0:T(128)} %occ_v_ref.1, s32[64]{0:T(128)} %occ_v_ref.1, s32[512]{0:T(512)} %virt_v_ref.1), custom_call_target="tpu_custom_call" | custom-call | tf_op jit(solution)/shard_map/pallas_call | solution.py:80
  1.6 2.7 %fusion = f32[1024,256]{1,0:T(8,128)S(1)} fusion(bf16[1024,1024]{1,0:T(8,128)(2,1)} %param.7, s32[1024]{0:T(1024)} %bitcast.40, s32[1024]{0:T(1024)} %bitcast.39, bf16[1024,256]{1,0:T(8,128)(2,1)} %param.8, s32[256]{0:T(256)} %bitcast.41), kind=kOutput, calls=%fused_computation.1 | convolution fusion | flops 539492352 | bytes 3679232 | tf_op jit(solution)/shard_map/dot_general | solution.py:119
  4.3 0.1 constant_dynamic-slice_fusion.3
  4.5 0.5 %collective-permute-start = (f32[2,2,2,2,32,256]{5,4,2,1,0,3:T(8,128)S(1)}, f32[2,2,2,2,32,256]{5,4,2,1,0,3:T(8,128)S(1)}, u32[]{:S(2)}, u32[]{:S(2)}) collective-permute-start(f32[2,2,2,2,32,256]{5,4,2,1,0,3:T(8,128)S(1)} %bitcast.38), channel_id=1, source_target_pairs={{0,1},{1,0},{2,3},{3,2},{4,5},{5,4},{6,7},{7,6},{8,9},{9,8},{10,11... | collective-permute-start | bytes 1572872 | tf_op jit(solution)/shard_map/ppermute | solution.py:44
  5.0 1.5 %collective-permute-done = f32[2,2,2,2,32,256]{5,4,2,1,0,3:T(8,128)S(1)} collective-permute-done((f32[2,2,2,2,32,256]{5,4,2,1,0,3:T(8,128)S(1)}, f32[2,2,2,2,32,256]{5,4,2,1,0,3:T(8,128)S(1)}, u32[]{:S(2)}, u32[]{:S(2)}) %collective-permute-start) | collective-permute-done | bytes 524320 | tf_op jit(solution)/shard_map/ppermute | solution.py:44
  6.5 0.0 copy-start
  6.5 0.0 copy-start.2
  6.5 0.1 bitcast_add_fusion
  6.6 0.0 copy-start.1
  6.7 2.9 %collective-permute-start.1 = (f32[2,2,2,32,256]{4,3,2,1,0:T(8,128)S(1)}, f32[2,2,2,32,256]{4,3,2,1,0:T(8,128)S(1)}, u32[]{:S(2)}, u32[]{:S(2)}) collective-permute-start(f32[2,2,2,32,256]{4,3,2,1,0:T(8,128)S(1)} %bitcast_select_fusion), channel_id=1, source_target_pairs={{0,2},{1,5},{2,0},{3,7},{4,6},{5,1},{6,4},{7,3},{8,10},{9,13},{10,... | collective-permute-start | bytes 786440 | tf_op jit(solution)/shard_map/ppermute | solution.py:44
  9.6 4.4 %collective-permute-done.1 = f32[2,2,2,32,256]{4,3,2,1,0:T(8,128)S(1)} collective-permute-done((f32[2,2,2,32,256]{4,3,2,1,0:T(8,128)S(1)}, f32[2,2,2,32,256]{4,3,2,1,0:T(8,128)S(1)}, u32[]{:S(2)}, u32[]{:S(2)}) %collective-permute-start.1) | collective-permute-done | bytes 262176 | tf_op jit(solution)/shard_map/ppermute | solution.py:44
  14.0 0.1 fusion.6
  14.1 2.1 %collective-permute-start.2 = (f32[2,2,32,256]{3,2,1,0:T(8,128)S(1)}, f32[2,2,32,256]{3,2,1,0:T(8,128)S(1)}, u32[]{:S(2)}, u32[]{:S(2)}) collective-permute-start(f32[2,2,32,256]{3,2,1,0:T(8,128)S(1)} %dynamic-slice_bitcast_fusion), channel_id=1, source_target_pairs={{0,4},{1,3},{2,6},{3,1},{4,0},{5,7},{6,2},{7,5},{8,12},{9,11},{10,... | collective-permute-start | bytes 393224 | tf_op jit(solution)/shard_map/ppermute | solution.py:44
  16.2 0.0 copy-done
  16.2 0.6 %fusion.11 = (s32[1]{0:T(128)}, s32[1]{0:T(128)}) fusion(s32[2]{0:T(128)S(1)} %copy-done), kind=kLoop, calls=%fused_computation.29 | loop fusion | bytes 16 | tf_op jit(solution)/shard_map/slice | solution.py:101
  18.8 0.0 copy-done.2
  18.8 0.1 dynamic_slice.64
  18.9 0.3 collective-permute-done.2
  19.2 2.1 %collective-permute-start.3 = (f32[2,32,256]{2,1,0:T(8,128)S(1)}, f32[2,32,256]{2,1,0:T(8,128)S(1)}, u32[]{:S(2)}, u32[]{:S(2)}) collective-permute-start(f32[2,32,256]{2,1,0:T(8,128)S(1)} %dynamic-slice_bitcast_fusion.1), channel_id=1, source_target_pairs={{0,8},{1,9},{2,10},{3,11},{4,12},{5,13},{6,14},{7,15},{8,0},{9,1},... | collective-permute-start | bytes 196616 | tf_op jit(solution)/shard_map/ppermute | solution.py:44
  21.3 0.0 copy-done.1
  21.3 0.1 broadcast_subtract_fusion.1
  23.3 0.1 dynamic_slice.66
  23.3 0.2 collective-permute-done.3
  23.6 3.4 %collective-permute-start.4 = (f32[32,256]{1,0:T(8,128)S(1)}, f32[32,256]{1,0:T(8,128)S(1)}, u32[]{:S(2)}, u32[]{:S(2)}) collective-permute-start(f32[32,256]{1,0:T(8,128)S(1)} %dynamic-slice_bitcast_fusion.2), channel_id=1, source_target_pairs={{0,16},{1,17},{2,18},{3,19},{4,20},{5,21},{6,22},{7,23},{8,24},{9,... | collective-permute-start | bytes 98312 | tf_op jit(solution)/shard_map/ppermute | solution.py:44
  27.0 0.1 broadcast_subtract_fusion
  27.1 0.1 sub.64
  27.2 0.1 sub.68
  27.3 0.1 dynamic_slice.65
  27.4 1.6 %collective-permute-done.4 = f32[32,256]{1,0:T(8,128)S(1)} collective-permute-done((f32[32,256]{1,0:T(8,128)S(1)}, f32[32,256]{1,0:T(8,128)S(1)}, u32[]{:S(2)}, u32[]{:S(2)}) %collective-permute-start.4) | collective-permute-done | bytes 32800 | tf_op jit(solution)/shard_map/ppermute | solution.py:44
  28.9 0.7 %fusion.9 = bf16[32,256]{1,0:T(8,128)(2,1)} fusion(f32[32,256]{1,0:T(8,128)S(1)} %collective-permute-done.4, f32[2,32,256]{2,1,0:T(8,128)S(1)} %bitcast_add_fusion.2, s32[]{:T(128)S(6)} %select_n.92, f32[256]{0:T(256)S(1)} %sub.68, f32[32]{0:T(128)S(1)} %dynamic_slice.65), kind=kLoop, calls=%fused_computation.20 | loop fusion | flops 32768 | bytes 83076 | tf_op jit(solution)/shard_map/convert_element_type | solution.py:127
  (8 shorter events, 0.2 us)
Async XLA Ops:
  4.5 2.0 %collective-permute-start = (f32[2,2,2,2,32,256]{5,4,2,1,0,3:T(8,128)S(1)}, f32[2,2,2,2,32,256]{5,4,2,1,0,3:T(8,128)S(1)}, u32[]{:S(2)}, u32[]{:S(2)}) collective-permute-start(f32[2,2,2,2,32,256]{5,4,2,1,0,3:T(8,128)S(1)} %bitcast.38), channel_id=1, source_target_pairs={{0,1},{1,0},{2,3},{3,2},{4,5},{5,4},{6,7},{7,6},{8,9},{9,8},{10,11... | collective-permute-start | bytes 1572872 | tf_op jit(solution)/shard_map/ppermute | solution.py:44
  6.5 9.7 %copy-start = (s32[2]{0:T(128)S(1)}, s32[2]{0:T(128)}, u32[]{:S(2)}) copy-start(s32[2]{0:T(128)} %slab_ref.1) | copy-start | bytes 28
  6.5 12.3 %copy-start.2 = (f32[512]{0:T(512)S(1)}, f32[512]{0:T(512)}, u32[]{:S(2)}) copy-start(f32[512]{0:T(512)} %param.12) | copy-start | bytes 6148
  6.6 14.7 %copy-start.1 = (f32[64]{0:T(128)S(1)}, f32[64]{0:T(128)}, u32[]{:S(2)}) copy-start(f32[64]{0:T(128)} %param.11) | copy-start | bytes 772
  6.7 7.3 %collective-permute-start.1 = (f32[2,2,2,32,256]{4,3,2,1,0:T(8,128)S(1)}, f32[2,2,2,32,256]{4,3,2,1,0:T(8,128)S(1)}, u32[]{:S(2)}, u32[]{:S(2)}) collective-permute-start(f32[2,2,2,32,256]{4,3,2,1,0:T(8,128)S(1)} %bitcast_select_fusion), channel_id=1, source_target_pairs={{0,2},{1,5},{2,0},{3,7},{4,6},{5,1},{6,4},{7,3},{8,10},{9,13},{10,... | collective-permute-start | bytes 786440 | tf_op jit(solution)/shard_map/ppermute | solution.py:44
  14.1 5.0 %collective-permute-start.2 = (f32[2,2,32,256]{3,2,1,0:T(8,128)S(1)}, f32[2,2,32,256]{3,2,1,0:T(8,128)S(1)}, u32[]{:S(2)}, u32[]{:S(2)}) collective-permute-start(f32[2,2,32,256]{3,2,1,0:T(8,128)S(1)} %dynamic-slice_bitcast_fusion), channel_id=1, source_target_pairs={{0,4},{1,3},{2,6},{3,1},{4,0},{5,7},{6,2},{7,5},{8,12},{9,11},{10,... | collective-permute-start | bytes 393224 | tf_op jit(solution)/shard_map/ppermute | solution.py:44
  19.2 4.4 %collective-permute-start.3 = (f32[2,32,256]{2,1,0:T(8,128)S(1)}, f32[2,32,256]{2,1,0:T(8,128)S(1)}, u32[]{:S(2)}, u32[]{:S(2)}) collective-permute-start(f32[2,32,256]{2,1,0:T(8,128)S(1)} %dynamic-slice_bitcast_fusion.1), channel_id=1, source_target_pairs={{0,8},{1,9},{2,10},{3,11},{4,12},{5,13},{6,14},{7,15},{8,0},{9,1},... | collective-permute-start | bytes 196616 | tf_op jit(solution)/shard_map/ppermute | solution.py:44
  23.6 5.3 %collective-permute-start.4 = (f32[32,256]{1,0:T(8,128)S(1)}, f32[32,256]{1,0:T(8,128)S(1)}, u32[]{:S(2)}, u32[]{:S(2)}) collective-permute-start(f32[32,256]{1,0:T(8,128)S(1)} %dynamic-slice_bitcast_fusion.2), channel_id=1, source_target_pairs={{0,16},{1,17},{2,18},{3,19},{4,20},{5,21},{6,22},{7,23},{8,24},{9,... | collective-permute-start | bytes 98312 | tf_op jit(solution)/shard_map/ppermute | solution.py:44

commit v10 on v9

--- a/solution.py
+++ b/solution.py
@@ -45,7 +45,8 @@
     return buf.reshape(block, cols)
 
 
-def _irrep_kernel(pair_rows, slab_ref, occ_s_ref, occ_v_ref, virt_v_ref, row_ref, kc_ref, col_ref):
+def _irrep_kernel(pair_rows, slab_ref, occ_s_ref, occ_v_ref, virt_v_ref, occ_e_ref, virt_e_ref,
+                  row_ref, kc_ref, col_ref, denom_ref):
     virt_count = virt_v_ref.shape[0]
     occ_count = occ_v_ref.shape[0]
     rows = row_ref.shape[1]
@@ -65,24 +66,45 @@
         virt_part = jnp.dot(virt_rows, (c_of == starts + x_of % per).astype(bf16), preferred_element_type=f32)
         return jnp.bitwise_xor(occ_part.astype(i32), virt_part.astype(i32))[0:1, :]
 
-    per_row = rows * pair_rows // occ_count
+    per_row = rows // occ_count
     row_ref[...] = spread(rows, slab_ref[0], per_row, None)
     col_ref[...] = spread(cols, slab_ref[1], cols // occ_count, None)
     base = lax.axis_index("contr") * occ_local
     parts = [jnp.bitwise_xor(virt_v_ref[...].reshape(1, virt_count), occ_s_ref[base + k]) for k in range(occ_local)]
     kc_ref[...] = jnp.concatenate(parts, axis=1) if occ_local > 1 else parts[0]
+    mine, all_cols = denom_ref.shape
+    per_col = all_cols // occ_count
+    q_of = lax.broadcasted_iota(i32, (1, all_cols), 1)
+
+    def col_step(j, acc):
+        return jnp.where(q_of // per_col == j, occ_e_ref[j], acc)
+
+    col_occ = lax.fori_loop(0, occ_count, col_step, jnp.zeros((1, all_cols), f32))
+    col_virt = jnp.zeros((1, all_cols), f32)
+    for b in range(per_col):
+        col_virt = jnp.where(q_of % per_col == b, virt_e_ref[slab_ref[1] + b], col_virt)
+    first_row = (lax.axis_index("pair") * lax.axis_size("contr") + lax.axis_index("contr")) * mine
+    t_of = lax.broadcasted_iota(i32, (mine, all_cols), 0)
+    row_occ = jnp.zeros((mine, all_cols), f32)
+    row_virt = jnp.zeros((mine, all_cols), f32)
+    for t in range(mine):
+        r = first_row + t
+        row_occ = jnp.where(t_of == t, occ_e_ref[r // per_row], row_occ)
+        row_virt = jnp.where(t_of == t, virt_e_ref[slab_ref[0] + r % per_row], row_virt)
+    denom_ref[...] = (row_occ - row_virt) + (col_occ - col_virt)
 
 
-def irreps(pair_count, slab_start, occ_irrep, virt_irrep, rows, kc_local, cols):
+def irreps(pair_count, slab_start, occ_irrep, virt_irrep, occ_energy, virt_energy, rows, kc_local, cols, mine):
     smem = pl.BlockSpec(memory_space=pltpu.SMEM)
     vmem = pl.BlockSpec(memory_space=pltpu.VMEM)
     shapes = [jax.ShapeDtypeStruct((1, n), jnp.int32) for n in (rows, kc_local, cols)]
+    shapes.append(jax.ShapeDtypeStruct((mine, cols), jnp.float32))
     return pl.pallas_call(
         functools.partial(_irrep_kernel, pair_count),
         out_shape=shapes,
-        in_specs=[smem, smem, vmem, vmem],
-        out_specs=[vmem, vmem, vmem],
-    )(slab_start, occ_irrep, occ_irrep, virt_irrep)
+        in_specs=[smem, smem, vmem, vmem, smem, smem],
+        out_specs=[vmem, vmem, vmem, vmem],
+    )(slab_start, occ_irrep, occ_irrep, virt_irrep, occ_energy, virt_energy)
 
 
 def body(amplitudes, integrals, occ_irrep, virt_irrep, occ_energy, virt_energy, slab_start):
@@ -96,22 +118,10 @@
     rows_pair = amplitudes.shape[0]
     cols_pair = integrals.shape[1]
     rows_device = rows_pair // contr_count
-    slab_first = amplitudes.shape[0] * pair_count // occ_irrep.shape[0]
-    slab_second = cols_pair * pair_count // occ_irrep.shape[0]
-    first_start = slab_start[0]
-    second_start = slab_start[1]
-    a_irrep = lax.dynamic_slice(virt_irrep, (first_start,), (slab_first,))
-    b_irrep = lax.dynamic_slice(virt_irrep, (second_start,), (slab_second,))
-    a_energy = lax.dynamic_slice(virt_energy, (first_start,), (slab_first,))
-    b_energy = lax.dynamic_slice(virt_energy, (second_start,), (slab_second,))
-    row_irrep = jnp.bitwise_xor(occ_irrep[:, None], a_irrep[None, :]).reshape(-1)
-    col_irrep = jnp.bitwise_xor(occ_irrep[:, None], b_irrep[None, :]).reshape(-1)
-    row_energy = (occ_energy[:, None] - a_energy[None, :]).reshape(-1)
-    col_energy = (occ_energy[:, None] - b_energy[None, :]).reshape(-1)
     zero = jnp.zeros((), jnp.bfloat16)
     whole_int = lax.all_gather(integrals, "pair", axis=1, tiled=True)
-    row_k, kc_k, col_k = irreps(pair_count, slab_start, occ_irrep, virt_irrep,
-                                rows_pair * pair_count, kc_local, cols_pair * pair_count)
+    row_k, kc_k, col_k, denom = irreps(pair_count, slab_start, occ_irrep, virt_irrep, occ_energy, virt_energy,
+                                       rows_pair * pair_count, kc_local, cols_pair * pair_count, rows_device)
     kc_irrep = kc_k.reshape(-1)
     int_masked = jnp.where(kc_irrep[:, None] == col_k.reshape(-1)[None, :], whole_int, zero)
     row_irrep_pair = lax.dynamic_slice(row_k.reshape(-1), (pair_index * rows_pair,), (rows_pair,))
@@ -121,10 +131,7 @@
         summed = halving_scatter(partial, "contr", contr_count, contr_index)
     else:
         summed = lax.psum_scatter(partial, "contr", scatter_dimension=0, tiled=True)
-    mine_energy = lax.dynamic_slice(
-        row_energy, (pair_index * rows_pair + contr_index * rows_device,), (rows_device,)
-    )
-    update = (summed / (mine_energy[:, None] + col_energy[None, :])).astype(jnp.bfloat16)
+    update = (summed / denom).astype(jnp.bfloat16)
     return update
 
 

time: 29.8 us -> 30.5 us (1.023)
  waiting for transfers between devices: 7.93 us -> 13 us
  between operations: 3.93 us -> 0.09 us
  local copies, waits for them, and re-layouts: 1.28 us -> 0.21 us
  Pallas kernels: 1.61 us -> 2.35 us
    ppermute x5, waiting for transfers between devices: 7.93 us -> 13 us  [halving_scatter(): buf = keep + lax.ppermute(send, axis, perm)]
    pallas_call x1, Pallas kernels: 1.61 us -> 2.35 us  [irreps(): pl.pallas_call(functools.partial(_irrep_kernel, pair_count), out_shape=sh...]
    slice x1 -> x0, local copies, waits for them, and re-layouts: 0.65 us -> none  [body(): first_start = slab_start[0]]
  transfers between devices with their start and end apart: 5 -> 5, of which waited for: 5 -> 5; matrix products, arithmetic and copies ran while one was open for 4% -> 0% of each run, Pallas kernels for 0% -> 0%
where the time goes in v10:
time: 30.5 us; the launch traced here: 30.3 us
  waiting for transfers between devices  13 us (43%)
  starting transfers between devices  11.2 us (37%)
  matrix products  2.7 us (9%)
  Pallas kernels  2.35 us (8%)
  other arithmetic  0.81 us (3%)
    ppermute x5, waiting for transfers between devices, halving_scatter(): buf = keep + lax.ppermute(send, axis, perm)  13 us
    ppermute x5, starting transfers between devices, halving_scatter(): buf = keep + lax.ppermute(send, axis, perm)  11.2 us
    dot_general x1, matrix products, body(): jnp.dot(amp_masked, int_masked, preferred_element_type=jnp.float32)  2.7 us
    pallas_call x1, Pallas kernels, irreps(): pl.pallas_call(functools.partial(_irrep_kernel, pair_count), out_shape=sh...  2.35 us
    convert_element_type x1, other arithmetic, body(): update = (summed / denom).astype(jnp.bfloat16)  0.62 us
  transfers between devices with their start and end apart: 5, of which 5 were waited for; matrix products, arithmetic and copies ran while one was open for 0% of the time, Pallas kernels for 0%

profile of v10, /device:TPU:0, one launch (start us, length us, event | category | flops | bytes accessed | tf_op | source)
XLA Modules:
  0.0 30.3 jit_solution(2869927178667962505)
XLA Ops:
  0.0 2.3 %shard_map.73 = (s32[1,1024]{1,0:T(1,128)}, s32[1,1024]{1,0:T(1,128)}, s32[1,256]{1,0:T(1,128)}, f32[32,256]{1,0:T(8,128)}) custom-call(s32[2]{0:T(128)} %slab_ref.1, s32[64]{0:T(128)} %occ_v_ref.1, s32[64]{0:T(128)} %occ_v_ref.1, s32[512]{0:T(512)} %virt_v_ref.1, f32[64]{0:T(128)} %occ_e_ref.1, f32[512]{0:T(512)} %virt_e_ref.1), custom_call_target="tpu_custom_call" | custom-call | tf_op jit(solution)/shard_map/pallas_call | solution.py:102
  2.3 2.7 %fusion = f32[1024,256]{1,0:T(8,128)S(1)} fusion(bf16[1024,1024]{1,0:T(8,128)(2,1)} %param.7, s32[1024]{0:T(1024)} %bitcast.38, s32[1024]{0:T(1024)} %bitcast.37, bf16[1024,256]{1,0:T(8,128)(2,1)} %param.8, s32[256]{0:T(256)} %bitcast.39), kind=kOutput, calls=%fused_computation.1 | convolution fusion | flops 539492352 | bytes 3679232 | tf_op jit(solution)/shard_map/dot_general | solution.py:129
  5.1 0.1 constant_dynamic-slice_fusion.3
  5.2 0.5 %collective-permute-start = (f32[2,2,2,2,32,256]{5,4,2,1,0,3:T(8,128)S(1)}, f32[2,2,2,2,32,256]{5,4,2,1,0,3:T(8,128)S(1)}, u32[]{:S(2)}, u32[]{:S(2)}) collective-permute-start(f32[2,2,2,2,32,256]{5,4,2,1,0,3:T(8,128)S(1)} %bitcast.36), channel_id=1, source_target_pairs={{0,1},{1,0},{2,3},{3,2},{4,5},{5,4},{6,7},{7,6},{8,9},{9,8},{10,11... | collective-permute-start | bytes 1572872 | tf_op jit(solution)/shard_map/ppermute | solution.py:44
  5.7 1.5 %collective-permute-done = f32[2,2,2,2,32,256]{5,4,2,1,0,3:T(8,128)S(1)} collective-permute-done((f32[2,2,2,2,32,256]{5,4,2,1,0,3:T(8,128)S(1)}, f32[2,2,2,2,32,256]{5,4,2,1,0,3:T(8,128)S(1)}, u32[]{:S(2)}, u32[]{:S(2)}) %collective-permute-start) | collective-permute-done | bytes 524320 | tf_op jit(solution)/shard_map/ppermute | solution.py:44
  7.2 0.1 bitcast_add_fusion
  7.3 0.0 copy-start
  7.4 2.9 %collective-permute-start.1 = (f32[2,2,2,32,256]{4,3,2,1,0:T(8,128)S(1)}, f32[2,2,2,32,256]{4,3,2,1,0:T(8,128)S(1)}, u32[]{:S(2)}, u32[]{:S(2)}) collective-permute-start(f32[2,2,2,32,256]{4,3,2,1,0:T(8,128)S(1)} %bitcast_select_fusion), channel_id=1, source_target_pairs={{0,2},{1,5},{2,0},{3,7},{4,6},{5,1},{6,4},{7,3},{8,10},{9,13},{10,... | collective-permute-start | bytes 786440 | tf_op jit(solution)/shard_map/ppermute | solution.py:44
  10.4 4.4 %collective-permute-done.1 = f32[2,2,2,32,256]{4,3,2,1,0:T(8,128)S(1)} collective-permute-done((f32[2,2,2,32,256]{4,3,2,1,0:T(8,128)S(1)}, f32[2,2,2,32,256]{4,3,2,1,0:T(8,128)S(1)}, u32[]{:S(2)}, u32[]{:S(2)}) %collective-permute-start.1) | collective-permute-done | bytes 262176 | tf_op jit(solution)/shard_map/ppermute | solution.py:44
  14.7 0.1 fusion.6
  14.8 2.1 %collective-permute-start.2 = (f32[2,2,32,256]{3,2,1,0:T(8,128)S(1)}, f32[2,2,32,256]{3,2,1,0:T(8,128)S(1)}, u32[]{:S(2)}, u32[]{:S(2)}) collective-permute-start(f32[2,2,32,256]{3,2,1,0:T(8,128)S(1)} %dynamic-slice_bitcast_fusion), channel_id=1, source_target_pairs={{0,4},{1,3},{2,6},{3,1},{4,0},{5,7},{6,2},{7,5},{8,12},{9,11},{10,... | collective-permute-start | bytes 393224 | tf_op jit(solution)/shard_map/ppermute | solution.py:44
  16.9 2.9 %collective-permute-done.2 = f32[2,2,32,256]{3,2,1,0:T(8,128)S(1)} collective-permute-done((f32[2,2,32,256]{3,2,1,0:T(8,128)S(1)}, f32[2,2,32,256]{3,2,1,0:T(8,128)S(1)}, u32[]{:S(2)}, u32[]{:S(2)}) %collective-permute-start.2) | collective-permute-done | bytes 131104 | tf_op jit(solution)/shard_map/ppermute | solution.py:44
  19.9 2.2 %collective-permute-start.3 = (f32[2,32,256]{2,1,0:T(8,128)S(1)}, f32[2,32,256]{2,1,0:T(8,128)S(1)}, u32[]{:S(2)}, u32[]{:S(2)}) collective-permute-start(f32[2,32,256]{2,1,0:T(8,128)S(1)} %dynamic-slice_bitcast_fusion.1), channel_id=1, source_target_pairs={{0,8},{1,9},{2,10},{3,11},{4,12},{5,13},{6,14},{7,15},{8,0},{9,1},... | collective-permute-start | bytes 196616 | tf_op jit(solution)/shard_map/ppermute | solution.py:44
  22.1 2.2 %collective-permute-done.3 = f32[2,32,256]{2,1,0:T(8,128)S(1)} collective-permute-done((f32[2,32,256]{2,1,0:T(8,128)S(1)}, f32[2,32,256]{2,1,0:T(8,128)S(1)}, u32[]{:S(2)}, u32[]{:S(2)}) %collective-permute-start.3) | collective-permute-done | bytes 65568 | tf_op jit(solution)/shard_map/ppermute | solution.py:44
  24.3 3.4 %collective-permute-start.4 = (f32[32,256]{1,0:T(8,128)S(1)}, f32[32,256]{1,0:T(8,128)S(1)}, u32[]{:S(2)}, u32[]{:S(2)}) collective-permute-start(f32[32,256]{1,0:T(8,128)S(1)} %dynamic-slice_bitcast_fusion.2), channel_id=1, source_target_pairs={{0,16},{1,17},{2,18},{3,19},{4,20},{5,21},{6,22},{7,23},{8,24},{9,... | collective-permute-start | bytes 98312 | tf_op jit(solution)/shard_map/ppermute | solution.py:44
  27.8 1.9 %collective-permute-done.4 = f32[32,256]{1,0:T(8,128)S(1)} collective-permute-done((f32[32,256]{1,0:T(8,128)S(1)}, f32[32,256]{1,0:T(8,128)S(1)}, u32[]{:S(2)}, u32[]{:S(2)}) %collective-permute-start.4) | collective-permute-done | bytes 32800 | tf_op jit(solution)/shard_map/ppermute | solution.py:44
  29.7 0.0 copy-done
  29.7 0.6 %fusion.9 = bf16[32,256]{1,0:T(8,128)(2,1)} fusion(f32[32,256]{1,0:T(8,128)S(1)} %copy-done, f32[32,256]{1,0:T(8,128)S(1)} %collective-permute-done.4, f32[2,32,256]{2,1,0:T(8,128)S(1)} %bitcast_add_fusion.2, s32[]{:T(128)S(6)} %select_n.83), kind=kLoop, calls=%fused_computation.20 | loop fusion | flops 24576 | bytes 114692 | tf_op jit(solution)/shard_map/convert_element_type | solution.py:134
  (8 shorter events, 0.2 us)
Async XLA Ops:
  5.2 2.1 %collective-permute-start = (f32[2,2,2,2,32,256]{5,4,2,1,0,3:T(8,128)S(1)}, f32[2,2,2,2,32,256]{5,4,2,1,0,3:T(8,128)S(1)}, u32[]{:S(2)}, u32[]{:S(2)}) collective-permute-start(f32[2,2,2,2,32,256]{5,4,2,1,0,3:T(8,128)S(1)} %bitcast.36), channel_id=1, source_target_pairs={{0,1},{1,0},{2,3},{3,2},{4,5},{5,4},{6,7},{7,6},{8,9},{9,8},{10,11... | collective-permute-start | bytes 1572872 | tf_op jit(solution)/shard_map/ppermute | solution.py:44
  7.3 22.3 %copy-start = (f32[32,256]{1,0:T(8,128)S(1)}, f32[32,256]{1,0:T(8,128)}, u32[]{:S(2)}) copy-start(f32[32,256]{1,0:T(8,128)} %get-tuple-element.12) | copy-start | bytes 98308
  7.4 7.3 %collective-permute-start.1 = (f32[2,2,2,32,256]{4,3,2,1,0:T(8,128)S(1)}, f32[2,2,2,32,256]{4,3,2,1,0:T(8,128)S(1)}, u32[]{:S(2)}, u32[]{:S(2)}) collective-permute-start(f32[2,2,2,32,256]{4,3,2,1,0:T(8,128)S(1)} %bitcast_select_fusion), channel_id=1, source_target_pairs={{0,2},{1,5},{2,0},{3,7},{4,6},{5,1},{6,4},{7,3},{8,10},{9,13},{10,... | collective-permute-start | bytes 786440 | tf_op jit(solution)/shard_map/ppermute | solution.py:44
  14.8 5.1 %collective-permute-start.2 = (f32[2,2,32,256]{3,2,1,0:T(8,128)S(1)}, f32[2,2,32,256]{3,2,1,0:T(8,128)S(1)}, u32[]{:S(2)}, u32[]{:S(2)}) collective-permute-start(f32[2,2,32,256]{3,2,1,0:T(8,128)S(1)} %dynamic-slice_bitcast_fusion), channel_id=1, source_target_pairs={{0,4},{1,3},{2,6},{3,1},{4,0},{5,7},{6,2},{7,5},{8,12},{9,11},{10,... | collective-permute-start | bytes 393224 | tf_op jit(solution)/shard_map/ppermute | solution.py:44
  19.9 4.4 %collective-permute-start.3 = (f32[2,32,256]{2,1,0:T(8,128)S(1)}, f32[2,32,256]{2,1,0:T(8,128)S(1)}, u32[]{:S(2)}, u32[]{:S(2)}) collective-permute-start(f32[2,32,256]{2,1,0:T(8,128)S(1)} %dynamic-slice_bitcast_fusion.1), channel_id=1, source_target_pairs={{0,8},{1,9},{2,10},{3,11},{4,12},{5,13},{6,14},{7,15},{8,0},{9,1},... | collective-permute-start | bytes 196616 | tf_op jit(solution)/shard_map/ppermute | solution.py:44
  24.3 5.3 %collective-permute-start.4 = (f32[32,256]{1,0:T(8,128)S(1)}, f32[32,256]{1,0:T(8,128)S(1)}, u32[]{:S(2)}, u32[]{:S(2)}) collective-permute-start(f32[32,256]{1,0:T(8,128)S(1)} %dynamic-slice_bitcast_fusion.2), channel_id=1, source_target_pairs={{0,16},{1,17},{2,18},{3,19},{4,20},{5,21},{6,22},{7,23},{8,24},{9,... | collective-permute-start | bytes 98312 | tf_op jit(solution)/shard_map/ppermute | solution.py:44

commit v11 on v9

--- a/solution.py
+++ b/solution.py
@@ -8,8 +8,10 @@
 from jax.sharding import PartitionSpec as P
 
 
-def halving_scatter(partial, axis, count, index):
+def halving_scatter(partial, axis, count, index, second=None):
     rows, cols = partial.shape
+    if second is not None:
+        rows = 2 * rows
     block = rows // count
     bits = count.bit_length() - 1
     first = (index & 1) == 0
@@ -20,9 +22,16 @@
             seq[1], seq[2] = seq[2], seq[1]
         return seq
 
-    buf = partial.reshape((2,) * bits + (block, cols))
     left = [list(range(bits - 1, -1, -1)) for _ in range(2)]
-    for stage in range(bits):
+    stages = range(bits)
+    if second is not None:
+        got = lax.ppermute(partial, axis, [(i, i ^ 1) for i in range(count)])
+        buf = (second() + got).reshape((2,) * (bits - 1) + (block, cols))
+        left = [seq[:-1] for seq in left]
+        stages = range(1, bits)
+    else:
+        buf = partial.reshape((2,) * bits + (block, cols))
+    for stage in stages:
         split = [order(c)[stage] for c in range(2)]
         where = [left[c].index(split[c]) for c in range(2)]
         mine = [(index >> split[c]) & 1 for c in range(2)]
@@ -65,7 +74,7 @@
         virt_part = jnp.dot(virt_rows, (c_of == starts + x_of % per).astype(bf16), preferred_element_type=f32)
         return jnp.bitwise_xor(occ_part.astype(i32), virt_part.astype(i32))[0:1, :]
 
-    per_row = rows * pair_rows // occ_count
+    per_row = rows // occ_count
     row_ref[...] = spread(rows, slab_ref[0], per_row, None)
     col_ref[...] = spread(cols, slab_ref[1], cols // occ_count, None)
     base = lax.axis_index("contr") * occ_local
@@ -115,11 +124,25 @@
     kc_irrep = kc_k.reshape(-1)
     int_masked = jnp.where(kc_irrep[:, None] == col_k.reshape(-1)[None, :], whole_int, zero)
     row_irrep_pair = lax.dynamic_slice(row_k.reshape(-1), (pair_index * rows_pair,), (rows_pair,))
-    amp_masked = jnp.where(row_irrep_pair[:, None] == kc_irrep[None, :], amplitudes, zero)
-    partial = jnp.dot(amp_masked, int_masked, preferred_element_type=jnp.float32)
-    if contr_count & (contr_count - 1) == 0 and rows_pair % contr_count == 0:
-        summed = halving_scatter(partial, "contr", contr_count, contr_index)
+    def product(amp, irrep):
+        masked = jnp.where(irrep[:, None] == kc_irrep[None, :], amp, zero)
+        return jnp.dot(masked, int_masked, preferred_element_type=jnp.float32)
+
+    block = rows_pair // contr_count
+    if contr_count & (contr_count - 1) == 0 and rows_pair % contr_count == 0 and contr_count >= 2:
+        amp4 = amplitudes.reshape(rows_pair // (2 * block), 2, block, kc_local)
+        irrep4 = row_irrep_pair.reshape(rows_pair // (2 * block), 2, block)
+        core = contr_index % 2
+
+        def half(parity):
+            amp = lax.dynamic_index_in_dim(amp4, parity, axis=1, keepdims=False)
+            irrep = lax.dynamic_index_in_dim(irrep4, parity, axis=1, keepdims=False)
+            return product(amp.reshape(rows_pair // 2, kc_local), irrep.reshape(-1))
+
+        summed = halving_scatter(half(1 - core), "contr", contr_count, contr_index,
+                                 lambda: lax.optimization_barrier(half(core)))
     else:
+        partial = product(amplitudes, row_irrep_pair)
         summed = lax.psum_scatter(partial, "contr", scatter_dimension=0, tiled=True)
     mine_energy = lax.dynamic_slice(
         row_energy, (pair_index * rows_pair + contr_index * rows_device,), (rows_device,)

time: 29.8 us -> 31.7 us (1.064)
  local copies, waits for them, and re-layouts: 1.28 us -> 3.88 us
  matrix products: 2.71 us -> 1.27 us
  other arithmetic: 1.03 us -> 2.35 us
  waiting for transfers between devices: 7.93 us -> 7.02 us
    dynamic_slice x2, local copies, waits for them, and re-layouts: 0.11 us -> 1.88 us  [the longest x1 1.82 us: half(): amp = lax.dynamic_index_in_dim(amp4, parity, axis=1, keepdims=False)]
    ppermute x5 -> x4, waiting for transfers between devices: 7.93 us -> 6.21 us  [halving_scatter(): buf = keep + lax.ppermute(send, axis, perm)]
    dot_general x1 -> x2, matrix products: 2.71 us -> 1.27 us  [product(): return jnp.dot(masked, int_masked, preferred_element_type=jnp.float32)]
    pallas_call x0 -> x1, other arithmetic: none -> 1.33 us  [irreps(): pl.pallas_call(functools.partial(_irrep_kernel, pair_count), out_shape=sh...]
    ppermute x0 -> x1, waiting for transfers between devices: none -> 0.81 us  [halving_scatter(): got = lax.ppermute(partial, axis, [(i, i ^ 1) for i in range(count)])]
    pallas_call x0 -> x1, local copies, waits for them, and re-layouts: none -> 0.54 us  [irreps(): pl.pallas_call(functools.partial(_irrep_kernel, pair_count), out_shape=sh...]
    ppermute x0 -> x1, starting transfers between devices: none -> 0.52 us  [halving_scatter(): got = lax.ppermute(partial, axis, [(i, i ^ 1) for i in range(count)])]
    ppermute x5 -> x4, starting transfers between devices: 11.1 us -> 10.6 us  [halving_scatter(): buf = keep + lax.ppermute(send, axis, perm)]
  transfers between devices with their start and end apart: 5 -> 5, of which waited for: 5 -> 4; matrix products, arithmetic and copies ran while one was open for 4% -> 6% of each run, Pallas kernels for 0% -> 0%
where the time goes in v11:
time: 31.7 us; the launch traced here: 31.5 us
  starting transfers between devices  11.2 us (35%)
  waiting for transfers between devices  7.02 us (22%)
  between operations  4.18 us (13%)
  local copies, waits for them, and re-layouts  3.88 us (12%)
  other arithmetic  2.35 us (7%)
  Pallas kernels  1.61 us (5%)
  matrix products  1.27 us (4%)
    ppermute x4, starting transfers between devices, halving_scatter(): buf = keep + lax.ppermute(send, axis, perm)  10.6 us
    ppermute x4, waiting for transfers between devices, halving_scatter(): buf = keep + lax.ppermute(send, axis, perm)  6.21 us
    dynamic_slice x1, local copies, waits for them, and re-layouts, half(): amp = lax.dynamic_index_in_dim(amp4, parity, axis=1, keepdims=False)  1.82 us
    pallas_call x1, Pallas kernels, irreps(): pl.pallas_call(functools.partial(_irrep_kernel, pair_count), out_shape=sh...  1.61 us
    pallas_call x1, other arithmetic, irreps(): pl.pallas_call(functools.partial(_irrep_kernel, pair_count), out_shape=sh...  1.33 us
    dot_general x2, matrix products, product(): return jnp.dot(masked, int_masked, preferred_element_type=jnp.float32)  1.27 us
    ppermute x1, waiting for transfers between devices, halving_scatter(): got = lax.ppermute(partial, axis, [(i, i ^ 1) for i in range(count)])  0.81 us
    convert_element_type x1, other arithmetic, body(): (summed / (mine_energy[:, None] + col_energy[None, :])).astype(jnp.bfloat16)  0.69 us
  transfers between devices with their start and end apart: 5, of which 4 were waited for; matrix products, arithmetic and copies ran while one was open for 6% of the time, Pallas kernels for 0%

profile of v11, /device:TPU:0, one launch (start us, length us, event | category | flops | bytes accessed | tf_op | source)
XLA Modules:
  0.0 31.5 jit_solution(2832291713143907187)
XLA Ops:
  0.0 1.6 %shard_map.73 = (s32[1,1024]{1,0:T(1,128)}, s32[1,1024]{1,0:T(1,128)}, s32[1,256]{1,0:T(1,128)}) custom-call(s32[2]{0:T(128)} %slab_ref.1, s32[64]{0:T(128)} %occ_v_ref.1, s32[64]{0:T(128)} %occ_v_ref.1, s32[512]{0:T(512)} %virt_v_ref.1), custom_call_target="tpu_custom_call" | custom-call | tf_op jit(solution)/shard_map/pallas_call | solution.py:89
  1.6 0.5 %broadcast.20 = s32[]{:T(128)} broadcast(s32[]{:T(128)} %constant.75.clone.1), dimensions={} | broadcast | bytes 8 | tf_op jit(solution)/shard_map/pallas_call | solution.py:89
  2.1 1.3 %reduce.11 = s32[1024]{0:T(1024)S(1)} reduce(s32[1,1024]{1,0:T(1,128)} %get-tuple-element.8, s32[]{:T(128)} %broadcast.20), dimensions={0}, to_apply=%get-tuple-element.8.reduce_sub_computation.3 | reduce | bytes 8196 | tf_op jit(solution)/shard_map/pallas_call | solution.py:89
  3.5 0.1 reshape.46
  3.6 0.0 copy-start.2
  3.6 0.0 copy-start.3
  3.6 0.0 copy-start.5
  3.6 1.8 %constant_dynamic-slice_fusion.4 = (bf16[16,1,32,1024]{3,2,1,0:T(8,128)(2,1)S(1)}, bf16[16,1,32,1024]{3,2,1,0:T(8,128)(2,1)S(1)}) fusion(bf16[16,2,32,1024]{3,2,1,0:T(8,128)(2,1)} %bitcast.36, s32[]{:T(128)S(6)} %select_n.93, s32[]{:T(128)S(6)} %select_n.90), kind=kLoop, calls=%fused_computation.30 | loop fusion | bytes 4194312 | tf_op jit(solution)/shard_map/jit(dynamic_index_in_dim)/dynamic_slice | solution.py:138
  5.4 0.1 dynamic-slice_reduce_fusion
  5.5 0.1 eq.60
  5.6 0.0 copy-done.2
  5.6 0.0 copy-done.3
  5.6 0.0 copy-done.5
  5.6 0.6 %fusion.1 = f32[512,256]{1,0:T(8,128)S(1)} fusion(bf16[512,1024]{1,0:T(8,128)(2,1)S(1)} %bitcast.38, s32[1024]{0:T(1024)S(1)} %bitcast.39, s32[512]{0:T(512)S(1)} %eq.60, bf16[1024,256]{1,0:T(8,128)(2,1)S(1)} %copy-done.2, s32[256]{0:T(256)S(1)} %bitcast.41), kind=kOutput, calls=%fused_computation.3 | convolution fusion | flops 270008320 | bytes 2104320 | tf_op jit(solution)/shard_map/dot_general | solution.py:129
  6.2 0.5 %collective-permute-start = (f32[512,256]{1,0:T(8,128)S(1)}, f32[512,256]{1,0:T(8,128)S(1)}, u32[]{:S(2)}, u32[]{:S(2)}) collective-permute-start(f32[512,256]{1,0:T(8,128)S(1)} %fusion.1), channel_id=1, source_target_pairs={{0,1},{1,0},{2,3},{3,2},{4,5},{5,4},{6,7},{7,6},{8,9},{9,8},{10,11... | collective-permute-start | bytes 1572872 | tf_op jit(solution)/shard_map/ppermute | solution.py:28
  6.7 0.1 eq.51
  6.8 0.6 %fusion = f32[512,256]{1,0:T(8,128)S(1)} fusion(bf16[512,1024]{1,0:T(8,128)(2,1)S(1)} %bitcast.37, s32[1024]{0:T(1024)S(1)} %bitcast.40, s32[512]{0:T(512)S(1)} %eq.51, bf16[1024,256]{1,0:T(8,128)(2,1)S(1)} %copy-done.2, s32[256]{0:T(256)S(1)} %bitcast.42), kind=kOutput, calls=%fused_computation.2 | convolution fusion | flops 270008320 | bytes 2104320 | tf_op jit(solution)/shard_map/dot_general | solution.py:129
  7.5 0.8 %collective-permute-done = f32[512,256]{1,0:T(8,128)S(1)} collective-permute-done((f32[512,256]{1,0:T(8,128)S(1)}, f32[512,256]{1,0:T(8,128)S(1)}, u32[]{:S(2)}, u32[]{:S(2)}) %collective-permute-start) | collective-permute-done | bytes 524320 | tf_op jit(solution)/shard_map/ppermute | solution.py:28
  8.3 0.1 add.97
  8.4 0.0 copy-start
  8.4 0.0 copy-start.4
  8.4 0.0 copy-start.1
  8.5 2.9 %collective-permute-start.1 = (f32[2,2,2,32,256]{4,3,1,0,2:T(8,128)S(1)}, f32[2,2,2,32,256]{4,3,1,0,2:T(8,128)S(1)}, u32[]{:S(2)}, u32[]{:S(2)}) collective-permute-start(f32[2,2,2,32,256]{4,3,1,0,2:T(8,128)S(1)} %bitcast_select_fusion), channel_id=1, source_target_pairs={{0,2},{1,5},{2,0},{3,7},{4,6},{5,1},{6,4},{7,3},{8,10},{9,13},{10,... | collective-permute-start | bytes 786440 | tf_op jit(solution)/shard_map/ppermute | solution.py:53
  11.5 4.4 %collective-permute-done.1 = f32[2,2,2,32,256]{4,3,1,0,2:T(8,128)S(1)} collective-permute-done((f32[2,2,2,32,256]{4,3,1,0,2:T(8,128)S(1)}, f32[2,2,2,32,256]{4,3,1,0,2:T(8,128)S(1)}, u32[]{:S(2)}, u32[]{:S(2)}) %collective-permute-start.1) | collective-permute-done | bytes 262176 | tf_op jit(solution)/shard_map/ppermute | solution.py:53
  15.8 0.1 fusion.8
  15.9 2.1 %collective-permute-start.2 = (f32[2,2,32,256]{3,2,1,0:T(8,128)S(1)}, f32[2,2,32,256]{3,2,1,0:T(8,128)S(1)}, u32[]{:S(2)}, u32[]{:S(2)}) collective-permute-start(f32[2,2,32,256]{3,2,1,0:T(8,128)S(1)} %dynamic-slice_bitcast_fusion), channel_id=1, source_target_pairs={{0,4},{1,3},{2,6},{3,1},{4,0},{5,7},{6,2},{7,5},{8,12},{9,11},{10,... | collective-permute-start | bytes 393224 | tf_op jit(solution)/shard_map/ppermute | solution.py:53
  18.0 0.0 copy-done
  18.0 0.7 %fusion.13 = (s32[1]{0:T(128)}, s32[1]{0:T(128)}) fusion(s32[2]{0:T(128)S(1)} %copy-done), kind=kLoop, calls=%fused_computation.34 | loop fusion | bytes 16 | tf_op jit(solution)/shard_map/slice | solution.py:110
  20.6 0.0 copy-done.4
  20.6 0.1 dynamic_slice.73
  20.7 0.3 collective-permute-done.2
  21.0 2.1 %collective-permute-start.3 = (f32[2,32,256]{2,1,0:T(8,128)S(1)}, f32[2,32,256]{2,1,0:T(8,128)S(1)}, u32[]{:S(2)}, u32[]{:S(2)}) collective-permute-start(f32[2,32,256]{2,1,0:T(8,128)S(1)} %dynamic-slice_bitcast_fusion.1), channel_id=1, source_target_pairs={{0,8},{1,9},{2,10},{3,11},{4,12},{5,13},{6,14},{7,15},{8,0},{9,1},... | collective-permute-start | bytes 196616 | tf_op jit(solution)/shard_map/ppermute | solution.py:53
  23.2 0.0 copy-done.1
  23.2 0.1 broadcast_subtract_fusion.1
  25.3 0.1 dynamic_slice.75
  25.4 0.0 collective-permute-done.3
  25.4 3.5 %collective-permute-start.4 = (f32[32,256]{1,0:T(8,128)S(1)}, f32[32,256]{1,0:T(8,128)S(1)}, u32[]{:S(2)}, u32[]{:S(2)}) collective-permute-start(f32[32,256]{1,0:T(8,128)S(1)} %dynamic-slice_bitcast_fusion.2), channel_id=1, source_target_pairs={{0,16},{1,17},{2,18},{3,19},{4,20},{5,21},{6,22},{7,23},{8,24},{9,... | collective-permute-start | bytes 98312 | tf_op jit(solution)/shard_map/ppermute | solution.py:53
  28.9 0.1 broadcast_subtract_fusion
  29.0 0.1 sub.64
  29.0 0.1 sub.68
  29.1 0.1 dynamic_slice.74
  29.2 1.6 %collective-permute-done.4 = f32[32,256]{1,0:T(8,128)S(1)} collective-permute-done((f32[32,256]{1,0:T(8,128)S(1)}, f32[32,256]{1,0:T(8,128)S(1)}, u32[]{:S(2)}, u32[]{:S(2)}) %collective-permute-start.4) | collective-permute-done | bytes 32800 | tf_op jit(solution)/shard_map/ppermute | solution.py:53
  30.8 0.7 %fusion.10 = bf16[32,256]{1,0:T(8,128)(2,1)} fusion(f32[32,256]{1,0:T(8,128)S(1)} %collective-permute-done.4, f32[2,32,256]{2,1,0:T(8,128)S(1)} %bitcast_add_fusion.1, s32[]{:T(128)S(6)} %select_n.106, f32[256]{0:T(256)S(1)} %sub.68, f32[32]{0:T(128)S(1)} %dynamic_slice.74), kind=kLoop, calls=%fused_computation.20 | loop fusion | flops 32768 | bytes 83076 | tf_op jit(solution)/shard_map/convert_element_type | solution.py:150
  (8 shorter events, 0.2 us)
Async XLA Ops:
  3.6 2.0 %copy-start.2 = (bf16[1024,256]{1,0:T(8,128)(2,1)S(1)}, bf16[1024,256]{1,0:T(8,128)(2,1)}, u32[]{:S(2)}) copy-start(bf16[1024,256]{1,0:T(8,128)(2,1)} %param.8) | copy-start | bytes 1572868
  3.6 2.0 %copy-start.3 = (s32[1,1024]{1,0:T(1,128)S(1)}, s32[1,1024]{1,0:T(1,128)}, u32[]{:S(2)}) copy-start(s32[1,1024]{1,0:T(1,128)} %get-tuple-element.9) | copy-start | bytes 12292
  3.6 2.0 %copy-start.5 = (s32[1,256]{1,0:T(1,128)S(1)}, s32[1,256]{1,0:T(1,128)}, u32[]{:S(2)}) copy-start(s32[1,256]{1,0:T(1,128)} %get-tuple-element.10) | copy-start | bytes 3076
  6.2 2.1 %collective-permute-start = (f32[512,256]{1,0:T(8,128)S(1)}, f32[512,256]{1,0:T(8,128)S(1)}, u32[]{:S(2)}, u32[]{:S(2)}) collective-permute-start(f32[512,256]{1,0:T(8,128)S(1)} %fusion.1), channel_id=1, source_target_pairs={{0,1},{1,0},{2,3},{3,2},{4,5},{5,4},{6,7},{7,6},{8,9},{9,8},{10,11... | collective-permute-start | bytes 1572872 | tf_op jit(solution)/shard_map/ppermute | solution.py:28
  8.4 9.7 %copy-start = (s32[2]{0:T(128)S(1)}, s32[2]{0:T(128)}, u32[]{:S(2)}) copy-start(s32[2]{0:T(128)} %slab_ref.1) | copy-start | bytes 28
  8.4 12.2 %copy-start.4 = (f32[512]{0:T(512)S(1)}, f32[512]{0:T(512)}, u32[]{:S(2)}) copy-start(f32[512]{0:T(512)} %param.12) | copy-start | bytes 6148
  8.4 14.7 %copy-start.1 = (f32[64]{0:T(128)S(1)}, f32[64]{0:T(128)}, u32[]{:S(2)}) copy-start(f32[64]{0:T(128)} %param.11) | copy-start | bytes 772
  8.5 7.3 %collective-permute-start.1 = (f32[2,2,2,32,256]{4,3,1,0,2:T(8,128)S(1)}, f32[2,2,2,32,256]{4,3,1,0,2:T(8,128)S(1)}, u32[]{:S(2)}, u32[]{:S(2)}) collective-permute-start(f32[2,2,2,32,256]{4,3,1,0,2:T(8,128)S(1)} %bitcast_select_fusion), channel_id=1, source_target_pairs={{0,2},{1,5},{2,0},{3,7},{4,6},{5,1},{6,4},{7,3},{8,10},{9,13},{10,... | collective-permute-start | bytes 786440 | tf_op jit(solution)/shard_map/ppermute | solution.py:53
  15.9 5.1 %collective-permute-start.2 = (f32[2,2,32,256]{3,2,1,0:T(8,128)S(1)}, f32[2,2,32,256]{3,2,1,0:T(8,128)S(1)}, u32[]{:S(2)}, u32[]{:S(2)}) collective-permute-start(f32[2,2,32,256]{3,2,1,0:T(8,128)S(1)} %dynamic-slice_bitcast_fusion), channel_id=1, source_target_pairs={{0,4},{1,3},{2,6},{3,1},{4,0},{5,7},{6,2},{7,5},{8,12},{9,11},{10,... | collective-permute-start | bytes 393224 | tf_op jit(solution)/shard_map/ppermute | solution.py:53
  21.0 4.4 %collective-permute-start.3 = (f32[2,32,256]{2,1,0:T(8,128)S(1)}, f32[2,32,256]{2,1,0:T(8,128)S(1)}, u32[]{:S(2)}, u32[]{:S(2)}) collective-permute-start(f32[2,32,256]{2,1,0:T(8,128)S(1)} %dynamic-slice_bitcast_fusion.1), channel_id=1, source_target_pairs={{0,8},{1,9},{2,10},{3,11},{4,12},{5,13},{6,14},{7,15},{8,0},{9,1},... | collective-permute-start | bytes 196616 | tf_op jit(solution)/shard_map/ppermute | solution.py:53
  25.4 5.3 %collective-permute-start.4 = (f32[32,256]{1,0:T(8,128)S(1)}, f32[32,256]{1,0:T(8,128)S(1)}, u32[]{:S(2)}, u32[]{:S(2)}) collective-permute-start(f32[32,256]{1,0:T(8,128)S(1)} %dynamic-slice_bitcast_fusion.2), channel_id=1, source_target_pairs={{0,16},{1,17},{2,18},{3,19},{4,20},{5,21},{6,22},{7,23},{8,24},{9,... | collective-permute-start | bytes 98312 | tf_op jit(solution)/shard_map/ppermute | solution.py:53

commit v12 on v11

--- a/solution.py
+++ b/solution.py
@@ -54,10 +54,9 @@
     return buf.reshape(block, cols)
 
 
-def _irrep_kernel(pair_rows, slab_ref, occ_s_ref, occ_v_ref, virt_v_ref, row_ref, kc_ref, col_ref):
+def _irrep_kernel(shape, slab_ref, occ_s_ref, occ_v_ref, virt_v_ref, row_ref, kc_ref, col_ref):
     virt_count = virt_v_ref.shape[0]
     occ_count = occ_v_ref.shape[0]
-    rows = row_ref.shape[1]
     kc_local = kc_ref.shape[1]
     cols = col_ref.shape[1]
     occ_local = kc_local // virt_count
@@ -65,29 +64,34 @@
     occ_rows = jnp.broadcast_to(occ_v_ref[...].reshape(1, occ_count), (8, occ_count)).astype(bf16)
     virt_rows = jnp.broadcast_to(virt_v_ref[...].reshape(1, virt_count), (8, virt_count)).astype(bf16)
 
-    def spread(count, starts, per, dst):
-        x_of = lax.broadcasted_iota(i32, (occ_count, count), 1)
+    def spread(count, starts, per, where=lambda x: x):
+        x_of = where(lax.broadcasted_iota(i32, (occ_count, count), 1))
         j_of = lax.broadcasted_iota(i32, (occ_count, count), 0)
         occ_part = jnp.dot(occ_rows, (x_of // per == j_of).astype(bf16), preferred_element_type=f32)
-        x_of = lax.broadcasted_iota(i32, (virt_count, count), 1)
+        x_of = where(lax.broadcasted_iota(i32, (virt_count, count), 1))
         c_of = lax.broadcasted_iota(i32, (virt_count, count), 0)
         virt_part = jnp.dot(virt_rows, (c_of == starts + x_of % per).astype(bf16), preferred_element_type=f32)
         return jnp.bitwise_xor(occ_part.astype(i32), virt_part.astype(i32))[0:1, :]
 
-    per_row = rows // occ_count
-    row_ref[...] = spread(rows, slab_ref[0], per_row, None)
-    col_ref[...] = spread(cols, slab_ref[1], cols // occ_count, None)
+    pair_count, rows_pair, block = shape
+    per_row = rows_pair * pair_count // occ_count
+    first = lax.axis_index("pair") * rows_pair
+    for parity in range(2):
+        row_ref[parity:parity + 1, :] = spread(
+            rows_pair // 2, slab_ref[0], per_row,
+            lambda x: first + ((x // block) * 2 + parity) * block + x % block)
+    col_ref[...] = spread(cols, slab_ref[1], cols // occ_count)
     base = lax.axis_index("contr") * occ_local
     parts = [jnp.bitwise_xor(virt_v_ref[...].reshape(1, virt_count), occ_s_ref[base + k]) for k in range(occ_local)]
     kc_ref[...] = jnp.concatenate(parts, axis=1) if occ_local > 1 else parts[0]
 
 
-def irreps(pair_count, slab_start, occ_irrep, virt_irrep, rows, kc_local, cols):
+def irreps(shape, slab_start, occ_irrep, virt_irrep, kc_local, cols):
     smem = pl.BlockSpec(memory_space=pltpu.SMEM)
     vmem = pl.BlockSpec(memory_space=pltpu.VMEM)
-    shapes = [jax.ShapeDtypeStruct((1, n), jnp.int32) for n in (rows, kc_local, cols)]
+    shapes = [jax.ShapeDtypeStruct(n, jnp.int32) for n in ((2, shape[1] // 2), (1, kc_local), (1, cols))]
     return pl.pallas_call(
-        functools.partial(_irrep_kernel, pair_count),
+        functools.partial(_irrep_kernel, shape),
         out_shape=shapes,
         in_specs=[smem, smem, vmem, vmem],
         out_specs=[vmem, vmem, vmem],
@@ -109,40 +113,35 @@
     slab_second = cols_pair * pair_count // occ_irrep.shape[0]
     first_start = slab_start[0]
     second_start = slab_start[1]
-    a_irrep = lax.dynamic_slice(virt_irrep, (first_start,), (slab_first,))
-    b_irrep = lax.dynamic_slice(virt_irrep, (second_start,), (slab_second,))
     a_energy = lax.dynamic_slice(virt_energy, (first_start,), (slab_first,))
     b_energy = lax.dynamic_slice(virt_energy, (second_start,), (slab_second,))
-    row_irrep = jnp.bitwise_xor(occ_irrep[:, None], a_irrep[None, :]).reshape(-1)
-    col_irrep = jnp.bitwise_xor(occ_irrep[:, None], b_irrep[None, :]).reshape(-1)
     row_energy = (occ_energy[:, None] - a_energy[None, :]).reshape(-1)
     col_energy = (occ_energy[:, None] - b_energy[None, :]).reshape(-1)
     zero = jnp.zeros((), jnp.bfloat16)
     whole_int = lax.all_gather(integrals, "pair", axis=1, tiled=True)
-    row_k, kc_k, col_k = irreps(pair_count, slab_start, occ_irrep, virt_irrep,
-                                rows_pair * pair_count, kc_local, cols_pair * pair_count)
+    block = rows_pair // contr_count
+    split = contr_count & (contr_count - 1) == 0 and rows_pair % (2 * contr_count) == 0
+    row_k, kc_k, col_k = irreps((pair_count, rows_pair, block if split else rows_pair // 2),
+                                slab_start, occ_irrep, virt_irrep, kc_local, cols_pair * pair_count)
     kc_irrep = kc_k.reshape(-1)
     int_masked = jnp.where(kc_irrep[:, None] == col_k.reshape(-1)[None, :], whole_int, zero)
-    row_irrep_pair = lax.dynamic_slice(row_k.reshape(-1), (pair_index * rows_pair,), (rows_pair,))
+
     def product(amp, irrep):
         masked = jnp.where(irrep[:, None] == kc_irrep[None, :], amp, zero)
         return jnp.dot(masked, int_masked, preferred_element_type=jnp.float32)
 
-    block = rows_pair // contr_count
-    if contr_count & (contr_count - 1) == 0 and rows_pair % contr_count == 0 and contr_count >= 2:
+    if split:
         amp4 = amplitudes.reshape(rows_pair // (2 * block), 2, block, kc_local)
-        irrep4 = row_irrep_pair.reshape(rows_pair // (2 * block), 2, block)
         core = contr_index % 2
 
         def half(parity):
-            amp = lax.dynamic_index_in_dim(amp4, parity, axis=1, keepdims=False)
-            irrep = lax.dynamic_index_in_dim(irrep4, parity, axis=1, keepdims=False)
-            return product(amp.reshape(rows_pair // 2, kc_local), irrep.reshape(-1))
+            return product(amp4[:, parity].reshape(rows_pair // 2, kc_local), row_k[parity])
 
-        summed = halving_scatter(half(1 - core), "contr", contr_count, contr_index,
-                                 lambda: lax.optimization_barrier(half(core)))
+        sent = lax.cond(core == 0, lambda: half(1), lambda: half(0))
+        summed = halving_scatter(sent, "contr", contr_count, contr_index, lambda: lax.optimization_barrier(
+            lax.cond(core == 0, lambda: half(0), lambda: half(1))))
     else:
-        partial = product(amplitudes, row_irrep_pair)
+        partial = product(amplitudes, row_k.reshape(-1))
         summed = lax.psum_scatter(partial, "contr", scatter_dimension=0, tiled=True)
     mine_energy = lax.dynamic_slice(
         row_energy, (pair_index * rows_pair + contr_index * rows_device,), (rows_device,)

time: 31.7 us -> 29.8 us (0.940)
  starting transfers between devices: 11.2 us -> 10.5 us
  waiting for transfers between devices: 7.02 us -> 6.4 us
    slice x0 -> x4, local copies, waits for them, and re-layouts: none -> 2.65 us  [the longest x2 2.64 us: half(): amp4[:, parity].reshape(rows_pair // 2, kc_local)]
    dynamic_slice x4 -> x2, local copies, waits for them, and re-layouts: 1.97 us -> 0.04 us  [the longest x1 0.03 us: halving_scatter(): keep = lax.dynamic_index_in_dim(buf, bit, axis=where[0], keepdims=False)]
    pallas_call x1 -> x0, other arithmetic: 1.33 us -> none  [irreps(): pl.pallas_call(functools.partial(_irrep_kernel, pair_count), out_shape=sh...]
    select_n x0 -> x1, other arithmetic: none -> 1.24 us  [body(): jnp.where(kc_irrep[:, None] == col_k.reshape(-1)[None, :], whole_int, zero)]
    ppermute x1, waiting for transfers between devices: 0.81 us -> 0.01 us  [halving_scatter(): got = lax.ppermute(partial, axis, [(i, i ^ 1) for i in range(count)])]
    ppermute x4, starting transfers between devices: 10.6 us -> 9.96 us  [halving_scatter(): buf = keep + lax.ppermute(send, axis, perm)]
    pallas_call x1 -> x0, local copies, waits for them, and re-layouts: 0.54 us -> none  [irreps(): pl.pallas_call(functools.partial(_irrep_kernel, pair_count), out_shape=sh...]
  transfers between devices with their start and end apart: 5 -> 5, of which waited for: 4 -> 4; matrix products, arithmetic and copies ran while one was open for 6% -> 10% of each run, Pallas kernels for 0% -> 0%
where the time goes in v12:
time: 29.8 us; the launch traced here: 29.5 us
  starting transfers between devices  10.5 us (35%)
  waiting for transfers between devices  6.4 us (21%)
  between operations  4.01 us (13%)
  local copies, waits for them, and re-layouts  3.75 us (13%)
  other arithmetic  2.27 us (8%)
  Pallas kernels  1.62 us (5%)
  matrix products  0.98 us (3%)
    ppermute x4, starting transfers between devices, halving_scatter(): buf = keep + lax.ppermute(send, axis, perm)  9.96 us
    ppermute x4, waiting for transfers between devices, halving_scatter(): buf = keep + lax.ppermute(send, axis, perm)  6.39 us
    slice x2, local copies, waits for them, and re-layouts, half(): amp4[:, parity].reshape(rows_pair // 2, kc_local)  2.64 us
    pallas_call x1, Pallas kernels, irreps(): pl.pallas_call(functools.partial(_irrep_kernel, shape), out_shape=shapes,...  1.62 us
    select_n x1, other arithmetic, body(): jnp.where(kc_irrep[:, None] == col_k.reshape(-1)[None, :], whole_int, zero)  1.24 us
    dot_general x2, matrix products, product(): return jnp.dot(masked, int_masked, preferred_element_type=jnp.float32)  0.98 us
    convert_element_type x1, other arithmetic, body(): (summed / (mine_energy[:, None] + col_energy[None, :])).astype(jnp.bfloat16)  0.69 us
    slice x1, local copies, waits for them, and re-layouts, body(): first_start = slab_start[0]  0.6 us
  transfers between devices with their start and end apart: 5, of which 4 were waited for; matrix products, arithmetic and copies ran while one was open for 10% of the time, Pallas kernels for 0%

profile of v12, /device:TPU:0, one launch (start us, length us, event | category | flops | bytes accessed | tf_op | source)
XLA Modules:
  0.0 29.5 jit_solution(15154228922043080724)
XLA Ops:
  0.0 1.6 %shard_map.73 = (s32[2,512]{1,0:T(2,128)S(1)}, s32[1,1024]{1,0:T(1,128)S(1)}, s32[1,256]{1,0:T(1,128)}) custom-call(s32[2]{0:T(128)} %slab_ref.1, s32[64]{0:T(128)} %occ_v_ref.1, s32[64]{0:T(128)} %occ_v_ref.1, s32[512]{0:T(512)} %virt_v_ref.1), custom_call_target="tpu_custom_call" | custom-call | tf_op jit(solution)/shard_map/pallas_call | solution.py:93
  1.6 1.2 %compare_select_fusion.8 = bf16[1024,256]{1,0:T(8,128)(2,1)S(1)} fusion(bf16[1024,256]{1,0:T(8,128)(2,1)} %param.12, s32[256]{0:T(256)} %bitcast.69, s32[1024]{0:T(1024)S(1)} %bitcast.60), kind=kLoop, calls=%fused_computation.24 | loop fusion | flops 524288 | bytes 1053696 | tf_op jit(solution)/shard_map/jit(_where)/select_n | solution.py:127
  2.9 1.9 %conditional.3 = (f32[512,256]{1,0:T(8,128)S(1)}) conditional(s32[]{:T(128)} %convert_element_type.7, (s32[2,512]{1,0:T(2,128)S(1)}, s32[1,1024]{1,0:T(1,128)S(1)}, bf16[16,2,32,1024]{3,2,1,0:T(8,128)(2,1)}, bf16[1024,256]{1,0:T(8,128)(2,1)S(1)}) %tuple.24, (s32[2,512]{1,0:T(2,128)S(1)}, s32[1,1024]{1,0:T(1,128)S(1)}, ...), branch_computations={%region_2.3_spmd, %region_3.4_spmd} | conditional | flops 269484032 | bytes 4204552 | solution.py:140
  2.9 1.3 %slice.27 = bf16[16,1,32,1024]{3,2,1,0:T(8,128)(2,1)S(1)} slice(bf16[16,2,32,1024]{3,2,1,0:T(8,128)(2,1)} %get-tuple-element.57), slice={[0:16], [1:2], [0:32], [0:1024]} | slice | bytes 2097152 | tf_op jit(solution)/shard_map/cond/branch_1_fun/slice | solution.py:138
  4.2 0.5 %fusion.15 = f32[512,256]{1,0:T(8,128)S(1)} fusion(bf16[1024,256]{1,0:T(8,128)(2,1)S(1)} %get-tuple-element.58, bf16[512,1024]{1,0:T(8,128)(2,1)S(1)} %bitcast.56, s32[1024]{0:T(1024)S(1)} %bitcast.62, s32[512]{0:T(512)S(1)} %bitcast.66), kind=kOutput, calls=%fused_computation.19 | convolution fusion | flops 269484032 | bytes 2103296 | tf_op jit(solution)/shard_map/cond/branch_1_fun/dot_general | solution.py:131
  4.7 0.5 %collective-permute-start = (f32[512,256]{1,0:T(8,128)S(1)}, f32[512,256]{1,0:T(8,128)S(1)}, u32[]{:S(2)}, u32[]{:S(2)}) collective-permute-start(f32[512,256]{1,0:T(8,128)S(1)} %get-tuple-element.70), channel_id=1, source_target_pairs={{0,1},{1,0},{2,3},{3,2},{4,5},{5,4},{6,7},{7,6},{8,9},{9,8},{10,11... | collective-permute-start | bytes 1572872 | tf_op jit(solution)/shard_map/ppermute | solution.py:28
  5.2 1.8 %conditional.2 = (f32[512,256]{1,0:T(8,128)S(1)}) conditional(s32[]{:T(128)} %convert_element_type.7, (s32[2,512]{1,0:T(2,128)S(1)}, s32[1,1024]{1,0:T(1,128)S(1)}, bf16[16,2,32,1024]{3,2,1,0:T(8,128)(2,1)}, bf16[1024,256]{1,0:T(8,128)(2,1)S(1)}) %tuple.26, (s32[2,512]{1,0:T(2,128)S(1)}, s32[1,1024]{1,0:T(1,128)S(1)}, ...), branch_computations={%region_0.1_spmd, %region_1.2_spmd} | conditional | flops 269484032 | bytes 4204552 | solution.py:142
  5.2 1.3 %slice.23 = bf16[16,1,32,1024]{3,2,1,0:T(8,128)(2,1)S(1)} slice(bf16[16,2,32,1024]{3,2,1,0:T(8,128)(2,1)} %get-tuple-element.49), slice={[0:16], [0:1], [0:32], [0:1024]} | slice | bytes 2097152 | tf_op jit(solution)/shard_map/cond/branch_1_fun/slice | solution.py:138
  6.6 0.5 %fusion.5 = f32[512,256]{1,0:T(8,128)S(1)} fusion(bf16[1024,256]{1,0:T(8,128)(2,1)S(1)} %get-tuple-element.50, bf16[512,1024]{1,0:T(8,128)(2,1)S(1)} %bitcast.58, s32[1024]{0:T(1024)S(1)} %bitcast.64, s32[512]{0:T(512)S(1)} %bitcast.68), kind=kOutput, calls=%fused_computation.7 | convolution fusion | flops 269484032 | bytes 2103296 | tf_op jit(solution)/shard_map/cond/branch_1_fun/dot_general | solution.py:131
  7.1 0.0 copy-start
  7.1 0.0 copy-start.2
  7.1 0.0 copy-start.1
  7.1 0.0 collective-permute-done
  7.1 0.1 add.83
  7.3 2.6 %collective-permute-start.1 = (f32[2,2,2,32,256]{4,3,2,1,0:T(8,128)S(1)}, f32[2,2,2,32,256]{4,3,2,1,0:T(8,128)S(1)}, u32[]{:S(2)}, u32[]{:S(2)}) collective-permute-start(f32[2,2,2,32,256]{4,3,2,1,0:T(8,128)S(1)} %bitcast_select_fusion), channel_id=1, source_target_pairs={{0,2},{1,5},{2,0},{3,7},{4,6},{5,1},{6,4},{7,3},{8,10},{9,13},{10,... | collective-permute-start | bytes 786440 | tf_op jit(solution)/shard_map/ppermute | solution.py:53
  9.9 4.4 %collective-permute-done.1 = f32[2,2,2,32,256]{4,3,2,1,0:T(8,128)S(1)} collective-permute-done((f32[2,2,2,32,256]{4,3,2,1,0:T(8,128)S(1)}, f32[2,2,2,32,256]{4,3,2,1,0:T(8,128)S(1)}, u32[]{:S(2)}, u32[]{:S(2)}) %collective-permute-start.1) | collective-permute-done | bytes 262176 | tf_op jit(solution)/shard_map/ppermute | solution.py:53
  14.2 0.1 fusion.20
  14.3 2.1 %collective-permute-start.2 = (f32[2,2,32,256]{3,2,0,1:T(8,128)S(1)}, f32[2,2,32,256]{3,2,0,1:T(8,128)S(1)}, u32[]{:S(2)}, u32[]{:S(2)}) collective-permute-start(f32[2,2,32,256]{3,2,0,1:T(8,128)S(1)} %bitcast.59), channel_id=1, source_target_pairs={{0,4},{1,3},{2,6},{3,1},{4,0},{5,7},{6,2},{7,5},{8,12},{9,11},{10,... | collective-permute-start | bytes 393224 | tf_op jit(solution)/shard_map/ppermute | solution.py:53
  16.4 0.0 copy-done
  16.5 0.6 %fusion.23 = (s32[1]{0:T(128)}, s32[1]{0:T(128)}) fusion(s32[2]{0:T(128)S(1)} %copy-done), kind=kLoop, calls=%fused_computation.40 | loop fusion | bytes 16 | tf_op jit(solution)/shard_map/slice | solution.py:114
  19.0 0.0 copy-done.2
  19.0 0.1 dynamic_slice.54
  19.1 0.3 %collective-permute-done.2 = f32[2,2,32,256]{3,2,0,1:T(8,128)S(1)} collective-permute-done((f32[2,2,32,256]{3,2,0,1:T(8,128)S(1)}, f32[2,2,32,256]{3,2,0,1:T(8,128)S(1)}, u32[]{:S(2)}, u32[]{:S(2)}) %collective-permute-start.2) | collective-permute-done | bytes 131104 | tf_op jit(solution)/shard_map/ppermute | solution.py:53
  19.4 2.1 %collective-permute-start.3 = (f32[2,32,256]{2,1,0:T(8,128)S(1)}, f32[2,32,256]{2,1,0:T(8,128)S(1)}, u32[]{:S(2)}, u32[]{:S(2)}) collective-permute-start(f32[2,32,256]{2,1,0:T(8,128)S(1)} %dynamic-slice_bitcast_fusion), channel_id=1, source_target_pairs={{0,8},{1,9},{2,10},{3,11},{4,12},{5,13},{6,14},{7,15},{8,0},{9,1},... | collective-permute-start | bytes 196616 | tf_op jit(solution)/shard_map/ppermute | solution.py:53
  21.6 0.0 copy-done.1
  21.6 0.1 broadcast_subtract_fusion.1
  23.6 0.1 dynamic_slice.56
  23.6 0.2 collective-permute-done.3
  23.8 3.1 %collective-permute-start.4 = (f32[32,256]{1,0:T(8,128)S(1)}, f32[32,256]{1,0:T(8,128)S(1)}, u32[]{:S(2)}, u32[]{:S(2)}) collective-permute-start(f32[32,256]{1,0:T(8,128)S(1)} %dynamic-slice_bitcast_fusion.1), channel_id=1, source_target_pairs={{0,16},{1,17},{2,18},{3,19},{4,20},{5,21},{6,22},{7,23},{8,24},{9,... | collective-permute-start | bytes 98312 | tf_op jit(solution)/shard_map/ppermute | solution.py:53
  27.0 0.1 broadcast_subtract_fusion
  27.0 0.1 sub.60
  27.1 0.1 sub.64
  27.2 0.1 dynamic_slice.55
  27.3 1.6 %collective-permute-done.4 = f32[32,256]{1,0:T(8,128)S(1)} collective-permute-done((f32[32,256]{1,0:T(8,128)S(1)}, f32[32,256]{1,0:T(8,128)S(1)}, u32[]{:S(2)}, u32[]{:S(2)}) %collective-permute-start.4) | collective-permute-done | bytes 32800 | tf_op jit(solution)/shard_map/ppermute | solution.py:53
  28.9 0.7 %fusion.22 = bf16[32,256]{1,0:T(8,128)(2,1)} fusion(f32[32,256]{1,0:T(8,128)S(1)} %collective-permute-done.4, f32[2,32,256]{2,1,0:T(8,128)S(1)} %bitcast_add_fusion.1, s32[]{:T(128)S(6)} %select_n.97, f32[256]{0:T(256)S(1)} %sub.64, f32[32]{0:T(128)S(1)} %dynamic_slice.55), kind=kLoop, calls=%fused_computation.34 | loop fusion | flops 32768 | bytes 83076 | tf_op jit(solution)/shard_map/convert_element_type | solution.py:149
  (9 shorter events, 0.1 us)
Async XLA Ops:
  4.7 2.4 %collective-permute-start = (f32[512,256]{1,0:T(8,128)S(1)}, f32[512,256]{1,0:T(8,128)S(1)}, u32[]{:S(2)}, u32[]{:S(2)}) collective-permute-start(f32[512,256]{1,0:T(8,128)S(1)} %get-tuple-element.70), channel_id=1, source_target_pairs={{0,1},{1,0},{2,3},{3,2},{4,5},{5,4},{6,7},{7,6},{8,9},{9,8},{10,11... | collective-permute-start | bytes 1572872 | tf_op jit(solution)/shard_map/ppermute | solution.py:28
  7.1 9.4 %copy-start = (s32[2]{0:T(128)S(1)}, s32[2]{0:T(128)}, u32[]{:S(2)}) copy-start(s32[2]{0:T(128)} %slab_ref.1) | copy-start | bytes 28
  7.1 11.9 %copy-start.2 = (f32[512]{0:T(512)S(1)}, f32[512]{0:T(512)}, u32[]{:S(2)}) copy-start(f32[512]{0:T(512)} %param.16) | copy-start | bytes 6148
  7.1 14.5 %copy-start.1 = (f32[64]{0:T(128)S(1)}, f32[64]{0:T(128)}, u32[]{:S(2)}) copy-start(f32[64]{0:T(128)} %param.15) | copy-start | bytes 772
  7.3 7.0 %collective-permute-start.1 = (f32[2,2,2,32,256]{4,3,2,1,0:T(8,128)S(1)}, f32[2,2,2,32,256]{4,3,2,1,0:T(8,128)S(1)}, u32[]{:S(2)}, u32[]{:S(2)}) collective-permute-start(f32[2,2,2,32,256]{4,3,2,1,0:T(8,128)S(1)} %bitcast_select_fusion), channel_id=1, source_target_pairs={{0,2},{1,5},{2,0},{3,7},{4,6},{5,1},{6,4},{7,3},{8,10},{9,13},{10,... | collective-permute-start | bytes 786440 | tf_op jit(solution)/shard_map/ppermute | solution.py:53
  14.3 5.1 %collective-permute-start.2 = (f32[2,2,32,256]{3,2,0,1:T(8,128)S(1)}, f32[2,2,32,256]{3,2,0,1:T(8,128)S(1)}, u32[]{:S(2)}, u32[]{:S(2)}) collective-permute-start(f32[2,2,32,256]{3,2,0,1:T(8,128)S(1)} %bitcast.59), channel_id=1, source_target_pairs={{0,4},{1,3},{2,6},{3,1},{4,0},{5,7},{6,2},{7,5},{8,12},{9,11},{10,... | collective-permute-start | bytes 393224 | tf_op jit(solution)/shard_map/ppermute | solution.py:53
  19.4 4.4 %collective-permute-start.3 = (f32[2,32,256]{2,1,0:T(8,128)S(1)}, f32[2,32,256]{2,1,0:T(8,128)S(1)}, u32[]{:S(2)}, u32[]{:S(2)}) collective-permute-start(f32[2,32,256]{2,1,0:T(8,128)S(1)} %dynamic-slice_bitcast_fusion), channel_id=1, source_target_pairs={{0,8},{1,9},{2,10},{3,11},{4,12},{5,13},{6,14},{7,15},{8,0},{9,1},... | collective-permute-start | bytes 196616 | tf_op jit(solution)/shard_map/ppermute | solution.py:53
  23.8 5.0 %collective-permute-start.4 = (f32[32,256]{1,0:T(8,128)S(1)}, f32[32,256]{1,0:T(8,128)S(1)}, u32[]{:S(2)}, u32[]{:S(2)}) collective-permute-start(f32[32,256]{1,0:T(8,128)S(1)} %dynamic-slice_bitcast_fusion.1), channel_id=1, source_target_pairs={{0,16},{1,17},{2,18},{3,19},{4,20},{5,21},{6,22},{7,23},{8,24},{9,... | collective-permute-start | bytes 98312 | tf_op jit(solution)/shard_map/ppermute | solution.py:53

commit v13 on v12

--- a/solution.py
+++ b/solution.py
@@ -54,11 +54,11 @@
     return buf.reshape(block, cols)
 
 
-def _irrep_kernel(shape, slab_ref, occ_s_ref, occ_v_ref, virt_v_ref, row_ref, kc_ref, col_ref):
+def _irrep_kernel(shape, slab_ref, occ_s_ref, occ_v_ref, virt_v_ref, int_ref, row_ref, kc_ref, masked_ref):
     virt_count = virt_v_ref.shape[0]
     occ_count = occ_v_ref.shape[0]
     kc_local = kc_ref.shape[1]
-    cols = col_ref.shape[1]
+    cols = int_ref.shape[1]
     occ_local = kc_local // virt_count
     f32, bf16, i32 = jnp.float32, jnp.bfloat16, jnp.int32
     occ_rows = jnp.broadcast_to(occ_v_ref[...].reshape(1, occ_count), (8, occ_count)).astype(bf16)
@@ -80,22 +80,33 @@
         row_ref[parity:parity + 1, :] = spread(
             rows_pair // 2, slab_ref[0], per_row,
             lambda x: first + ((x // block) * 2 + parity) * block + x % block)
-    col_ref[...] = spread(cols, slab_ref[1], cols // occ_count)
+    col_irrep = spread(cols, slab_ref[1], cols // occ_count)
     base = lax.axis_index("contr") * occ_local
     parts = [jnp.bitwise_xor(virt_v_ref[...].reshape(1, virt_count), occ_s_ref[base + k]) for k in range(occ_local)]
     kc_ref[...] = jnp.concatenate(parts, axis=1) if occ_local > 1 else parts[0]
+    eye = (lax.broadcasted_iota(i32, (virt_count, virt_count), 0)
+           == lax.broadcasted_iota(i32, (virt_count, virt_count), 1)).astype(bf16)
+    virt_col = lax.dot_general(eye, virt_rows, (((1,), (1,)), ((), ())), preferred_element_type=f32)
+    virt_col = virt_col.astype(i32)[:, 0:1]
+    for k in range(occ_local):
+        kc_col = jnp.bitwise_xor(virt_col, occ_s_ref[base + k])
+        block = int_ref[k * virt_count:(k + 1) * virt_count, :]
+        masked_ref[k * virt_count:(k + 1) * virt_count, :] = jnp.where(
+            kc_col == col_irrep, block, jnp.zeros_like(block))
 
 
-def irreps(shape, slab_start, occ_irrep, virt_irrep, kc_local, cols):
+def irreps(shape, slab_start, occ_irrep, virt_irrep, integrals):
     smem = pl.BlockSpec(memory_space=pltpu.SMEM)
     vmem = pl.BlockSpec(memory_space=pltpu.VMEM)
-    shapes = [jax.ShapeDtypeStruct(n, jnp.int32) for n in ((2, shape[1] // 2), (1, kc_local), (1, cols))]
+    shapes = [jax.ShapeDtypeStruct((2, shape[1] // 2), jnp.int32),
+              jax.ShapeDtypeStruct((1, integrals.shape[0]), jnp.int32),
+              jax.ShapeDtypeStruct(integrals.shape, integrals.dtype)]
     return pl.pallas_call(
         functools.partial(_irrep_kernel, shape),
         out_shape=shapes,
-        in_specs=[smem, smem, vmem, vmem],
+        in_specs=[smem, smem, vmem, vmem, vmem],
         out_specs=[vmem, vmem, vmem],
-    )(slab_start, occ_irrep, occ_irrep, virt_irrep)
+    )(slab_start, occ_irrep, occ_irrep, virt_irrep, integrals)
 
 
 def body(amplitudes, integrals, occ_irrep, virt_irrep, occ_energy, virt_energy, slab_start):
@@ -121,10 +132,9 @@
     whole_int = lax.all_gather(integrals, "pair", axis=1, tiled=True)
     block = rows_pair // contr_count
     split = contr_count & (contr_count - 1) == 0 and rows_pair % (2 * contr_count) == 0
-    row_k, kc_k, col_k = irreps((pair_count, rows_pair, block if split else rows_pair // 2),
-                                slab_start, occ_irrep, virt_irrep, kc_local, cols_pair * pair_count)
+    row_k, kc_k, int_masked = irreps((pair_count, rows_pair, block if split else rows_pair // 2),
+                                     slab_start, occ_irrep, virt_irrep, whole_int)
     kc_irrep = kc_k.reshape(-1)
-    int_masked = jnp.where(kc_irrep[:, None] == col_k.reshape(-1)[None, :], whole_int, zero)
 
     def product(amp, irrep):
         masked = jnp.where(irrep[:, None] == kc_irrep[None, :], amp, zero)

time: 29.8 us -> 28.6 us (0.960)
  other arithmetic: 2.27 us -> 1.02 us
    select_n x1 -> x0, other arithmetic: 1.24 us -> none  [body(): jnp.where(kc_irrep[:, None] == col_k.reshape(-1)[None, :], whole_int, zero)]
  transfers between devices with their start and end apart: 5 -> 5, of which waited for: 4 -> 4; matrix products, arithmetic and copies ran while one was open for 10% -> 11% of each run, Pallas kernels for 0% -> 0%
where the time goes in v13:
time: 28.6 us; the launch traced here: 28.3 us
  starting transfers between devices  10.5 us (37%)
  waiting for transfers between devices  6.4 us (22%)
  between operations  4.01 us (14%)
  local copies, waits for them, and re-layouts  3.75 us (13%)
  Pallas kernels  1.67 us (6%)
  other arithmetic  1.02 us (4%)
  matrix products  0.98 us (3%)
    ppermute x4, starting transfers between devices, halving_scatter(): buf = keep + lax.ppermute(send, axis, perm)  9.95 us
    ppermute x4, waiting for transfers between devices, halving_scatter(): buf = keep + lax.ppermute(send, axis, perm)  6.39 us
    slice x2, local copies, waits for them, and re-layouts, half(): amp4[:, parity].reshape(rows_pair // 2, kc_local)  2.64 us
    pallas_call x1, Pallas kernels, irreps(): pl.pallas_call(functools.partial(_irrep_kernel, shape), out_shape=shapes,...  1.67 us
    dot_general x2, matrix products, product(): return jnp.dot(masked, int_masked, preferred_element_type=jnp.float32)  0.98 us
    convert_element_type x1, other arithmetic, body(): (summed / (mine_energy[:, None] + col_energy[None, :])).astype(jnp.bfloat16)  0.69 us
    slice x1, local copies, waits for them, and re-layouts, body(): first_start = slab_start[0]  0.6 us
  transfers between devices with their start and end apart: 5, of which 4 were waited for; matrix products, arithmetic and copies ran while one was open for 11% of the time, Pallas kernels for 0%

profile of v13, /device:TPU:0, one launch (start us, length us, event | category | flops | bytes accessed | tf_op | source)
XLA Modules:
  0.0 28.3 jit_solution(5078793165903271885)
XLA Ops:
  0.0 1.7 %shard_map.73 = (s32[2,512]{1,0:T(2,128)S(1)}, s32[1,1024]{1,0:T(1,128)S(1)}, bf16[1024,256]{1,0:T(8,128)(2,1)S(1)}) custom-call(s32[2]{0:T(128)} %slab_ref.1, s32[64]{0:T(128)} %occ_v_ref.1, s32[64]{0:T(128)} %occ_v_ref.1, s32[512]{0:T(512)} %virt_v_ref.1, bf16[1024,256]{1,0:T(8,128)(2,1)} %int_ref), custom_call_target="tpu_custom_call" | custom-call | tf_op jit(solution)/shard_map/pallas_call | solution.py:104
  1.7 1.9 %conditional.3 = (f32[512,256]{1,0:T(8,128)S(1)}) conditional(s32[]{:T(128)} %convert_element_type.7, (s32[2,512]{1,0:T(2,128)S(1)}, s32[1,1024]{1,0:T(1,128)S(1)}, bf16[16,2,32,1024]{3,2,1,0:T(8,128)(2,1)}, bf16[1024,256]{1,0:T(8,128)(2,1)S(1)}) %tuple.24, (s32[2,512]{1,0:T(2,128)S(1)}, s32[1,1024]{1,0:T(1,128)S(1)}, ...), branch_computations={%region_2.3_spmd, %region_3.4_spmd} | conditional | flops 269484032 | bytes 4204552 | solution.py:150
  1.7 1.3 %slice.27 = bf16[16,1,32,1024]{3,2,1,0:T(8,128)(2,1)S(1)} slice(bf16[16,2,32,1024]{3,2,1,0:T(8,128)(2,1)} %get-tuple-element.57), slice={[0:16], [1:2], [0:32], [0:1024]} | slice | bytes 2097152 | tf_op jit(solution)/shard_map/cond/branch_1_fun/slice | solution.py:148
  3.0 0.5 %fusion.15 = f32[512,256]{1,0:T(8,128)S(1)} fusion(bf16[1024,256]{1,0:T(8,128)(2,1)S(1)} %get-tuple-element.58, bf16[512,1024]{1,0:T(8,128)(2,1)S(1)} %bitcast.54, s32[1024]{0:T(1024)S(1)} %bitcast.63, s32[512]{0:T(512)S(1)} %bitcast.59), kind=kOutput, calls=%fused_computation.19 | convolution fusion | flops 269484032 | bytes 2103296 | tf_op jit(solution)/shard_map/cond/branch_1_fun/dot_general | solution.py:141
  3.5 0.5 %collective-permute-start = (f32[512,256]{1,0:T(8,128)S(1)}, f32[512,256]{1,0:T(8,128)S(1)}, u32[]{:S(2)}, u32[]{:S(2)}) collective-permute-start(f32[512,256]{1,0:T(8,128)S(1)} %get-tuple-element.70), channel_id=1, source_target_pairs={{0,1},{1,0},{2,3},{3,2},{4,5},{5,4},{6,7},{7,6},{8,9},{9,8},{10,11... | collective-permute-start | bytes 1572872 | tf_op jit(solution)/shard_map/ppermute | solution.py:28
  4.1 1.8 %conditional.2 = (f32[512,256]{1,0:T(8,128)S(1)}) conditional(s32[]{:T(128)} %convert_element_type.7, (s32[2,512]{1,0:T(2,128)S(1)}, s32[1,1024]{1,0:T(1,128)S(1)}, bf16[16,2,32,1024]{3,2,1,0:T(8,128)(2,1)}, bf16[1024,256]{1,0:T(8,128)(2,1)S(1)}) %tuple.26, (s32[2,512]{1,0:T(2,128)S(1)}, s32[1,1024]{1,0:T(1,128)S(1)}, ...), branch_computations={%region_0.1_spmd, %region_1.2_spmd} | conditional | flops 269484032 | bytes 4204552 | solution.py:152
  4.1 1.3 %slice.23 = bf16[16,1,32,1024]{3,2,1,0:T(8,128)(2,1)S(1)} slice(bf16[16,2,32,1024]{3,2,1,0:T(8,128)(2,1)} %get-tuple-element.49), slice={[0:16], [0:1], [0:32], [0:1024]} | slice | bytes 2097152 | tf_op jit(solution)/shard_map/cond/branch_1_fun/slice | solution.py:148
  5.4 0.5 %fusion.5 = f32[512,256]{1,0:T(8,128)S(1)} fusion(bf16[1024,256]{1,0:T(8,128)(2,1)S(1)} %get-tuple-element.50, bf16[512,1024]{1,0:T(8,128)(2,1)S(1)} %bitcast.56, s32[1024]{0:T(1024)S(1)} %bitcast.65, s32[512]{0:T(512)S(1)} %bitcast.61), kind=kOutput, calls=%fused_computation.7 | convolution fusion | flops 269484032 | bytes 2103296 | tf_op jit(solution)/shard_map/cond/branch_1_fun/dot_general | solution.py:141
  5.9 0.0 copy-start
  5.9 0.0 copy-start.2
  5.9 0.0 copy-start.1
  5.9 0.0 collective-permute-done
  5.9 0.1 add.83
  6.1 2.6 %collective-permute-start.1 = (f32[2,2,2,32,256]{4,3,2,1,0:T(8,128)S(1)}, f32[2,2,2,32,256]{4,3,2,1,0:T(8,128)S(1)}, u32[]{:S(2)}, u32[]{:S(2)}) collective-permute-start(f32[2,2,2,32,256]{4,3,2,1,0:T(8,128)S(1)} %bitcast_select_fusion), channel_id=1, source_target_pairs={{0,2},{1,5},{2,0},{3,7},{4,6},{5,1},{6,4},{7,3},{8,10},{9,13},{10,... | collective-permute-start | bytes 786440 | tf_op jit(solution)/shard_map/ppermute | solution.py:53
  8.7 4.4 %collective-permute-done.1 = f32[2,2,2,32,256]{4,3,2,1,0:T(8,128)S(1)} collective-permute-done((f32[2,2,2,32,256]{4,3,2,1,0:T(8,128)S(1)}, f32[2,2,2,32,256]{4,3,2,1,0:T(8,128)S(1)}, u32[]{:S(2)}, u32[]{:S(2)}) %collective-permute-start.1) | collective-permute-done | bytes 262176 | tf_op jit(solution)/shard_map/ppermute | solution.py:53
  13.0 0.1 fusion.20
  13.1 2.1 %collective-permute-start.2 = (f32[2,2,32,256]{3,2,0,1:T(8,128)S(1)}, f32[2,2,32,256]{3,2,0,1:T(8,128)S(1)}, u32[]{:S(2)}, u32[]{:S(2)}) collective-permute-start(f32[2,2,32,256]{3,2,0,1:T(8,128)S(1)} %bitcast.57), channel_id=1, source_target_pairs={{0,4},{1,3},{2,6},{3,1},{4,0},{5,7},{6,2},{7,5},{8,12},{9,11},{10,... | collective-permute-start | bytes 393224 | tf_op jit(solution)/shard_map/ppermute | solution.py:53
  15.3 0.0 copy-done
  15.3 0.6 %fusion.23 = (s32[1]{0:T(128)}, s32[1]{0:T(128)}) fusion(s32[2]{0:T(128)S(1)} %copy-done), kind=kLoop, calls=%fused_computation.39 | loop fusion | bytes 16 | tf_op jit(solution)/shard_map/slice | solution.py:125
  17.8 0.0 copy-done.2
  17.8 0.1 dynamic_slice.54
  17.9 0.3 %collective-permute-done.2 = f32[2,2,32,256]{3,2,0,1:T(8,128)S(1)} collective-permute-done((f32[2,2,32,256]{3,2,0,1:T(8,128)S(1)}, f32[2,2,32,256]{3,2,0,1:T(8,128)S(1)}, u32[]{:S(2)}, u32[]{:S(2)}) %collective-permute-start.2) | collective-permute-done | bytes 131104 | tf_op jit(solution)/shard_map/ppermute | solution.py:53
  18.2 2.1 %collective-permute-start.3 = (f32[2,32,256]{2,1,0:T(8,128)S(1)}, f32[2,32,256]{2,1,0:T(8,128)S(1)}, u32[]{:S(2)}, u32[]{:S(2)}) collective-permute-start(f32[2,32,256]{2,1,0:T(8,128)S(1)} %dynamic-slice_bitcast_fusion), channel_id=1, source_target_pairs={{0,8},{1,9},{2,10},{3,11},{4,12},{5,13},{6,14},{7,15},{8,0},{9,1},... | collective-permute-start | bytes 196616 | tf_op jit(solution)/shard_map/ppermute | solution.py:53
  20.4 0.0 copy-done.1
  20.4 0.1 broadcast_subtract_fusion.1
  22.4 0.1 dynamic_slice.56
  22.4 0.2 collective-permute-done.3
  22.7 3.1 %collective-permute-start.4 = (f32[32,256]{1,0:T(8,128)S(1)}, f32[32,256]{1,0:T(8,128)S(1)}, u32[]{:S(2)}, u32[]{:S(2)}) collective-permute-start(f32[32,256]{1,0:T(8,128)S(1)} %dynamic-slice_bitcast_fusion.1), channel_id=1, source_target_pairs={{0,16},{1,17},{2,18},{3,19},{4,20},{5,21},{6,22},{7,23},{8,24},{9,... | collective-permute-start | bytes 98312 | tf_op jit(solution)/shard_map/ppermute | solution.py:53
  25.8 0.1 broadcast_subtract_fusion
  25.8 0.1 sub.60
  25.9 0.1 sub.64
  26.0 0.1 dynamic_slice.55
  26.1 1.6 %collective-permute-done.4 = f32[32,256]{1,0:T(8,128)S(1)} collective-permute-done((f32[32,256]{1,0:T(8,128)S(1)}, f32[32,256]{1,0:T(8,128)S(1)}, u32[]{:S(2)}, u32[]{:S(2)}) %collective-permute-start.4) | collective-permute-done | bytes 32800 | tf_op jit(solution)/shard_map/ppermute | solution.py:53
  27.7 0.7 %fusion.22 = bf16[32,256]{1,0:T(8,128)(2,1)} fusion(f32[32,256]{1,0:T(8,128)S(1)} %collective-permute-done.4, f32[2,32,256]{2,1,0:T(8,128)S(1)} %bitcast_add_fusion.1, s32[]{:T(128)S(6)} %select_n.92, f32[256]{0:T(256)S(1)} %sub.64, f32[32]{0:T(128)S(1)} %dynamic_slice.55), kind=kLoop, calls=%fused_computation.33 | loop fusion | flops 32768 | bytes 83076 | tf_op jit(solution)/shard_map/convert_element_type | solution.py:159
  (9 shorter events, 0.1 us)
Async XLA Ops:
  3.5 2.4 %collective-permute-start = (f32[512,256]{1,0:T(8,128)S(1)}, f32[512,256]{1,0:T(8,128)S(1)}, u32[]{:S(2)}, u32[]{:S(2)}) collective-permute-start(f32[512,256]{1,0:T(8,128)S(1)} %get-tuple-element.70), channel_id=1, source_target_pairs={{0,1},{1,0},{2,3},{3,2},{4,5},{5,4},{6,7},{7,6},{8,9},{9,8},{10,11... | collective-permute-start | bytes 1572872 | tf_op jit(solution)/shard_map/ppermute | solution.py:28
  5.9 9.4 %copy-start = (s32[2]{0:T(128)S(1)}, s32[2]{0:T(128)}, u32[]{:S(2)}) copy-start(s32[2]{0:T(128)} %slab_ref.1) | copy-start | bytes 28
  5.9 11.9 %copy-start.2 = (f32[512]{0:T(512)S(1)}, f32[512]{0:T(512)}, u32[]{:S(2)}) copy-start(f32[512]{0:T(512)} %param.16) | copy-start | bytes 6148
  5.9 14.5 %copy-start.1 = (f32[64]{0:T(128)S(1)}, f32[64]{0:T(128)}, u32[]{:S(2)}) copy-start(f32[64]{0:T(128)} %param.15) | copy-start | bytes 772
  6.1 6.9 %collective-permute-start.1 = (f32[2,2,2,32,256]{4,3,2,1,0:T(8,128)S(1)}, f32[2,2,2,32,256]{4,3,2,1,0:T(8,128)S(1)}, u32[]{:S(2)}, u32[]{:S(2)}) collective-permute-start(f32[2,2,2,32,256]{4,3,2,1,0:T(8,128)S(1)} %bitcast_select_fusion), channel_id=1, source_target_pairs={{0,2},{1,5},{2,0},{3,7},{4,6},{5,1},{6,4},{7,3},{8,10},{9,13},{10,... | collective-permute-start | bytes 786440 | tf_op jit(solution)/shard_map/ppermute | solution.py:53
  13.1 5.1 %collective-permute-start.2 = (f32[2,2,32,256]{3,2,0,1:T(8,128)S(1)}, f32[2,2,32,256]{3,2,0,1:T(8,128)S(1)}, u32[]{:S(2)}, u32[]{:S(2)}) collective-permute-start(f32[2,2,32,256]{3,2,0,1:T(8,128)S(1)} %bitcast.57), channel_id=1, source_target_pairs={{0,4},{1,3},{2,6},{3,1},{4,0},{5,7},{6,2},{7,5},{8,12},{9,11},{10,... | collective-permute-start | bytes 393224 | tf_op jit(solution)/shard_map/ppermute | solution.py:53
  18.2 4.4 %collective-permute-start.3 = (f32[2,32,256]{2,1,0:T(8,128)S(1)}, f32[2,32,256]{2,1,0:T(8,128)S(1)}, u32[]{:S(2)}, u32[]{:S(2)}) collective-permute-start(f32[2,32,256]{2,1,0:T(8,128)S(1)} %dynamic-slice_bitcast_fusion), channel_id=1, source_target_pairs={{0,8},{1,9},{2,10},{3,11},{4,12},{5,13},{6,14},{7,15},{8,0},{9,1},... | collective-permute-start | bytes 196616 | tf_op jit(solution)/shard_map/ppermute | solution.py:53
  22.7 5.0 %collective-permute-start.4 = (f32[32,256]{1,0:T(8,128)S(1)}, f32[32,256]{1,0:T(8,128)S(1)}, u32[]{:S(2)}, u32[]{:S(2)}) collective-permute-start(f32[32,256]{1,0:T(8,128)S(1)} %dynamic-slice_bitcast_fusion.1), channel_id=1, source_target_pairs={{0,16},{1,17},{2,18},{3,19},{4,20},{5,21},{6,22},{7,23},{8,24},{9,... | collective-permute-start | bytes 98312 | tf_op jit(solution)/shard_map/ppermute | solution.py:53

commit v14 on v13

--- a/solution.py
+++ b/solution.py
@@ -54,7 +54,10 @@
     return buf.reshape(block, cols)
 
 
-def _irrep_kernel(shape, slab_ref, occ_s_ref, occ_v_ref, virt_v_ref, int_ref, row_ref, kc_ref, masked_ref):
+def _irrep_kernel(shape, slab_ref, occ_s_ref, occ_v_ref, virt_v_ref, int_hbm, row_ref, kc_ref, masked_ref,
+                  int_ref, sem):
+    fetch = pltpu.make_async_copy(int_hbm, int_ref, sem)
+    fetch.start()
     virt_count = virt_v_ref.shape[0]
     occ_count = occ_v_ref.shape[0]
     kc_local = kc_ref.shape[1]
@@ -88,6 +91,7 @@
            == lax.broadcasted_iota(i32, (virt_count, virt_count), 1)).astype(bf16)
     virt_col = lax.dot_general(eye, virt_rows, (((1,), (1,)), ((), ())), preferred_element_type=f32)
     virt_col = virt_col.astype(i32)[:, 0:1]
+    fetch.wait()
     for k in range(occ_local):
         kc_col = jnp.bitwise_xor(virt_col, occ_s_ref[base + k])
         block = int_ref[k * virt_count:(k + 1) * virt_count, :]
@@ -104,8 +108,9 @@
     return pl.pallas_call(
         functools.partial(_irrep_kernel, shape),
         out_shape=shapes,
-        in_specs=[smem, smem, vmem, vmem, vmem],
+        in_specs=[smem, smem, vmem, vmem, pl.BlockSpec(memory_space=pl.ANY)],
         out_specs=[vmem, vmem, vmem],
+        scratch_shapes=[pltpu.VMEM(integrals.shape, integrals.dtype), pltpu.SemaphoreType.DMA(())],
     )(slab_start, occ_irrep, occ_irrep, virt_irrep, integrals)
 
 

time: 28.6 us -> 29.3 us (1.024)
  Pallas kernels: 1.67 us -> 2.31 us
    pallas_call x1, Pallas kernels: 1.67 us -> 2.31 us  [irreps(): pl.pallas_call(functools.partial(_irrep_kernel, shape), out_shape=shapes,...]
  transfers between devices with their start and end apart: 5 -> 5, of which waited for: 4 -> 4; matrix products, arithmetic and copies ran while one was open for 11% -> 10% of each run, Pallas kernels for 0% -> 0%
where the time goes in v14:
time: 29.3 us; the launch traced here: 29 us
  starting transfers between devices  10.5 us (36%)
  waiting for transfers between devices  6.4 us (22%)
  between operations  4.01 us (14%)
  local copies, waits for them, and re-layouts  3.75 us (13%)
  Pallas kernels  2.31 us (8%)
  other arithmetic  1.02 us (3%)
  matrix products  0.98 us (3%)
    ppermute x4, starting transfers between devices, halving_scatter(): buf = keep + lax.ppermute(send, axis, perm)  9.95 us
    ppermute x4, waiting for transfers between devices, halving_scatter(): buf = keep + lax.ppermute(send, axis, perm)  6.39 us
    slice x2, local copies, waits for them, and re-layouts, half(): amp4[:, parity].reshape(rows_pair // 2, kc_local)  2.64 us
    pallas_call x1, Pallas kernels, irreps(): pl.pallas_call(functools.partial(_irrep_kernel, shape), out_shape=shapes,...  2.31 us
    dot_general x2, matrix products, product(): return jnp.dot(masked, int_masked, preferred_element_type=jnp.float32)  0.98 us
    convert_element_type x1, other arithmetic, body(): (summed / (mine_energy[:, None] + col_energy[None, :])).astype(jnp.bfloat16)  0.69 us
    slice x1, local copies, waits for them, and re-layouts, body(): first_start = slab_start[0]  0.6 us
  transfers between devices with their start and end apart: 5, of which 4 were waited for; matrix products, arithmetic and copies ran while one was open for 10% of the time, Pallas kernels for 0%

profile of v14, /device:TPU:0, one launch (start us, length us, event | category | flops | bytes accessed | tf_op | source)
XLA Modules:
  0.0 29.0 jit_solution(1836486644687424201)
XLA Ops:
  0.0 2.3 %shard_map.73 = (s32[2,512]{1,0:T(2,128)S(1)}, s32[1,1024]{1,0:T(1,128)S(1)}, bf16[1024,256]{1,0:T(8,128)(2,1)S(1)}) custom-call(s32[2]{0:T(128)} %slab_ref.1, s32[64]{0:T(128)} %occ_v_ref.1, s32[64]{0:T(128)} %occ_v_ref.1, s32[512]{0:T(512)} %virt_v_ref.1, bf16[1024,256]{1,0:T(8,128)(2,1)} %int_hbm), custom_call_target="tpu_custom_call" | custom-call | tf_op jit(solution)/shard_map/pallas_call | solution.py:108
  2.3 1.8 %conditional.3 = (f32[512,256]{1,0:T(8,128)S(1)}) conditional(s32[]{:T(128)} %convert_element_type.7, (s32[2,512]{1,0:T(2,128)S(1)}, s32[1,1024]{1,0:T(1,128)S(1)}, bf16[16,2,32,1024]{3,2,1,0:T(8,128)(2,1)}, bf16[1024,256]{1,0:T(8,128)(2,1)S(1)}) %tuple.24, (s32[2,512]{1,0:T(2,128)S(1)}, s32[1,1024]{1,0:T(1,128)S(1)}, ...), branch_computations={%region_2.3_spmd, %region_3.4_spmd} | conditional | flops 269484032 | bytes 4204552 | solution.py:155
  2.3 1.3 %slice.27 = bf16[16,1,32,1024]{3,2,1,0:T(8,128)(2,1)S(1)} slice(bf16[16,2,32,1024]{3,2,1,0:T(8,128)(2,1)} %get-tuple-element.57), slice={[0:16], [1:2], [0:32], [0:1024]} | slice | bytes 2097152 | tf_op jit(solution)/shard_map/cond/branch_1_fun/slice | solution.py:153
  3.7 0.5 %fusion.15 = f32[512,256]{1,0:T(8,128)S(1)} fusion(bf16[1024,256]{1,0:T(8,128)(2,1)S(1)} %get-tuple-element.58, bf16[512,1024]{1,0:T(8,128)(2,1)S(1)} %bitcast.54, s32[1024]{0:T(1024)S(1)} %bitcast.63, s32[512]{0:T(512)S(1)} %bitcast.59), kind=kOutput, calls=%fused_computation.19 | convolution fusion | flops 269484032 | bytes 2103296 | tf_op jit(solution)/shard_map/cond/branch_1_fun/dot_general | solution.py:146
  4.2 0.5 %collective-permute-start = (f32[512,256]{1,0:T(8,128)S(1)}, f32[512,256]{1,0:T(8,128)S(1)}, u32[]{:S(2)}, u32[]{:S(2)}) collective-permute-start(f32[512,256]{1,0:T(8,128)S(1)} %get-tuple-element.70), channel_id=1, source_target_pairs={{0,1},{1,0},{2,3},{3,2},{4,5},{5,4},{6,7},{7,6},{8,9},{9,8},{10,11... | collective-permute-start | bytes 1572872 | tf_op jit(solution)/shard_map/ppermute | solution.py:28
  4.7 1.8 %conditional.2 = (f32[512,256]{1,0:T(8,128)S(1)}) conditional(s32[]{:T(128)} %convert_element_type.7, (s32[2,512]{1,0:T(2,128)S(1)}, s32[1,1024]{1,0:T(1,128)S(1)}, bf16[16,2,32,1024]{3,2,1,0:T(8,128)(2,1)}, bf16[1024,256]{1,0:T(8,128)(2,1)S(1)}) %tuple.26, (s32[2,512]{1,0:T(2,128)S(1)}, s32[1,1024]{1,0:T(1,128)S(1)}, ...), branch_computations={%region_0.1_spmd, %region_1.2_spmd} | conditional | flops 269484032 | bytes 4204552 | solution.py:157
  4.7 1.3 %slice.23 = bf16[16,1,32,1024]{3,2,1,0:T(8,128)(2,1)S(1)} slice(bf16[16,2,32,1024]{3,2,1,0:T(8,128)(2,1)} %get-tuple-element.49), slice={[0:16], [0:1], [0:32], [0:1024]} | slice | bytes 2097152 | tf_op jit(solution)/shard_map/cond/branch_1_fun/slice | solution.py:153
  6.0 0.5 %fusion.5 = f32[512,256]{1,0:T(8,128)S(1)} fusion(bf16[1024,256]{1,0:T(8,128)(2,1)S(1)} %get-tuple-element.50, bf16[512,1024]{1,0:T(8,128)(2,1)S(1)} %bitcast.56, s32[1024]{0:T(1024)S(1)} %bitcast.65, s32[512]{0:T(512)S(1)} %bitcast.61), kind=kOutput, calls=%fused_computation.7 | convolution fusion | flops 269484032 | bytes 2103296 | tf_op jit(solution)/shard_map/cond/branch_1_fun/dot_general | solution.py:146
  6.5 0.0 copy-start
  6.6 0.0 copy-start.2
  6.6 0.0 copy-start.1
  6.6 0.0 collective-permute-done
  6.6 0.1 add.83
  6.7 2.6 %collective-permute-start.1 = (f32[2,2,2,32,256]{4,3,2,1,0:T(8,128)S(1)}, f32[2,2,2,32,256]{4,3,2,1,0:T(8,128)S(1)}, u32[]{:S(2)}, u32[]{:S(2)}) collective-permute-start(f32[2,2,2,32,256]{4,3,2,1,0:T(8,128)S(1)} %bitcast_select_fusion), channel_id=1, source_target_pairs={{0,2},{1,5},{2,0},{3,7},{4,6},{5,1},{6,4},{7,3},{8,10},{9,13},{10,... | collective-permute-start | bytes 786440 | tf_op jit(solution)/shard_map/ppermute | solution.py:53
  9.3 4.4 %collective-permute-done.1 = f32[2,2,2,32,256]{4,3,2,1,0:T(8,128)S(1)} collective-permute-done((f32[2,2,2,32,256]{4,3,2,1,0:T(8,128)S(1)}, f32[2,2,2,32,256]{4,3,2,1,0:T(8,128)S(1)}, u32[]{:S(2)}, u32[]{:S(2)}) %collective-permute-start.1) | collective-permute-done | bytes 262176 | tf_op jit(solution)/shard_map/ppermute | solution.py:53
  13.7 0.1 fusion.20
  13.8 2.1 %collective-permute-start.2 = (f32[2,2,32,256]{3,2,0,1:T(8,128)S(1)}, f32[2,2,32,256]{3,2,0,1:T(8,128)S(1)}, u32[]{:S(2)}, u32[]{:S(2)}) collective-permute-start(f32[2,2,32,256]{3,2,0,1:T(8,128)S(1)} %bitcast.57), channel_id=1, source_target_pairs={{0,4},{1,3},{2,6},{3,1},{4,0},{5,7},{6,2},{7,5},{8,12},{9,11},{10,... | collective-permute-start | bytes 393224 | tf_op jit(solution)/shard_map/ppermute | solution.py:53
  15.9 0.0 copy-done
  15.9 0.6 %fusion.23 = (s32[1]{0:T(128)}, s32[1]{0:T(128)}) fusion(s32[2]{0:T(128)S(1)} %copy-done), kind=kLoop, calls=%fused_computation.39 | loop fusion | bytes 16 | tf_op jit(solution)/shard_map/slice | solution.py:130
  18.4 0.0 copy-done.2
  18.4 0.1 dynamic_slice.54
  18.5 0.3 %collective-permute-done.2 = f32[2,2,32,256]{3,2,0,1:T(8,128)S(1)} collective-permute-done((f32[2,2,32,256]{3,2,0,1:T(8,128)S(1)}, f32[2,2,32,256]{3,2,0,1:T(8,128)S(1)}, u32[]{:S(2)}, u32[]{:S(2)}) %collective-permute-start.2) | collective-permute-done | bytes 131104 | tf_op jit(solution)/shard_map/ppermute | solution.py:53
  18.9 2.1 %collective-permute-start.3 = (f32[2,32,256]{2,1,0:T(8,128)S(1)}, f32[2,32,256]{2,1,0:T(8,128)S(1)}, u32[]{:S(2)}, u32[]{:S(2)}) collective-permute-start(f32[2,32,256]{2,1,0:T(8,128)S(1)} %dynamic-slice_bitcast_fusion), channel_id=1, source_target_pairs={{0,8},{1,9},{2,10},{3,11},{4,12},{5,13},{6,14},{7,15},{8,0},{9,1},... | collective-permute-start | bytes 196616 | tf_op jit(solution)/shard_map/ppermute | solution.py:53
  21.0 0.0 copy-done.1
  21.0 0.1 broadcast_subtract_fusion.1
  23.0 0.1 dynamic_slice.56
  23.1 0.2 collective-permute-done.3
  23.3 3.1 %collective-permute-start.4 = (f32[32,256]{1,0:T(8,128)S(1)}, f32[32,256]{1,0:T(8,128)S(1)}, u32[]{:S(2)}, u32[]{:S(2)}) collective-permute-start(f32[32,256]{1,0:T(8,128)S(1)} %dynamic-slice_bitcast_fusion.1), channel_id=1, source_target_pairs={{0,16},{1,17},{2,18},{3,19},{4,20},{5,21},{6,22},{7,23},{8,24},{9,... | collective-permute-start | bytes 98312 | tf_op jit(solution)/shard_map/ppermute | solution.py:53
  26.4 0.1 broadcast_subtract_fusion
  26.5 0.1 sub.60
  26.5 0.1 sub.64
  26.7 0.1 dynamic_slice.55
  26.7 1.6 %collective-permute-done.4 = f32[32,256]{1,0:T(8,128)S(1)} collective-permute-done((f32[32,256]{1,0:T(8,128)S(1)}, f32[32,256]{1,0:T(8,128)S(1)}, u32[]{:S(2)}, u32[]{:S(2)}) %collective-permute-start.4) | collective-permute-done | bytes 32800 | tf_op jit(solution)/shard_map/ppermute | solution.py:53
  28.3 0.7 %fusion.22 = bf16[32,256]{1,0:T(8,128)(2,1)} fusion(f32[32,256]{1,0:T(8,128)S(1)} %collective-permute-done.4, f32[2,32,256]{2,1,0:T(8,128)S(1)} %bitcast_add_fusion.1, s32[]{:T(128)S(6)} %select_n.92, f32[256]{0:T(256)S(1)} %sub.64, f32[32]{0:T(128)S(1)} %dynamic_slice.55), kind=kLoop, calls=%fused_computation.33 | loop fusion | flops 32768 | bytes 83076 | tf_op jit(solution)/shard_map/convert_element_type | solution.py:164
  (9 shorter events, 0.1 us)
Async XLA Ops:
  4.2 2.4 %collective-permute-start = (f32[512,256]{1,0:T(8,128)S(1)}, f32[512,256]{1,0:T(8,128)S(1)}, u32[]{:S(2)}, u32[]{:S(2)}) collective-permute-start(f32[512,256]{1,0:T(8,128)S(1)} %get-tuple-element.70), channel_id=1, source_target_pairs={{0,1},{1,0},{2,3},{3,2},{4,5},{5,4},{6,7},{7,6},{8,9},{9,8},{10,11... | collective-permute-start | bytes 1572872 | tf_op jit(solution)/shard_map/ppermute | solution.py:28
  6.5 9.3 %copy-start = (s32[2]{0:T(128)S(1)}, s32[2]{0:T(128)}, u32[]{:S(2)}) copy-start(s32[2]{0:T(128)} %slab_ref.1) | copy-start | bytes 28
  6.6 11.9 %copy-start.2 = (f32[512]{0:T(512)S(1)}, f32[512]{0:T(512)}, u32[]{:S(2)}) copy-start(f32[512]{0:T(512)} %param.16) | copy-start | bytes 6148
  6.6 14.5 %copy-start.1 = (f32[64]{0:T(128)S(1)}, f32[64]{0:T(128)}, u32[]{:S(2)}) copy-start(f32[64]{0:T(128)} %param.15) | copy-start | bytes 772
  6.7 6.9 %collective-permute-start.1 = (f32[2,2,2,32,256]{4,3,2,1,0:T(8,128)S(1)}, f32[2,2,2,32,256]{4,3,2,1,0:T(8,128)S(1)}, u32[]{:S(2)}, u32[]{:S(2)}) collective-permute-start(f32[2,2,2,32,256]{4,3,2,1,0:T(8,128)S(1)} %bitcast_select_fusion), channel_id=1, source_target_pairs={{0,2},{1,5},{2,0},{3,7},{4,6},{5,1},{6,4},{7,3},{8,10},{9,13},{10,... | collective-permute-start | bytes 786440 | tf_op jit(solution)/shard_map/ppermute | solution.py:53
  13.8 5.1 %collective-permute-start.2 = (f32[2,2,32,256]{3,2,0,1:T(8,128)S(1)}, f32[2,2,32,256]{3,2,0,1:T(8,128)S(1)}, u32[]{:S(2)}, u32[]{:S(2)}) collective-permute-start(f32[2,2,32,256]{3,2,0,1:T(8,128)S(1)} %bitcast.57), channel_id=1, source_target_pairs={{0,4},{1,3},{2,6},{3,1},{4,0},{5,7},{6,2},{7,5},{8,12},{9,11},{10,... | collective-permute-start | bytes 393224 | tf_op jit(solution)/shard_map/ppermute | solution.py:53
  18.9 4.4 %collective-permute-start.3 = (f32[2,32,256]{2,1,0:T(8,128)S(1)}, f32[2,32,256]{2,1,0:T(8,128)S(1)}, u32[]{:S(2)}, u32[]{:S(2)}) collective-permute-start(f32[2,32,256]{2,1,0:T(8,128)S(1)} %dynamic-slice_bitcast_fusion), channel_id=1, source_target_pairs={{0,8},{1,9},{2,10},{3,11},{4,12},{5,13},{6,14},{7,15},{8,0},{9,1},... | collective-permute-start | bytes 196616 | tf_op jit(solution)/shard_map/ppermute | solution.py:53
  23.3 5.0 %collective-permute-start.4 = (f32[32,256]{1,0:T(8,128)S(1)}, f32[32,256]{1,0:T(8,128)S(1)}, u32[]{:S(2)}, u32[]{:S(2)}) collective-permute-start(f32[32,256]{1,0:T(8,128)S(1)} %dynamic-slice_bitcast_fusion.1), channel_id=1, source_target_pairs={{0,16},{1,17},{2,18},{3,19},{4,20},{5,21},{6,22},{7,23},{8,24},{9,... | collective-permute-start | bytes 98312 | tf_op jit(solution)/shard_map/ppermute | solution.py:53

commit v15 on v13

--- a/solution.py
+++ b/solution.py
@@ -18,8 +18,6 @@
 
     def order(c):
         seq = list(range(bits))
-        if c == 1 and bits >= 3:
-            seq[1], seq[2] = seq[2], seq[1]
         return seq
 
     left = [list(range(bits - 1, -1, -1)) for _ in range(2)]

time: 28.6 us -> 31.3 us (1.094)
  waiting for transfers between devices: 6.4 us -> 10.3 us
  starting transfers between devices: 10.5 us -> 9.28 us
    ppermute x4, waiting for transfers between devices: 6.39 us -> 10.3 us  [halving_scatter(): buf = keep + lax.ppermute(send, axis, perm)]
    ppermute x4, starting transfers between devices: 9.95 us -> 8.77 us  [halving_scatter(): buf = keep + lax.ppermute(send, axis, perm)]
  transfers between devices with their start and end apart: 5 -> 5, of which waited for: 4 -> 4; matrix products, arithmetic and copies ran while one was open for 11% -> 10% of each run, Pallas kernels for 0% -> 0%
where the time goes in v15:
time: 31.3 us; the launch traced here: 31 us
  waiting for transfers between devices  10.3 us (33%)
  starting transfers between devices  9.28 us (30%)
  between operations  4 us (13%)
  local copies, waits for them, and re-layouts  3.78 us (12%)
  Pallas kernels  1.67 us (5%)
  matrix products  0.98 us (3%)
  other arithmetic  0.96 us (3%)
    ppermute x4, waiting for transfers between devices, halving_scatter(): buf = keep + lax.ppermute(send, axis, perm)  10.3 us
    ppermute x4, starting transfers between devices, halving_scatter(): buf = keep + lax.ppermute(send, axis, perm)  8.77 us
    slice x2, local copies, waits for them, and re-layouts, half(): amp4[:, parity].reshape(rows_pair // 2, kc_local)  2.64 us
    pallas_call x1, Pallas kernels, irreps(): pl.pallas_call(functools.partial(_irrep_kernel, shape), out_shape=shapes,...  1.67 us
    dot_general x2, matrix products, product(): return jnp.dot(masked, int_masked, preferred_element_type=jnp.float32)  0.98 us
    convert_element_type x1, other arithmetic, body(): (summed / (mine_energy[:, None] + col_energy[None, :])).astype(jnp.bfloat16)  0.69 us
  transfers between devices with their start and end apart: 5, of which 4 were waited for; matrix products, arithmetic and copies ran while one was open for 10% of the time, Pallas kernels for 0%

profile of v15, /device:TPU:0, one launch (start us, length us, event | category | flops | bytes accessed | tf_op | source)
XLA Modules:
  0.0 31.0 jit_solution(12466958936191892713)
XLA Ops:
  0.0 1.7 %shard_map.73 = (s32[2,512]{1,0:T(2,128)S(1)}, s32[1,1024]{1,0:T(1,128)S(1)}, bf16[1024,256]{1,0:T(8,128)(2,1)S(1)}) custom-call(s32[2]{0:T(128)} %slab_ref.1, s32[64]{0:T(128)} %occ_v_ref.1, s32[64]{0:T(128)} %occ_v_ref.1, s32[512]{0:T(512)} %virt_v_ref.1, bf16[1024,256]{1,0:T(8,128)(2,1)} %int_ref), custom_call_target="tpu_custom_call" | custom-call | tf_op jit(solution)/shard_map/pallas_call | solution.py:102
  1.7 1.9 %conditional.3 = (f32[512,256]{1,0:T(8,128)S(1)}) conditional(s32[]{:T(128)} %convert_element_type.7, (s32[2,512]{1,0:T(2,128)S(1)}, s32[1,1024]{1,0:T(1,128)S(1)}, bf16[16,2,32,1024]{3,2,1,0:T(8,128)(2,1)}, bf16[1024,256]{1,0:T(8,128)(2,1)S(1)}) %tuple.24, (s32[2,512]{1,0:T(2,128)S(1)}, s32[1,1024]{1,0:T(1,128)S(1)}, ...), branch_computations={%region_2.3_spmd, %region_3.4_spmd} | conditional | flops 269484032 | bytes 4204552 | solution.py:148
  1.7 1.3 %slice.27 = bf16[16,1,32,1024]{3,2,1,0:T(8,128)(2,1)S(1)} slice(bf16[16,2,32,1024]{3,2,1,0:T(8,128)(2,1)} %get-tuple-element.57), slice={[0:16], [1:2], [0:32], [0:1024]} | slice | bytes 2097152 | tf_op jit(solution)/shard_map/cond/branch_1_fun/slice | solution.py:146
  3.0 0.5 %fusion.15 = f32[512,256]{1,0:T(8,128)S(1)} fusion(bf16[1024,256]{1,0:T(8,128)(2,1)S(1)} %get-tuple-element.58, bf16[512,1024]{1,0:T(8,128)(2,1)S(1)} %bitcast.48, s32[1024]{0:T(1024)S(1)} %bitcast.57, s32[512]{0:T(512)S(1)} %bitcast.53), kind=kOutput, calls=%fused_computation.19 | convolution fusion | flops 269484032 | bytes 2103296 | tf_op jit(solution)/shard_map/cond/branch_1_fun/dot_general | solution.py:139
  3.5 0.5 %collective-permute-start = (f32[512,256]{1,0:T(8,128)S(1)}, f32[512,256]{1,0:T(8,128)S(1)}, u32[]{:S(2)}, u32[]{:S(2)}) collective-permute-start(f32[512,256]{1,0:T(8,128)S(1)} %get-tuple-element.70), channel_id=1, source_target_pairs={{0,1},{1,0},{2,3},{3,2},{4,5},{5,4},{6,7},{7,6},{8,9},{9,8},{10,11... | collective-permute-start | bytes 1572872 | tf_op jit(solution)/shard_map/ppermute | solution.py:26
  4.1 1.8 %conditional.2 = (f32[512,256]{1,0:T(8,128)S(1)}) conditional(s32[]{:T(128)} %convert_element_type.7, (s32[2,512]{1,0:T(2,128)S(1)}, s32[1,1024]{1,0:T(1,128)S(1)}, bf16[16,2,32,1024]{3,2,1,0:T(8,128)(2,1)}, bf16[1024,256]{1,0:T(8,128)(2,1)S(1)}) %tuple.26, (s32[2,512]{1,0:T(2,128)S(1)}, s32[1,1024]{1,0:T(1,128)S(1)}, ...), branch_computations={%region_0.1_spmd, %region_1.2_spmd} | conditional | flops 269484032 | bytes 4204552 | solution.py:150
  4.1 1.3 %slice.23 = bf16[16,1,32,1024]{3,2,1,0:T(8,128)(2,1)S(1)} slice(bf16[16,2,32,1024]{3,2,1,0:T(8,128)(2,1)} %get-tuple-element.49), slice={[0:16], [0:1], [0:32], [0:1024]} | slice | bytes 2097152 | tf_op jit(solution)/shard_map/cond/branch_1_fun/slice | solution.py:146
  5.4 0.5 %fusion.5 = f32[512,256]{1,0:T(8,128)S(1)} fusion(bf16[1024,256]{1,0:T(8,128)(2,1)S(1)} %get-tuple-element.50, bf16[512,1024]{1,0:T(8,128)(2,1)S(1)} %bitcast.50, s32[1024]{0:T(1024)S(1)} %bitcast.59, s32[512]{0:T(512)S(1)} %bitcast.55), kind=kOutput, calls=%fused_computation.7 | convolution fusion | flops 269484032 | bytes 2103296 | tf_op jit(solution)/shard_map/cond/branch_1_fun/dot_general | solution.py:139
  5.9 0.0 copy-start
  5.9 0.0 copy-start.2
  5.9 0.0 copy-start.1
  5.9 0.0 collective-permute-done
  5.9 0.1 add.75
  6.1 2.6 %collective-permute-start.1 = (f32[2,2,2,32,256]{4,3,2,1,0:T(8,128)S(1)}, f32[2,2,2,32,256]{4,3,2,1,0:T(8,128)S(1)}, u32[]{:S(2)}, u32[]{:S(2)}) collective-permute-start(f32[2,2,2,32,256]{4,3,2,1,0:T(8,128)S(1)} %dynamic-slice_bitcast_fusion), channel_id=1, source_target_pairs={{0,2},{1,3},{2,0},{3,1},{4,6},{5,7},{6,4},{7,5},{8,10},{9,11},{10,... | collective-permute-start | bytes 786440 | tf_op jit(solution)/shard_map/ppermute | solution.py:51
  8.6 7.0 %collective-permute-done.1 = f32[2,2,2,32,256]{4,3,2,1,0:T(8,128)S(1)} collective-permute-done((f32[2,2,2,32,256]{4,3,2,1,0:T(8,128)S(1)}, f32[2,2,2,32,256]{4,3,2,1,0:T(8,128)S(1)}, u32[]{:S(2)}, u32[]{:S(2)}) %collective-permute-start.1) | collective-permute-done | bytes 262176 | tf_op jit(solution)/shard_map/ppermute | solution.py:51
  15.7 1.8 %collective-permute-start.2 = (f32[2,2,32,256]{3,2,0,1:T(8,128)S(1)}, f32[2,2,32,256]{3,2,0,1:T(8,128)S(1)}, u32[]{:S(2)}, u32[]{:S(2)}) collective-permute-start(f32[2,2,32,256]{3,2,0,1:T(8,128)S(1)} %bitcast.51), channel_id=1, source_target_pairs={{0,4},{1,5},{2,6},{3,7},{4,0},{5,1},{6,2},{7,3},{8,12},{9,13},{10,... | collective-permute-start | bytes 393224 | tf_op jit(solution)/shard_map/ppermute | solution.py:51
  17.5 0.0 copy-done
  17.5 0.6 %fusion.22 = (s32[1]{0:T(128)}, s32[1]{0:T(128)}) fusion(s32[2]{0:T(128)S(1)} %copy-done), kind=kLoop, calls=%fused_computation.38 | loop fusion | bytes 16 | tf_op jit(solution)/shard_map/slice | solution.py:123
  20.1 0.0 copy-done.2
  20.1 0.1 dynamic_slice.45
  20.2 0.9 %collective-permute-done.2 = f32[2,2,32,256]{3,2,0,1:T(8,128)S(1)} collective-permute-done((f32[2,2,32,256]{3,2,0,1:T(8,128)S(1)}, f32[2,2,32,256]{3,2,0,1:T(8,128)S(1)}, u32[]{:S(2)}, u32[]{:S(2)}) %collective-permute-start.2) | collective-permute-done | bytes 131104 | tf_op jit(solution)/shard_map/ppermute | solution.py:51
  21.1 1.7 %collective-permute-start.3 = (f32[2,32,256]{2,1,0:T(8,128)S(1)}, f32[2,32,256]{2,1,0:T(8,128)S(1)}, u32[]{:S(2)}, u32[]{:S(2)}) collective-permute-start(f32[2,32,256]{2,1,0:T(8,128)S(1)} %dynamic-slice_bitcast_fusion.1), channel_id=1, source_target_pairs={{0,8},{1,9},{2,10},{3,11},{4,12},{5,13},{6,14},{7,15},{8,0},{9,1},... | collective-permute-start | bytes 196616 | tf_op jit(solution)/shard_map/ppermute | solution.py:51
  22.8 0.0 copy-done.1
  22.8 0.1 broadcast_subtract_fusion.1
  24.8 0.1 dynamic_slice.47
  24.9 0.6 %collective-permute-done.3 = f32[2,32,256]{2,1,0:T(8,128)S(1)} collective-permute-done((f32[2,32,256]{2,1,0:T(8,128)S(1)}, f32[2,32,256]{2,1,0:T(8,128)S(1)}, u32[]{:S(2)}, u32[]{:S(2)}) %collective-permute-start.3) | collective-permute-done | bytes 65568 | tf_op jit(solution)/shard_map/ppermute | solution.py:51
  25.5 2.7 %collective-permute-start.4 = (f32[32,256]{1,0:T(8,128)S(1)}, f32[32,256]{1,0:T(8,128)S(1)}, u32[]{:S(2)}, u32[]{:S(2)}) collective-permute-start(f32[32,256]{1,0:T(8,128)S(1)} %dynamic-slice_bitcast_fusion.2), channel_id=1, source_target_pairs={{0,16},{1,17},{2,18},{3,19},{4,20},{5,21},{6,22},{7,23},{8,24},{9,... | collective-permute-start | bytes 98312 | tf_op jit(solution)/shard_map/ppermute | solution.py:51
  28.1 0.1 broadcast_subtract_fusion
  28.2 0.1 sub.56
  28.3 0.1 sub.60
  28.4 0.1 dynamic_slice.46
  28.5 1.9 %collective-permute-done.4 = f32[32,256]{1,0:T(8,128)S(1)} collective-permute-done((f32[32,256]{1,0:T(8,128)S(1)}, f32[32,256]{1,0:T(8,128)S(1)}, u32[]{:S(2)}, u32[]{:S(2)}) %collective-permute-start.4) | collective-permute-done | bytes 32800 | tf_op jit(solution)/shard_map/ppermute | solution.py:51
  30.4 0.7 %fusion.21 = bf16[32,256]{1,0:T(8,128)(2,1)} fusion(f32[32,256]{1,0:T(8,128)S(1)} %collective-permute-done.4, f32[2,32,256]{2,1,0:T(8,128)S(1)} %bitcast_add_fusion.2, s32[]{:T(128)S(6)} %select_n.64, f32[256]{0:T(256)S(1)} %sub.60, f32[32]{0:T(128)S(1)} %dynamic_slice.46), kind=kLoop, calls=%fused_computation.32 | loop fusion | flops 32768 | bytes 83076 | tf_op jit(solution)/shard_map/convert_element_type | solution.py:157
  (10 shorter events, 0.2 us)
Async XLA Ops:
  3.5 2.4 %collective-permute-start = (f32[512,256]{1,0:T(8,128)S(1)}, f32[512,256]{1,0:T(8,128)S(1)}, u32[]{:S(2)}, u32[]{:S(2)}) collective-permute-start(f32[512,256]{1,0:T(8,128)S(1)} %get-tuple-element.70), channel_id=1, source_target_pairs={{0,1},{1,0},{2,3},{3,2},{4,5},{5,4},{6,7},{7,6},{8,9},{9,8},{10,11... | collective-permute-start | bytes 1572872 | tf_op jit(solution)/shard_map/ppermute | solution.py:26
  5.9 11.6 %copy-start = (s32[2]{0:T(128)S(1)}, s32[2]{0:T(128)}, u32[]{:S(2)}) copy-start(s32[2]{0:T(128)} %slab_ref.1) | copy-start | bytes 28
  5.9 14.2 %copy-start.2 = (f32[512]{0:T(512)S(1)}, f32[512]{0:T(512)}, u32[]{:S(2)}) copy-start(f32[512]{0:T(512)} %param.16) | copy-start | bytes 6148
  5.9 16.9 %copy-start.1 = (f32[64]{0:T(128)S(1)}, f32[64]{0:T(128)}, u32[]{:S(2)}) copy-start(f32[64]{0:T(128)} %param.15) | copy-start | bytes 772
  6.1 9.5 %collective-permute-start.1 = (f32[2,2,2,32,256]{4,3,2,1,0:T(8,128)S(1)}, f32[2,2,2,32,256]{4,3,2,1,0:T(8,128)S(1)}, u32[]{:S(2)}, u32[]{:S(2)}) collective-permute-start(f32[2,2,2,32,256]{4,3,2,1,0:T(8,128)S(1)} %dynamic-slice_bitcast_fusion), channel_id=1, source_target_pairs={{0,2},{1,3},{2,0},{3,1},{4,6},{5,7},{6,4},{7,5},{8,10},{9,11},{10,... | collective-permute-start | bytes 786440 | tf_op jit(solution)/shard_map/ppermute | solution.py:51
  15.7 5.4 %collective-permute-start.2 = (f32[2,2,32,256]{3,2,0,1:T(8,128)S(1)}, f32[2,2,32,256]{3,2,0,1:T(8,128)S(1)}, u32[]{:S(2)}, u32[]{:S(2)}) collective-permute-start(f32[2,2,32,256]{3,2,0,1:T(8,128)S(1)} %bitcast.51), channel_id=1, source_target_pairs={{0,4},{1,5},{2,6},{3,7},{4,0},{5,1},{6,2},{7,3},{8,12},{9,13},{10,... | collective-permute-start | bytes 393224 | tf_op jit(solution)/shard_map/ppermute | solution.py:51
  21.1 4.3 %collective-permute-start.3 = (f32[2,32,256]{2,1,0:T(8,128)S(1)}, f32[2,32,256]{2,1,0:T(8,128)S(1)}, u32[]{:S(2)}, u32[]{:S(2)}) collective-permute-start(f32[2,32,256]{2,1,0:T(8,128)S(1)} %dynamic-slice_bitcast_fusion.1), channel_id=1, source_target_pairs={{0,8},{1,9},{2,10},{3,11},{4,12},{5,13},{6,14},{7,15},{8,0},{9,1},... | collective-permute-start | bytes 196616 | tf_op jit(solution)/shard_map/ppermute | solution.py:51
  25.5 4.9 %collective-permute-start.4 = (f32[32,256]{1,0:T(8,128)S(1)}, f32[32,256]{1,0:T(8,128)S(1)}, u32[]{:S(2)}, u32[]{:S(2)}) collective-permute-start(f32[32,256]{1,0:T(8,128)S(1)} %dynamic-slice_bitcast_fusion.2), channel_id=1, source_target_pairs={{0,16},{1,17},{2,18},{3,19},{4,20},{5,21},{6,22},{7,23},{8,24},{9,... | collective-permute-start | bytes 98312 | tf_op jit(solution)/shard_map/ppermute | solution.py:51

commit v16 on v15

--- a/solution.py
+++ b/solution.py
@@ -18,6 +18,10 @@
 
     def order(c):
         seq = list(range(bits))
+        if c == 1 and bits >= 5:
+            seq[1:4] = [3, 1, 2]
+        elif c == 1 and bits >= 3:
+            seq[1], seq[2] = seq[2], seq[1]
         return seq
 
     left = [list(range(bits - 1, -1, -1)) for _ in range(2)]

time: 31.3 us -> 28.6 us (0.914)
  waiting for transfers between devices: 10.3 us -> 6.4 us
  starting transfers between devices: 9.28 us -> 10.5 us
    ppermute x4, waiting for transfers between devices: 10.3 us -> 6.39 us  [halving_scatter(): buf = keep + lax.ppermute(send, axis, perm)]
    ppermute x4, starting transfers between devices: 8.77 us -> 9.95 us  [halving_scatter(): buf = keep + lax.ppermute(send, axis, perm)]
  transfers between devices with their start and end apart: 5 -> 5, of which waited for: 4 -> 4; matrix products, arithmetic and copies ran while one was open for 10% -> 11% of each run, Pallas kernels for 0% -> 0%
where the time goes in v16:
time: 28.6 us; the launch traced here: 28.3 us
  starting transfers between devices  10.5 us (37%)
  waiting for transfers between devices  6.4 us (22%)
  between operations  4.01 us (14%)
  local copies, waits for them, and re-layouts  3.75 us (13%)
  Pallas kernels  1.67 us (6%)
  other arithmetic  1.02 us (4%)
  matrix products  0.98 us (3%)
    ppermute x4, starting transfers between devices, halving_scatter(): buf = keep + lax.ppermute(send, axis, perm)  9.95 us
    ppermute x4, waiting for transfers between devices, halving_scatter(): buf = keep + lax.ppermute(send, axis, perm)  6.39 us
    slice x2, local copies, waits for them, and re-layouts, half(): amp4[:, parity].reshape(rows_pair // 2, kc_local)  2.64 us
    pallas_call x1, Pallas kernels, irreps(): pl.pallas_call(functools.partial(_irrep_kernel, shape), out_shape=shapes,...  1.67 us
    dot_general x2, matrix products, product(): return jnp.dot(masked, int_masked, preferred_element_type=jnp.float32)  0.98 us
    convert_element_type x1, other arithmetic, body(): (summed / (mine_energy[:, None] + col_energy[None, :])).astype(jnp.bfloat16)  0.69 us
    slice x1, local copies, waits for them, and re-layouts, body(): first_start = slab_start[0]  0.6 us
  transfers between devices with their start and end apart: 5, of which 4 were waited for; matrix products, arithmetic and copies ran while one was open for 11% of the time, Pallas kernels for 0%

profile of v16, /device:TPU:0, one launch (start us, length us, event | category | flops | bytes accessed | tf_op | source)
XLA Modules:
  0.0 28.3 jit_solution(680060364113594946)
XLA Ops:
  0.0 1.7 %shard_map.73 = (s32[2,512]{1,0:T(2,128)S(1)}, s32[1,1024]{1,0:T(1,128)S(1)}, bf16[1024,256]{1,0:T(8,128)(2,1)S(1)}) custom-call(s32[2]{0:T(128)} %slab_ref.1, s32[64]{0:T(128)} %occ_v_ref.1, s32[64]{0:T(128)} %occ_v_ref.1, s32[512]{0:T(512)} %virt_v_ref.1, bf16[1024,256]{1,0:T(8,128)(2,1)} %int_ref), custom_call_target="tpu_custom_call" | custom-call | tf_op jit(solution)/shard_map/pallas_call | solution.py:106
  1.7 1.9 %conditional.3 = (f32[512,256]{1,0:T(8,128)S(1)}) conditional(s32[]{:T(128)} %convert_element_type.7, (s32[2,512]{1,0:T(2,128)S(1)}, s32[1,1024]{1,0:T(1,128)S(1)}, bf16[16,2,32,1024]{3,2,1,0:T(8,128)(2,1)}, bf16[1024,256]{1,0:T(8,128)(2,1)S(1)}) %tuple.24, (s32[2,512]{1,0:T(2,128)S(1)}, s32[1,1024]{1,0:T(1,128)S(1)}, ...), branch_computations={%region_2.3_spmd, %region_3.4_spmd} | conditional | flops 269484032 | bytes 4204552 | solution.py:152
  1.7 1.3 %slice.27 = bf16[16,1,32,1024]{3,2,1,0:T(8,128)(2,1)S(1)} slice(bf16[16,2,32,1024]{3,2,1,0:T(8,128)(2,1)} %get-tuple-element.57), slice={[0:16], [1:2], [0:32], [0:1024]} | slice | bytes 2097152 | tf_op jit(solution)/shard_map/cond/branch_1_fun/slice | solution.py:150
  3.0 0.5 %fusion.15 = f32[512,256]{1,0:T(8,128)S(1)} fusion(bf16[1024,256]{1,0:T(8,128)(2,1)S(1)} %get-tuple-element.58, bf16[512,1024]{1,0:T(8,128)(2,1)S(1)} %bitcast.54, s32[1024]{0:T(1024)S(1)} %bitcast.63, s32[512]{0:T(512)S(1)} %bitcast.59), kind=kOutput, calls=%fused_computation.19 | convolution fusion | flops 269484032 | bytes 2103296 | tf_op jit(solution)/shard_map/cond/branch_1_fun/dot_general | solution.py:143
  3.5 0.5 %collective-permute-start = (f32[512,256]{1,0:T(8,128)S(1)}, f32[512,256]{1,0:T(8,128)S(1)}, u32[]{:S(2)}, u32[]{:S(2)}) collective-permute-start(f32[512,256]{1,0:T(8,128)S(1)} %get-tuple-element.70), channel_id=1, source_target_pairs={{0,1},{1,0},{2,3},{3,2},{4,5},{5,4},{6,7},{7,6},{8,9},{9,8},{10,11... | collective-permute-start | bytes 1572872 | tf_op jit(solution)/shard_map/ppermute | solution.py:30
  4.1 1.8 %conditional.2 = (f32[512,256]{1,0:T(8,128)S(1)}) conditional(s32[]{:T(128)} %convert_element_type.7, (s32[2,512]{1,0:T(2,128)S(1)}, s32[1,1024]{1,0:T(1,128)S(1)}, bf16[16,2,32,1024]{3,2,1,0:T(8,128)(2,1)}, bf16[1024,256]{1,0:T(8,128)(2,1)S(1)}) %tuple.26, (s32[2,512]{1,0:T(2,128)S(1)}, s32[1,1024]{1,0:T(1,128)S(1)}, ...), branch_computations={%region_0.1_spmd, %region_1.2_spmd} | conditional | flops 269484032 | bytes 4204552 | solution.py:154
  4.1 1.3 %slice.23 = bf16[16,1,32,1024]{3,2,1,0:T(8,128)(2,1)S(1)} slice(bf16[16,2,32,1024]{3,2,1,0:T(8,128)(2,1)} %get-tuple-element.49), slice={[0:16], [0:1], [0:32], [0:1024]} | slice | bytes 2097152 | tf_op jit(solution)/shard_map/cond/branch_1_fun/slice | solution.py:150
  5.4 0.5 %fusion.5 = f32[512,256]{1,0:T(8,128)S(1)} fusion(bf16[1024,256]{1,0:T(8,128)(2,1)S(1)} %get-tuple-element.50, bf16[512,1024]{1,0:T(8,128)(2,1)S(1)} %bitcast.56, s32[1024]{0:T(1024)S(1)} %bitcast.65, s32[512]{0:T(512)S(1)} %bitcast.61), kind=kOutput, calls=%fused_computation.7 | convolution fusion | flops 269484032 | bytes 2103296 | tf_op jit(solution)/shard_map/cond/branch_1_fun/dot_general | solution.py:143
  5.9 0.0 copy-start
  5.9 0.0 copy-start.2
  5.9 0.0 copy-start.1
  5.9 0.0 collective-permute-done
  5.9 0.1 add.83
  6.1 2.6 %collective-permute-start.1 = (f32[2,2,2,32,256]{4,3,2,1,0:T(8,128)S(1)}, f32[2,2,2,32,256]{4,3,2,1,0:T(8,128)S(1)}, u32[]{:S(2)}, u32[]{:S(2)}) collective-permute-start(f32[2,2,2,32,256]{4,3,2,1,0:T(8,128)S(1)} %bitcast_select_fusion), channel_id=1, source_target_pairs={{0,2},{1,9},{2,0},{3,11},{4,6},{5,13},{6,4},{7,15},{8,10},{9,1},{1... | collective-permute-start | bytes 786440 | tf_op jit(solution)/shard_map/ppermute | solution.py:55
  8.7 4.4 %collective-permute-done.1 = f32[2,2,2,32,256]{4,3,2,1,0:T(8,128)S(1)} collective-permute-done((f32[2,2,2,32,256]{4,3,2,1,0:T(8,128)S(1)}, f32[2,2,2,32,256]{4,3,2,1,0:T(8,128)S(1)}, u32[]{:S(2)}, u32[]{:S(2)}) %collective-permute-start.1) | collective-permute-done | bytes 262176 | tf_op jit(solution)/shard_map/ppermute | solution.py:55
  13.0 0.1 fusion.20
  13.1 2.1 %collective-permute-start.2 = (f32[2,2,32,256]{3,2,0,1:T(8,128)S(1)}, f32[2,2,32,256]{3,2,0,1:T(8,128)S(1)}, u32[]{:S(2)}, u32[]{:S(2)}) collective-permute-start(f32[2,2,32,256]{3,2,0,1:T(8,128)S(1)} %bitcast.57), channel_id=1, source_target_pairs={{0,4},{1,3},{2,6},{3,1},{4,0},{5,7},{6,2},{7,5},{8,12},{9,11},{10,... | collective-permute-start | bytes 393224 | tf_op jit(solution)/shard_map/ppermute | solution.py:55
  15.3 0.0 copy-done
  15.3 0.6 %fusion.23 = (s32[1]{0:T(128)}, s32[1]{0:T(128)}) fusion(s32[2]{0:T(128)S(1)} %copy-done), kind=kLoop, calls=%fused_computation.39 | loop fusion | bytes 16 | tf_op jit(solution)/shard_map/slice | solution.py:127
  17.8 0.0 copy-done.2
  17.8 0.1 dynamic_slice.54
  17.9 0.3 %collective-permute-done.2 = f32[2,2,32,256]{3,2,0,1:T(8,128)S(1)} collective-permute-done((f32[2,2,32,256]{3,2,0,1:T(8,128)S(1)}, f32[2,2,32,256]{3,2,0,1:T(8,128)S(1)}, u32[]{:S(2)}, u32[]{:S(2)}) %collective-permute-start.2) | collective-permute-done | bytes 131104 | tf_op jit(solution)/shard_map/ppermute | solution.py:55
  18.2 2.1 %collective-permute-start.3 = (f32[2,32,256]{2,1,0:T(8,128)S(1)}, f32[2,32,256]{2,1,0:T(8,128)S(1)}, u32[]{:S(2)}, u32[]{:S(2)}) collective-permute-start(f32[2,32,256]{2,1,0:T(8,128)S(1)} %dynamic-slice_bitcast_fusion), channel_id=1, source_target_pairs={{0,8},{1,5},{2,10},{3,7},{4,12},{5,1},{6,14},{7,3},{8,0},{9,13},{1... | collective-permute-start | bytes 196616 | tf_op jit(solution)/shard_map/ppermute | solution.py:55
  20.4 0.0 copy-done.1
  20.4 0.1 broadcast_subtract_fusion.1
  22.4 0.1 dynamic_slice.56
  22.4 0.2 collective-permute-done.3
  22.7 3.1 %collective-permute-start.4 = (f32[32,256]{1,0:T(8,128)S(1)}, f32[32,256]{1,0:T(8,128)S(1)}, u32[]{:S(2)}, u32[]{:S(2)}) collective-permute-start(f32[32,256]{1,0:T(8,128)S(1)} %dynamic-slice_bitcast_fusion.1), channel_id=1, source_target_pairs={{0,16},{1,17},{2,18},{3,19},{4,20},{5,21},{6,22},{7,23},{8,24},{9,... | collective-permute-start | bytes 98312 | tf_op jit(solution)/shard_map/ppermute | solution.py:55
  25.8 0.1 broadcast_subtract_fusion
  25.8 0.1 sub.60
  25.9 0.1 sub.64
  26.0 0.1 dynamic_slice.55
  26.1 1.6 %collective-permute-done.4 = f32[32,256]{1,0:T(8,128)S(1)} collective-permute-done((f32[32,256]{1,0:T(8,128)S(1)}, f32[32,256]{1,0:T(8,128)S(1)}, u32[]{:S(2)}, u32[]{:S(2)}) %collective-permute-start.4) | collective-permute-done | bytes 32800 | tf_op jit(solution)/shard_map/ppermute | solution.py:55
  27.7 0.7 %fusion.22 = bf16[32,256]{1,0:T(8,128)(2,1)} fusion(f32[32,256]{1,0:T(8,128)S(1)} %collective-permute-done.4, f32[2,32,256]{2,1,0:T(8,128)S(1)} %bitcast_add_fusion.1, s32[]{:T(128)S(6)} %select_n.96, f32[256]{0:T(256)S(1)} %sub.64, f32[32]{0:T(128)S(1)} %dynamic_slice.55), kind=kLoop, calls=%fused_computation.33 | loop fusion | flops 32768 | bytes 83076 | tf_op jit(solution)/shard_map/convert_element_type | solution.py:161
  (9 shorter events, 0.1 us)
Async XLA Ops:
  3.5 2.4 %collective-permute-start = (f32[512,256]{1,0:T(8,128)S(1)}, f32[512,256]{1,0:T(8,128)S(1)}, u32[]{:S(2)}, u32[]{:S(2)}) collective-permute-start(f32[512,256]{1,0:T(8,128)S(1)} %get-tuple-element.70), channel_id=1, source_target_pairs={{0,1},{1,0},{2,3},{3,2},{4,5},{5,4},{6,7},{7,6},{8,9},{9,8},{10,11... | collective-permute-start | bytes 1572872 | tf_op jit(solution)/shard_map/ppermute | solution.py:30
  5.9 9.4 %copy-start = (s32[2]{0:T(128)S(1)}, s32[2]{0:T(128)}, u32[]{:S(2)}) copy-start(s32[2]{0:T(128)} %slab_ref.1) | copy-start | bytes 28
  5.9 11.9 %copy-start.2 = (f32[512]{0:T(512)S(1)}, f32[512]{0:T(512)}, u32[]{:S(2)}) copy-start(f32[512]{0:T(512)} %param.16) | copy-start | bytes 6148
  5.9 14.5 %copy-start.1 = (f32[64]{0:T(128)S(1)}, f32[64]{0:T(128)}, u32[]{:S(2)}) copy-start(f32[64]{0:T(128)} %param.15) | copy-start | bytes 772
  6.1 6.9 %collective-permute-start.1 = (f32[2,2,2,32,256]{4,3,2,1,0:T(8,128)S(1)}, f32[2,2,2,32,256]{4,3,2,1,0:T(8,128)S(1)}, u32[]{:S(2)}, u32[]{:S(2)}) collective-permute-start(f32[2,2,2,32,256]{4,3,2,1,0:T(8,128)S(1)} %bitcast_select_fusion), channel_id=1, source_target_pairs={{0,2},{1,9},{2,0},{3,11},{4,6},{5,13},{6,4},{7,15},{8,10},{9,1},{1... | collective-permute-start | bytes 786440 | tf_op jit(solution)/shard_map/ppermute | solution.py:55
  13.1 5.1 %collective-permute-start.2 = (f32[2,2,32,256]{3,2,0,1:T(8,128)S(1)}, f32[2,2,32,256]{3,2,0,1:T(8,128)S(1)}, u32[]{:S(2)}, u32[]{:S(2)}) collective-permute-start(f32[2,2,32,256]{3,2,0,1:T(8,128)S(1)} %bitcast.57), channel_id=1, source_target_pairs={{0,4},{1,3},{2,6},{3,1},{4,0},{5,7},{6,2},{7,5},{8,12},{9,11},{10,... | collective-permute-start | bytes 393224 | tf_op jit(solution)/shard_map/ppermute | solution.py:55
  18.2 4.4 %collective-permute-start.3 = (f32[2,32,256]{2,1,0:T(8,128)S(1)}, f32[2,32,256]{2,1,0:T(8,128)S(1)}, u32[]{:S(2)}, u32[]{:S(2)}) collective-permute-start(f32[2,32,256]{2,1,0:T(8,128)S(1)} %dynamic-slice_bitcast_fusion), channel_id=1, source_target_pairs={{0,8},{1,5},{2,10},{3,7},{4,12},{5,1},{6,14},{7,3},{8,0},{9,13},{1... | collective-permute-start | bytes 196616 | tf_op jit(solution)/shard_map/ppermute | solution.py:55
  22.7 5.0 %collective-permute-start.4 = (f32[32,256]{1,0:T(8,128)S(1)}, f32[32,256]{1,0:T(8,128)S(1)}, u32[]{:S(2)}, u32[]{:S(2)}) collective-permute-start(f32[32,256]{1,0:T(8,128)S(1)} %dynamic-slice_bitcast_fusion.1), channel_id=1, source_target_pairs={{0,16},{1,17},{2,18},{3,19},{4,20},{5,21},{6,22},{7,23},{8,24},{9,... | collective-permute-start | bytes 98312 | tf_op jit(solution)/shard_map/ppermute | solution.py:55

commit v17 on v16

--- a/solution.py
+++ b/solution.py
@@ -19,7 +19,7 @@
     def order(c):
         seq = list(range(bits))
         if c == 1 and bits >= 5:
-            seq[1:4] = [3, 1, 2]
+            seq[1:4] = [2, 3, 1]
         elif c == 1 and bits >= 3:
             seq[1], seq[2] = seq[2], seq[1]
         return seq

time: 28.6 us -> 28.7 us (level)
  waiting for transfers between devices: 6.4 us -> 6.72 us
    ppermute x4, waiting for transfers between devices: 6.39 us -> 6.72 us  [halving_scatter(): buf = keep + lax.ppermute(send, axis, perm)]
  transfers between devices with their start and end apart: 5 -> 5, of which waited for: 4 -> 4; matrix products, arithmetic and copies ran while one was open for 11% -> 10% of each run, Pallas kernels for 0% -> 0%
where the time goes in v17:
time: 28.7 us; the launch traced here: 28.4 us
  starting transfers between devices  10.5 us (37%)
  waiting for transfers between devices  6.72 us (23%)
  between operations  3.74 us (13%)
  local copies, waits for them, and re-layouts  3.72 us (13%)
  Pallas kernels  1.67 us (6%)
  other arithmetic  1.05 us (4%)
  matrix products  0.98 us (3%)
    ppermute x4, starting transfers between devices, halving_scatter(): buf = keep + lax.ppermute(send, axis, perm)  9.95 us
    ppermute x4, waiting for transfers between devices, halving_scatter(): buf = keep + lax.ppermute(send, axis, perm)  6.72 us
    slice x2, local copies, waits for them, and re-layouts, half(): amp4[:, parity].reshape(rows_pair // 2, kc_local)  2.64 us
    pallas_call x1, Pallas kernels, irreps(): pl.pallas_call(functools.partial(_irrep_kernel, shape), out_shape=shapes,...  1.67 us
    dot_general x2, matrix products, product(): return jnp.dot(masked, int_masked, preferred_element_type=jnp.float32)  0.98 us
    convert_element_type x1, other arithmetic, body(): (summed / (mine_energy[:, None] + col_energy[None, :])).astype(jnp.bfloat16)  0.69 us
  transfers between devices with their start and end apart: 5, of which 4 were waited for; matrix products, arithmetic and copies ran while one was open for 10% of the time, Pallas kernels for 0%

profile of v17, /device:TPU:0, one launch (start us, length us, event | category | flops | bytes accessed | tf_op | source)
XLA Modules:
  0.0 28.4 jit_solution(8130737081318448382)
XLA Ops:
  0.0 1.7 %shard_map.73 = (s32[2,512]{1,0:T(2,128)S(1)}, s32[1,1024]{1,0:T(1,128)S(1)}, bf16[1024,256]{1,0:T(8,128)(2,1)S(1)}) custom-call(s32[2]{0:T(128)} %slab_ref.1, s32[64]{0:T(128)} %occ_v_ref.1, s32[64]{0:T(128)} %occ_v_ref.1, s32[512]{0:T(512)} %virt_v_ref.1, bf16[1024,256]{1,0:T(8,128)(2,1)} %int_ref), custom_call_target="tpu_custom_call" | custom-call | tf_op jit(solution)/shard_map/pallas_call | solution.py:106
  1.7 1.9 %conditional.3 = (f32[512,256]{1,0:T(8,128)S(1)}) conditional(s32[]{:T(128)} %convert_element_type.7, (s32[2,512]{1,0:T(2,128)S(1)}, s32[1,1024]{1,0:T(1,128)S(1)}, bf16[16,2,32,1024]{3,2,1,0:T(8,128)(2,1)}, bf16[1024,256]{1,0:T(8,128)(2,1)S(1)}) %tuple.25, (s32[2,512]{1,0:T(2,128)S(1)}, s32[1,1024]{1,0:T(1,128)S(1)}, ...), branch_computations={%region_2.3_spmd, %region_3.4_spmd} | conditional | flops 269484032 | bytes 4204552 | solution.py:152
  1.7 1.3 %slice.27 = bf16[16,1,32,1024]{3,2,1,0:T(8,128)(2,1)S(1)} slice(bf16[16,2,32,1024]{3,2,1,0:T(8,128)(2,1)} %get-tuple-element.57), slice={[0:16], [1:2], [0:32], [0:1024]} | slice | bytes 2097152 | tf_op jit(solution)/shard_map/cond/branch_1_fun/slice | solution.py:150
  3.0 0.5 %fusion.15 = f32[512,256]{1,0:T(8,128)S(1)} fusion(bf16[1024,256]{1,0:T(8,128)(2,1)S(1)} %get-tuple-element.58, bf16[512,1024]{1,0:T(8,128)(2,1)S(1)} %bitcast.59, s32[1024]{0:T(1024)S(1)} %bitcast.67, s32[512]{0:T(512)S(1)} %bitcast.63), kind=kOutput, calls=%fused_computation.19 | convolution fusion | flops 269484032 | bytes 2103296 | tf_op jit(solution)/shard_map/cond/branch_1_fun/dot_general | solution.py:143
  3.5 0.5 %collective-permute-start = (f32[512,256]{1,0:T(8,128)S(1)}, f32[512,256]{1,0:T(8,128)S(1)}, u32[]{:S(2)}, u32[]{:S(2)}) collective-permute-start(f32[512,256]{1,0:T(8,128)S(1)} %get-tuple-element.72), channel_id=1, source_target_pairs={{0,1},{1,0},{2,3},{3,2},{4,5},{5,4},{6,7},{7,6},{8,9},{9,8},{10,11... | collective-permute-start | bytes 1572872 | tf_op jit(solution)/shard_map/ppermute | solution.py:30
  4.1 1.8 %conditional.2 = (f32[512,256]{1,0:T(8,128)S(1)}) conditional(s32[]{:T(128)} %convert_element_type.7, (s32[2,512]{1,0:T(2,128)S(1)}, s32[1,1024]{1,0:T(1,128)S(1)}, bf16[16,2,32,1024]{3,2,1,0:T(8,128)(2,1)}, bf16[1024,256]{1,0:T(8,128)(2,1)S(1)}) %tuple.27, (s32[2,512]{1,0:T(2,128)S(1)}, s32[1,1024]{1,0:T(1,128)S(1)}, ...), branch_computations={%region_0.1_spmd, %region_1.2_spmd} | conditional | flops 269484032 | bytes 4204552 | solution.py:154
  4.1 1.3 %slice.23 = bf16[16,1,32,1024]{3,2,1,0:T(8,128)(2,1)S(1)} slice(bf16[16,2,32,1024]{3,2,1,0:T(8,128)(2,1)} %get-tuple-element.49), slice={[0:16], [0:1], [0:32], [0:1024]} | slice | bytes 2097152 | tf_op jit(solution)/shard_map/cond/branch_1_fun/slice | solution.py:150
  5.4 0.5 %fusion.5 = f32[512,256]{1,0:T(8,128)S(1)} fusion(bf16[1024,256]{1,0:T(8,128)(2,1)S(1)} %get-tuple-element.50, bf16[512,1024]{1,0:T(8,128)(2,1)S(1)} %bitcast.61, s32[1024]{0:T(1024)S(1)} %bitcast.69, s32[512]{0:T(512)S(1)} %bitcast.65), kind=kOutput, calls=%fused_computation.7 | convolution fusion | flops 269484032 | bytes 2103296 | tf_op jit(solution)/shard_map/cond/branch_1_fun/dot_general | solution.py:143
  5.9 0.0 copy-start
  5.9 0.0 copy-start.2
  5.9 0.0 collective-permute-done
  5.9 0.1 add.86
  6.0 0.0 copy-start.1
  6.1 2.6 %collective-permute-start.1 = (f32[2,2,2,32,256]{4,3,2,1,0:T(8,128)S(1)}, f32[2,2,2,32,256]{4,3,2,1,0:T(8,128)S(1)}, u32[]{:S(2)}, u32[]{:S(2)}) collective-permute-start(f32[2,2,2,32,256]{4,3,2,1,0:T(8,128)S(1)} %bitcast_select_fusion), channel_id=1, source_target_pairs={{0,2},{1,5},{2,0},{3,7},{4,6},{5,1},{6,4},{7,3},{8,10},{9,13},{10,... | collective-permute-start | bytes 786440 | tf_op jit(solution)/shard_map/ppermute | solution.py:55
  8.7 4.4 %collective-permute-done.1 = f32[2,2,2,32,256]{4,3,2,1,0:T(8,128)S(1)} collective-permute-done((f32[2,2,2,32,256]{4,3,2,1,0:T(8,128)S(1)}, f32[2,2,2,32,256]{4,3,2,1,0:T(8,128)S(1)}, u32[]{:S(2)}, u32[]{:S(2)}) %collective-permute-start.1) | collective-permute-done | bytes 262176 | tf_op jit(solution)/shard_map/ppermute | solution.py:55
  13.0 0.1 fusion.20
  13.2 2.1 %collective-permute-start.2 = (f32[2,2,32,256]{3,2,0,1:T(8,128)S(1)}, f32[2,2,32,256]{3,2,0,1:T(8,128)S(1)}, u32[]{:S(2)}, u32[]{:S(2)}) collective-permute-start(f32[2,2,32,256]{3,2,0,1:T(8,128)S(1)} %bitcast_select_fusion.2), channel_id=1, source_target_pairs={{0,4},{1,9},{2,6},{3,11},{4,0},{5,13},{6,2},{7,15},{8,12},{9,1},{1... | collective-permute-start | bytes 393224 | tf_op jit(solution)/shard_map/ppermute | solution.py:55
  15.3 0.0 copy-done
  15.3 0.6 %fusion.24 = (s32[1]{0:T(128)}, s32[1]{0:T(128)}) fusion(s32[2]{0:T(128)S(1)} %copy-done), kind=kLoop, calls=%fused_computation.42 | loop fusion | bytes 16 | tf_op jit(solution)/shard_map/slice | solution.py:127
  17.8 0.0 copy-done.2
  17.8 0.1 dynamic_slice.63
  17.9 0.4 %collective-permute-done.2 = f32[2,2,32,256]{3,2,0,1:T(8,128)S(1)} collective-permute-done((f32[2,2,32,256]{3,2,0,1:T(8,128)S(1)}, f32[2,2,32,256]{3,2,0,1:T(8,128)S(1)}, u32[]{:S(2)}, u32[]{:S(2)}) %collective-permute-start.2) | collective-permute-done | bytes 131104 | tf_op jit(solution)/shard_map/ppermute | solution.py:55
  18.3 2.1 %collective-permute-start.3 = (f32[2,32,256]{2,1,0:T(8,128)S(1)}, f32[2,32,256]{2,1,0:T(8,128)S(1)}, u32[]{:S(2)}, u32[]{:S(2)}) collective-permute-start(f32[2,32,256]{2,1,0:T(8,128)S(1)} %dynamic-slice_bitcast_fusion), channel_id=1, source_target_pairs={{0,8},{1,3},{2,10},{3,1},{4,12},{5,7},{6,14},{7,5},{8,0},{9,11},{1... | collective-permute-start | bytes 196616 | tf_op jit(solution)/shard_map/ppermute | solution.py:55
  20.4 0.0 copy-done.1
  20.4 0.1 broadcast_subtract_fusion.1
  22.2 0.1 dynamic_slice.65
  22.2 0.4 %collective-permute-done.3 = f32[2,32,256]{2,1,0:T(8,128)S(1)} collective-permute-done((f32[2,32,256]{2,1,0:T(8,128)S(1)}, f32[2,32,256]{2,1,0:T(8,128)S(1)}, u32[]{:S(2)}, u32[]{:S(2)}) %collective-permute-start.3) | collective-permute-done | bytes 65568 | tf_op jit(solution)/shard_map/ppermute | solution.py:55
  22.7 3.1 %collective-permute-start.4 = (f32[32,256]{1,0:T(8,128)S(1)}, f32[32,256]{1,0:T(8,128)S(1)}, u32[]{:S(2)}, u32[]{:S(2)}) collective-permute-start(f32[32,256]{1,0:T(8,128)S(1)} %dynamic-slice_bitcast_fusion.1), channel_id=1, source_target_pairs={{0,16},{1,17},{2,18},{3,19},{4,20},{5,21},{6,22},{7,23},{8,24},{9,... | collective-permute-start | bytes 98312 | tf_op jit(solution)/shard_map/ppermute | solution.py:55
  25.8 0.1 broadcast_subtract_fusion
  25.9 0.1 sub.61
  26.0 0.1 sub.65
  26.1 0.1 dynamic_slice.64
  26.2 1.6 %collective-permute-done.4 = f32[32,256]{1,0:T(8,128)S(1)} collective-permute-done((f32[32,256]{1,0:T(8,128)S(1)}, f32[32,256]{1,0:T(8,128)S(1)}, u32[]{:S(2)}, u32[]{:S(2)}) %collective-permute-start.4) | collective-permute-done | bytes 32800 | tf_op jit(solution)/shard_map/ppermute | solution.py:55
  27.7 0.7 %fusion.23 = bf16[32,256]{1,0:T(8,128)(2,1)} fusion(f32[32,256]{1,0:T(8,128)S(1)} %collective-permute-done.4, f32[2,32,256]{2,1,0:T(8,128)S(1)} %bitcast_add_fusion, s32[]{:T(128)S(6)} %select_n.110, f32[256]{0:T(256)S(1)} %sub.65, f32[32]{0:T(128)S(1)} %dynamic_slice.64), kind=kLoop, calls=%fused_computation.34 | loop fusion | flops 32768 | bytes 83076 | tf_op jit(solution)/shard_map/convert_element_type | solution.py:161
  (10 shorter events, 0.2 us)
Async XLA Ops:
  3.5 2.4 %collective-permute-start = (f32[512,256]{1,0:T(8,128)S(1)}, f32[512,256]{1,0:T(8,128)S(1)}, u32[]{:S(2)}, u32[]{:S(2)}) collective-permute-start(f32[512,256]{1,0:T(8,128)S(1)} %get-tuple-element.72), channel_id=1, source_target_pairs={{0,1},{1,0},{2,3},{3,2},{4,5},{5,4},{6,7},{7,6},{8,9},{9,8},{10,11... | collective-permute-start | bytes 1572872 | tf_op jit(solution)/shard_map/ppermute | solution.py:30
  5.9 9.4 %copy-start = (s32[2]{0:T(128)S(1)}, s32[2]{0:T(128)}, u32[]{:S(2)}) copy-start(s32[2]{0:T(128)} %slab_ref.1) | copy-start | bytes 28
  5.9 11.9 %copy-start.2 = (f32[512]{0:T(512)S(1)}, f32[512]{0:T(512)}, u32[]{:S(2)}) copy-start(f32[512]{0:T(512)} %param.16) | copy-start | bytes 6148
  6.0 14.4 %copy-start.1 = (f32[64]{0:T(128)S(1)}, f32[64]{0:T(128)}, u32[]{:S(2)}) copy-start(f32[64]{0:T(128)} %param.15) | copy-start | bytes 772
  6.1 6.9 %collective-permute-start.1 = (f32[2,2,2,32,256]{4,3,2,1,0:T(8,128)S(1)}, f32[2,2,2,32,256]{4,3,2,1,0:T(8,128)S(1)}, u32[]{:S(2)}, u32[]{:S(2)}) collective-permute-start(f32[2,2,2,32,256]{4,3,2,1,0:T(8,128)S(1)} %bitcast_select_fusion), channel_id=1, source_target_pairs={{0,2},{1,5},{2,0},{3,7},{4,6},{5,1},{6,4},{7,3},{8,10},{9,13},{10,... | collective-permute-start | bytes 786440 | tf_op jit(solution)/shard_map/ppermute | solution.py:55
  13.2 5.1 %collective-permute-start.2 = (f32[2,2,32,256]{3,2,0,1:T(8,128)S(1)}, f32[2,2,32,256]{3,2,0,1:T(8,128)S(1)}, u32[]{:S(2)}, u32[]{:S(2)}) collective-permute-start(f32[2,2,32,256]{3,2,0,1:T(8,128)S(1)} %bitcast_select_fusion.2), channel_id=1, source_target_pairs={{0,4},{1,9},{2,6},{3,11},{4,0},{5,13},{6,2},{7,15},{8,12},{9,1},{1... | collective-permute-start | bytes 393224 | tf_op jit(solution)/shard_map/ppermute | solution.py:55
  18.3 4.4 %collective-permute-start.3 = (f32[2,32,256]{2,1,0:T(8,128)S(1)}, f32[2,32,256]{2,1,0:T(8,128)S(1)}, u32[]{:S(2)}, u32[]{:S(2)}) collective-permute-start(f32[2,32,256]{2,1,0:T(8,128)S(1)} %dynamic-slice_bitcast_fusion), channel_id=1, source_target_pairs={{0,8},{1,3},{2,10},{3,1},{4,12},{5,7},{6,14},{7,5},{8,0},{9,11},{1... | collective-permute-start | bytes 196616 | tf_op jit(solution)/shard_map/ppermute | solution.py:55
  22.7 5.0 %collective-permute-start.4 = (f32[32,256]{1,0:T(8,128)S(1)}, f32[32,256]{1,0:T(8,128)S(1)}, u32[]{:S(2)}, u32[]{:S(2)}) collective-permute-start(f32[32,256]{1,0:T(8,128)S(1)} %dynamic-slice_bitcast_fusion.1), channel_id=1, source_target_pairs={{0,16},{1,17},{2,18},{3,19},{4,20},{5,21},{6,22},{7,23},{8,24},{9,... | collective-permute-start | bytes 98312 | tf_op jit(solution)/shard_map/ppermute | solution.py:55
